TPU v7x, 256 devices: a whole 4x4x8 slice. The times are simulated.
256 devices in a mesh: lat: 32 (over x_lo, z, core), lon: 8 (over y, x_hi).
Axes of the slice: x: 4 (x_hi: 2, x_lo: 2; x = x_hi * 2 + x_lo), y: 4, z: 8, core: 2. Of those that a mesh axis runs over, the one named last changes fastest.
Arguments:
- tokens: bfloat16 [4, 192, 96, 512], P(None, 'lat', 'lon'), may hold values from -6 to 6
- w_qkv: bfloat16 [512, 1536], P('lon'), may hold values from -0.25 to 0.25
- w_out: bfloat16 [512, 512], P('lon'), may hold values from -0.25 to 0.25
- gain: float32 [512], replicated, may hold values from 0.1 to 1.9
- tau: float32 [8], replicated, may hold values from 1 to 12
- cotangent: bfloat16 [4, 192, 96, 512], P(None, 'lat', 'lon'), may hold values from -6 to 6
Outputs:
- output: bfloat16 [4, 192, 96, 512], P(None, 'lat', 'lon')
- grad_tokens: bfloat16 [4, 192, 96, 512], P(None, 'lat', 'lon')
- grad_qkv: float32 [512, 1536], P('lon')
- grad_out: float32 [512, 512], P('lon')
All inputs are finite; a program needn't handle non-finite values.
Results may differ from a plain program's by a relative error of at most 0.035.
Values may be sent and summed in bfloat16 or wider, within the bound.
No kernel may reach another device: no remote copies, remote signals or barrier semaphores. Data moves between devices by JAX's collectives and lax.ppermute only.
A program may use at most 128 MiB of HBM per device.

v0:
```python
import jax
import jax.numpy as jnp
from jax import lax
from jax.sharding import PartitionSpec as P
from jax.experimental import pallas as pl
from jax.experimental.pallas import tpu as pltpu

LV = 4
WL = 2
WH = 6
WW = 12
KEYS = 288


NORM_EPS = 1e-05
UNIT_EPS = 1e-06
HEADS_K = 8
HD_K = 64


def _nt(a, b):
    return lax.dot_general(a, b, (((1,), (1,)), ((), ())), preferred_element_type=jnp.float32)


def _tn(a, b):
    return lax.dot_general(a, b, (((0,), (0,)), ((), ())), preferred_element_type=jnp.float32)


def _block_probs(tau_ref, head, query, kv_ref, mask_ref):
    lanes = pl.ds(head * HD_K, HD_K)
    weights = []
    for r in range(2):
        for c in range(2):
            scores = _nt(query, kv_ref[r, c, :, lanes]) * tau_ref[head]
            weights.append(jnp.exp(scores) * mask_ref[r])
    total = sum(jnp.sum(w, axis=-1, keepdims=True) for w in weights)
    return [w / total for w in weights]


def attn_fwd_kernel(tau_ref, q_ref, kv_ref, mask_ref, out_ref):
    width = q_ref.shape[3]
    for head in range(HEADS_K):
        lanes = pl.ds(head * HD_K, HD_K)
        value_lanes = pl.ds(width + head * HD_K, HD_K)
        probs = _block_probs(tau_ref, head, q_ref[0, 0, :, lanes], kv_ref, mask_ref)
        mixed = None
        for n, p in enumerate(probs):
            part = jnp.dot(
                p.astype(jnp.bfloat16),
                kv_ref[n // 2, n % 2, :, value_lanes],
                preferred_element_type=jnp.float32,
            )
            mixed = part if mixed is None else mixed + part
        out_ref[0, 0, :, lanes] = mixed


def attn_bwd_kernel(tau_ref, q_ref, kv_ref, g_ref, mask_ref, dq_ref, dkv_ref):
    width = q_ref.shape[3]
    for head in range(HEADS_K):
        lanes = pl.ds(head * HD_K, HD_K)
        value_lanes = pl.ds(width + head * HD_K, HD_K)
        query = q_ref[0, 0, :, lanes]
        grad = g_ref[0, 0, :, lanes]
        probs = _block_probs(tau_ref, head, query, kv_ref, mask_ref)
        dprobs = [_nt(grad, kv_ref[n // 2, n % 2, :, value_lanes]) for n in range(4)]
        total = sum(jnp.sum(p * d, axis=-1, keepdims=True) for p, d in zip(probs, dprobs))
        dquery = None
        for n in range(4):
            r, c = n // 2, n % 2
            dscore = (tau_ref[head] * (probs[n] * (dprobs[n] - total))).astype(jnp.bfloat16)
            part = jnp.dot(dscore, kv_ref[r, c, :, lanes], preferred_element_type=jnp.float32)
            dquery = part if dquery is None else dquery + part
            dkv_ref[r, c, :, lanes] = _tn(dscore, query)
            dkv_ref[r, c, :, value_lanes] = _tn(probs[n].astype(jnp.bfloat16), grad)
        dq_ref[0, 0, :, lanes] = dquery


def _window_of(i, j):
    return ((i + 1) // 2, (j + 1) // 2, 0, 0)


def window_fwd(tau, query, ext_kv, mask):
    row_units, col_units, queries, width = query.shape
    return pl.pallas_call(
        attn_fwd_kernel,
        grid=(row_units, col_units),
        in_specs=[
            pl.BlockSpec(memory_space=pltpu.SMEM),
            pl.BlockSpec((1, 1, queries, width), lambda i, j: (i, j, 0, 0)),
            pl.BlockSpec((2, 2, queries, 2 * width), _window_of),
            pl.BlockSpec((2, queries, queries), lambda i, j: ((i + 1) // 2, 0, 0)),
        ],
        out_specs=pl.BlockSpec((1, 1, queries, width), lambda i, j: (i, j, 0, 0)),
        out_shape=jax.ShapeDtypeStruct(query.shape, jnp.float32),
    )(tau, query, ext_kv, mask)


def window_bwd(tau, query, ext_kv, grad, mask):
    row_units, col_units, queries, width = query.shape
    return pl.pallas_call(
        attn_bwd_kernel,
        grid=(row_units, col_units),
        in_specs=[
            pl.BlockSpec(memory_space=pltpu.SMEM),
            pl.BlockSpec((1, 1, queries, width), lambda i, j: (i, j, 0, 0)),
            pl.BlockSpec((2, 2, queries, 2 * width), _window_of),
            pl.BlockSpec((1, 1, queries, width), lambda i, j: (i, j, 0, 0)),
            pl.BlockSpec((2, queries, queries), lambda i, j: ((i + 1) // 2, 0, 0)),
        ],
        out_specs=[
            pl.BlockSpec((1, 1, queries, width), lambda i, j: (i, j, 0, 0)),
            pl.BlockSpec((2, 2, queries, 2 * width), _window_of),
        ],
        out_shape=[
            jax.ShapeDtypeStruct(query.shape, jnp.float32),
            jax.ShapeDtypeStruct(ext_kv.shape, jnp.float32),
        ],
    )(tau, query, ext_kv, grad, mask)


def with_halo(shard, sides, width, wrap):
    for axis, dim in sides:
        peers, length = (lax.axis_size(axis), shard.shape[dim])
        up = [(i, (i + 1) % peers) for i in range(peers if wrap else peers - 1)]
        down = [(j, i) for i, j in up]
        last = lax.slice_in_dim(shard, length - width, length, axis=dim)
        initial = lax.slice_in_dim(shard, 0, width, axis=dim)
        before = lax.ppermute(last, axis, up)
        after = lax.ppermute(initial, axis, down)
        shard = jnp.concatenate([before, shard, after], axis=dim)
    return shard


def from_behind(block, axis, distance):
    devices = range(lax.axis_size(axis))
    route = [((i - distance) % len(devices), i) for i in devices]
    return lax.ppermute(block, axis, route)


def from_behind_2(block, axis, distance):
    devices = range(lax.axis_size(axis))
    route = [(i - distance, i) for i in devices if i - distance in devices]
    return lax.ppermute(block, axis, route)


def gather_rows(block, axis):
    peers = lax.axis_size(axis)
    copies = jnp.broadcast_to(block[None], (peers,) + block.shape)
    spread = lax.all_to_all(copies, axis, 0, 0, tiled=False)
    return spread.reshape((peers * block.shape[0],) + block.shape[1:])


def sum_rows(partial, axis):
    peers = lax.axis_size(axis)
    chunks = partial.reshape((peers, partial.shape[0] // peers) + partial.shape[1:])
    spread = lax.all_to_all(chunks, axis, 0, 0, tiled=False)
    return jnp.sum(spread.astype(jnp.float32), axis=0)


def sum_everywhere(partial, axis):
    peers = lax.axis_size(axis)
    own = sum_rows(partial, axis).astype(jnp.bfloat16)
    copies = jnp.broadcast_to(own[None], (peers,) + own.shape)
    spread = lax.all_to_all(copies, axis, 0, 0, tiled=False)
    return spread.reshape((peers * own.shape[0],) + own.shape[1:])


def unit_rows(vectors):
    scaling = lax.rsqrt(jnp.sum(vectors * vectors, axis=-1, keepdims=True) + UNIT_EPS)
    return (vectors * scaling, scaling)


def unit_back(vectors, scaling, gradient):
    inner_sum = jnp.sum(vectors * gradient, axis=-1, keepdims=True)
    return scaling * (gradient - vectors * (inner_sum * scaling * scaling))


def norm_forward(y_rows):
    centered = y_rows - jnp.mean(y_rows, axis=-1, keepdims=True)
    inverse = lax.rsqrt(jnp.mean(centered * centered, axis=-1, keepdims=True) + NORM_EPS)
    return (centered * inverse, inverse)


def norm_back(normed, inverse, upstream):
    mean_up = jnp.mean(upstream, axis=-1, keepdims=True)
    mean_cross = jnp.mean(upstream * normed, axis=-1, keepdims=True)
    return inverse * (upstream - mean_up - normed * mean_cross)


def query_units(own_grid):
    lat_rows = own_grid.shape[1]
    lon_cols = own_grid.shape[2]
    channels = own_grid.shape[3]
    half_h = WH // 2
    half_w = WW // 2
    shaped = own_grid.reshape(LV, lat_rows // half_h, half_h, lon_cols // half_w, half_w, channels)
    return shaped.transpose(1, 3, 0, 2, 4, 5).reshape(
        lat_rows // half_h, lon_cols // half_w, LV * half_h * half_w, channels
    )


def query_layout(units):
    row_units = units.shape[0]
    col_units = units.shape[1]
    channels = units.shape[3]
    half_h = WH // 2
    half_w = WW // 2
    shaped = units.reshape(row_units, col_units, LV, half_h, half_w, channels)
    return shaped.transpose(2, 0, 3, 1, 4, 5).reshape(
        LV, row_units * half_h, col_units * half_w, channels
    )


def cross_rows(left_mat, right_mat):
    return lax.dot_general(
        left_mat, right_mat, (((0,), (0,)), ((), ())), preferred_element_type=jnp.float32
    )


def on_device(tokens, w_qkv, w_out, gain, tau, cotangent):
    lat_rows = tokens.shape[1]
    model_width = tokens.shape[3]
    head_count = tau.shape[0]
    head_dim = model_width // head_count
    half_h = WH // 2
    half_w = WW // 2
    tok_units = query_units(tokens)
    row_units, col_units, query_count = tok_units.shape[:3]
    assert row_units == 2 and col_units == 2
    tok_count = row_units * col_units * query_count
    tok_flat = tok_units.reshape(tok_count, model_width)
    cot_flat = query_units(cotangent).reshape(tok_count, model_width).astype(jnp.float32)
    weights_all = gather_rows(jnp.concatenate([w_qkv, w_out], axis=1), "lon")
    w_qkv_all = weights_all[:, : 3 * model_width]
    w_out_all = weights_all[:, 3 * model_width :]
    projected = jnp.dot(tok_flat, w_qkv_all, preferred_element_type=jnp.float32)
    proj_b = projected.astype(jnp.bfloat16)
    query_f = proj_b[:, :model_width].astype(jnp.float32).reshape(tok_count, head_count, head_dim)
    key_f = (
        proj_b[:, model_width : 2 * model_width]
        .astype(jnp.float32)
        .reshape(tok_count, head_count, head_dim)
    )
    query_n, query_scale = unit_rows(query_f)
    key_n, key_scale = unit_rows(key_f)
    query_u = query_n.astype(jnp.bfloat16).reshape(row_units, col_units, query_count, model_width)
    key_b = key_n.astype(jnp.bfloat16).reshape(tok_count, model_width)
    kv_source = jnp.concatenate([key_b, proj_b[:, 2 * model_width :]], axis=1).reshape(
        row_units, col_units, query_count, 2 * model_width
    )
    ext_rows = with_halo(kv_source, (("lat", 0),), 1, False)
    ext_kv = with_halo(ext_rows, (("lon", 1),), 1, True)
    level_win = (jnp.arange(query_count) // (half_h * half_w) + WL // 2) // WL
    same_level = level_win[:, None] == level_win[None, :]
    block_row = jnp.arange(row_units + 2)
    first_row = lax.axis_index("lat") * lat_rows - half_h + half_h * block_row
    inside = (first_row >= 0) & (first_row < lat_rows * lax.axis_size("lat"))
    allowed = (same_level[None, :, :] & inside[:, None, None]).astype(jnp.float32)
    mixed = window_fwd(tau, query_u, ext_kv, allowed)
    attended = mixed.astype(jnp.bfloat16).reshape(tok_count, model_width)
    y_rows = jnp.dot(attended, w_out_all, preferred_element_type=jnp.float32)
    normed, inverse = norm_forward(y_rows)
    output = (tok_flat.astype(jnp.float32) + gain * normed).astype(jnp.bfloat16)
    grad_y = norm_back(normed, inverse, gain * cot_flat).astype(jnp.bfloat16)
    grad_att = jnp.dot(grad_y, w_out_all.T, preferred_element_type=jnp.float32)
    grad_u = grad_att.astype(jnp.bfloat16).reshape(row_units, col_units, query_count, model_width)
    dquery, ext_grad = window_bwd(tau, query_u, ext_kv, grad_u, allowed)
    grad_q = unit_back(
        query_f, query_scale, dquery.reshape(tok_count, head_count, head_dim)
    ).reshape(tok_count, model_width)
    west_rim = ext_grad[:, :1]
    east_rim = ext_grad[:, col_units + 1 :]
    center = ext_grad[:, 1 : col_units + 1]
    from_east = from_behind(west_rim.astype(jnp.bfloat16), "lon", -1).astype(west_rim.dtype)
    from_west = from_behind(east_rim.astype(jnp.bfloat16), "lon", 1).astype(east_rim.dtype)
    center = center.at[:, :1].add(from_west).at[:, col_units - 1 :].add(from_east)
    north_rim = center[:1]
    south_rim = center[row_units + 1 :]
    middle = center[1 : row_units + 1]
    from_south = from_behind_2(north_rim.astype(jnp.bfloat16), "lat", -1).astype(north_rim.dtype)
    from_north = from_behind_2(south_rim.astype(jnp.bfloat16), "lat", 1).astype(south_rim.dtype)
    middle = middle.at[:1].add(from_north).at[row_units - 1 :].add(from_south)
    own_grads = middle.reshape(tok_count, 2 * model_width)
    grad_k = unit_back(
        key_f, key_scale, own_grads[:, :model_width].reshape(tok_count, head_count, head_dim)
    ).reshape(tok_count, model_width)
    dvalue_src = own_grads[:, model_width:]
    grad_proj = jnp.concatenate([grad_q, grad_k, dvalue_src], axis=1).astype(jnp.bfloat16)
    grad_in = jnp.dot(grad_proj, w_qkv_all.T, preferred_element_type=jnp.float32)
    grad_tok = (cot_flat + grad_in).astype(jnp.bfloat16)
    partial = jnp.concatenate(
        [cross_rows(tok_flat, grad_proj), cross_rows(attended, grad_y)], axis=1
    ).astype(jnp.bfloat16)
    shard_sum = sum_rows(partial, "lon").astype(jnp.bfloat16)
    summed = sum_everywhere(shard_sum, "lat").astype(jnp.float32)
    grad_qkv = summed[:, : 3 * model_width]
    grad_out = summed[:, 3 * model_width :]
    unit_shape = (row_units, col_units, query_count, model_width)
    output = query_layout(output.reshape(unit_shape))
    grad_tokens = query_layout(grad_tok.reshape(unit_shape))
    return (output, grad_tokens, grad_qkv, grad_out)


def solution(mesh):
    in_specs = (
        P(None, "lat", "lon", None),
        P("lon", None),
        P("lon", None),
        P(),
        P(),
        P(None, "lat", "lon", None),
    )
    out_specs = (
        P(None, "lat", "lon", None),
        P(None, "lat", "lon", None),
        P("lon", None),
        P("lon", None),
    )
    return jax.shard_map(
        on_device, mesh=mesh, in_specs=in_specs, out_specs=out_specs, check_vma=False
    )
```

profile of v0, /device:TPU:1, one launch (start us, length us, event | category | flops | bytes accessed | tf_op | source)
XLA Modules:
  0.0 264.3 jit_solution(16536905211268002838)
XLA Ops:
  1.6 1.6 broadcast_in_dim.4
  3.2 7.6 %all-to-all-start = ((bf16[8,64,2048]{2,1,0:T(8,128)(2,1)}), bf16[8,64,2048]{2,1,0:T(8,128)(2,1)S(1)}, u32[]{:S(2)}, u32[]{:S(2)}) async-start(bf16[8,64,2048]{2,1,0:T(8,128)(2,1)} %broadcast_in_dim.4), calls=%async_computation | async-start | bytes 4194304 | tf_op jit(solution)/shard_map/all_to_all | solution.py:149
  13.6 24.8 %all-to-all-done = bf16[8,64,2048]{2,1,0:T(8,128)(2,1)S(1)} async-done(((bf16[8,64,2048]{2,1,0:T(8,128)(2,1)}), bf16[8,64,2048]{2,1,0:T(8,128)(2,1)S(1)}, u32[]{:S(2)}, u32[]{:S(2)}) %all-to-all-start) | async-done | bytes 2097184 | tf_op jit(solution)/shard_map/all_to_all | solution.py:149
  38.4 1.4 copy-done.8
  39.7 2.1 fusion
  42.9 1.3 copy.78
  45.3 1.4 copy.79
  47.8 3.8 %collective-permute-start.1 = (bf16[1,2,72,1024]{3,2,1,0:T(8,128)(2,1)}, bf16[1,2,72,1024]{3,2,1,0:T(8,128)(2,1)S(1)}, u32[]{:S(2)}, u32[]{:S(2)}) collective-permute-start(bf16[1,2,72,1024]{3,2,1,0:T(8,128)(2,1)} %bitcast.11), channel_id=1, source_target_pairs={{8,0},{16,8},{24,16},{32,24},{40,32},{48,40},{56,48},{64,56},{72,6... | collective-permute-start | bytes 884744 | tf_op jit(solution)/shard_map/ppermute | solution.py:129
  51.6 3.4 %collective-permute-start = (bf16[1,2,72,1024]{3,2,1,0:T(8,128)(2,1)}, bf16[1,2,72,1024]{3,2,1,0:T(8,128)(2,1)}, u32[]{:S(2)}, u32[]{:S(2)}) collective-permute-start(bf16[1,2,72,1024]{3,2,1,0:T(8,128)(2,1)} %bitcast.8), channel_id=1, source_target_pairs={{0,8},{8,16},{16,24},{24,32},{32,40},{40,48},{48,56},{56,64},{64,7... | collective-permute-start | bytes 884744 | tf_op jit(solution)/shard_map/ppermute | solution.py:128
  56.1 1.6 collective-permute-done.1
  57.7 1.3 collective-permute-done
  59.0 1.2 pad_maximum_fusion.2
  60.2 1.1 fusion.29
  61.9 4.5 %collective-permute-start.3 = (bf16[4,1,72,1024]{3,2,1,0:T(8,128)(2,1)}, bf16[4,1,72,1024]{3,2,1,0:T(8,128)(2,1)}, u32[]{:S(2)}, u32[]{:S(2)}) collective-permute-start(bf16[4,1,72,1024]{3,2,1,0:T(8,128)(2,1)} %get-tuple-element.61), channel_id=1, source_target_pairs={{1,0},{2,1},{3,2},{4,3},{5,4},{6,5},{7,6},{0,7},{9,8},{10,9},{11,1... | collective-permute-start | bytes 1769480 | tf_op jit(solution)/shard_map/ppermute | solution.py:129
  66.6 2.1 reshape.386
  68.7 2.1 copy.92
  70.8 1.9 multiply_convert_fusion.1.q_ref
  72.7 7.9 %collective-permute-done.2 = bf16[4,1,72,1024]{3,2,1,0:T(8,128)(2,1)} collective-permute-done((bf16[4,1,72,1024]{3,2,1,0:T(8,128)(2,1)}, bf16[4,1,72,1024]{3,2,1,0:T(8,128)(2,1)}, u32[]{:S(2)}, u32[]{:S(2)}) %collective-permute-start.2) | collective-permute-done | bytes 589856 | tf_op jit(solution)/shard_map/ppermute | solution.py:128
  80.6 10.3 %collective-permute-done.3 = bf16[4,1,72,1024]{3,2,1,0:T(8,128)(2,1)} collective-permute-done((bf16[4,1,72,1024]{3,2,1,0:T(8,128)(2,1)}, bf16[4,1,72,1024]{3,2,1,0:T(8,128)(2,1)}, u32[]{:S(2)}, u32[]{:S(2)}) %collective-permute-start.3) | collective-permute-done | bytes 589856 | tf_op jit(solution)/shard_map/ppermute | solution.py:129
  90.8 2.9 %pad_maximum_fusion.kv_ref = bf16[4,4,72,1024]{3,2,1,0:T(8,128)(2,1)} fusion(bf16[4,1,72,1024]{3,2,1,0:T(8,128)(2,1)} %collective-permute-done.3, bf16[1,2,72,1024]{3,2,1,0:T(8,128)(2,1)} %copy-done.13, bf16[2,2,72,512]{3,2,1,0:T(8,128)(2,1)S(1)} %bitcast.67, bf16[2,2,72,512]{3,2,1,0:T(8,128)(2,1)S(1)} %bitcast.69, ...), kind=kLoop, calls=%fused_computation.3 | loop fusion | flops 14155776 | bytes 4718592 | tf_op jit(solution)/shard_map/concatenate | solution.py:130
  93.7 8.4 %shard_map.93 = f32[2,2,72,512]{3,2,1,0:T(8,128)} custom-call(f32[8]{0:T(128)} %tau_ref.3, bf16[2,2,72,512]{3,2,1,0:T(8,128)(2,1)} %multiply_convert_fusion.1.q_ref, bf16[4,4,72,1024]{3,2,1,0:T(8,128)(2,1)} %pad_maximum_fusion.kv_ref, f32[4,72,72]{2,1,0:T(8,128)} %and_convert_fusion.mask_ref), custom_call_target="tpu_custom_call" | custom-call | tf_op jit(solution)/shard_map/pallas_call | solution.py:84
  102.1 1.1 convert_element_type.95
  103.3 1.5 fusion.31
  106.3 2.2 convolution_convert_fusion.3
  108.5 21.5 %shard_map.94 = (f32[2,2,72,512]{3,2,1,0:T(8,128)}, f32[4,4,72,1024]{3,2,1,0:T(8,128)}) custom-call(f32[8]{0:T(128)} %tau_ref.3, bf16[2,2,72,512]{3,2,1,0:T(8,128)(2,1)} %multiply_convert_fusion.1.q_ref, bf16[4,4,72,1024]{3,2,1,0:T(8,128)(2,1)} %pad_maximum_fusion.kv_ref, bf16[2,2,72,512]{3,2,1,0:T(8,128)(2,1)} %bitcast.87, ...), custom_call_target="tpu_custom_call" | custom-call | tf_op jit(solution)/shard_map/pallas_call | solution.py:100
  130.0 2.7 %convert.34 = bf16[4,4,72,1024]{3,2,1,0:T(8,128)(2,1)S(1)} convert(f32[4,4,72,1024]{3,2,1,0:T(8,128)} %get-tuple-element.55) | non-fusion elementwise | flops 1179648 | bytes 7077888 | tf_op jit(solution)/shard_map/convert.18
  132.7 1.1 fusion.27
  134.9 4.0 %collective-permute-start.5 = (bf16[4,1,72,1024]{3,2,1,0:T(8,128)(2,1)}, bf16[4,1,72,1024]{3,2,1,0:T(8,128)(2,1)}, u32[]{:S(2)}, u32[]{:S(2)}) collective-permute-start(bf16[4,1,72,1024]{3,2,1,0:T(8,128)(2,1)} %get-tuple-element.56), channel_id=1, source_target_pairs={{1,0},{2,1},{3,2},{4,3},{5,4},{6,5},{7,6},{0,7},{9,8},{10,9},{11,1... | collective-permute-start | bytes 1769480 | tf_op jit(solution)/shard_map/ppermute | solution.py:137
  140.0 1.8 slice.197
  142.7 2.4 reshape.377
  145.1 2.6 copy.83
  147.7 2.2 convolution_convert_fusion.2
  149.9 2.3 collective-permute-done.4
  152.3 1.6 add_dynamic-update-slice_fusion
  153.9 9.3 %collective-permute-done.5 = bf16[4,1,72,1024]{3,2,1,0:T(8,128)(2,1)} collective-permute-done((bf16[4,1,72,1024]{3,2,1,0:T(8,128)(2,1)}, bf16[4,1,72,1024]{3,2,1,0:T(8,128)(2,1)}, u32[]{:S(2)}, u32[]{:S(2)}) %collective-permute-start.5) | collective-permute-done | bytes 589856 | tf_op jit(solution)/shard_map/ppermute | solution.py:137
  163.2 1.4 fusion.10
  165.6 2.8 %collective-permute-start.6 = (bf16[1,2,72,1024]{3,2,1,0:T(8,128)(2,1)}, bf16[1,2,72,1024]{3,2,1,0:T(8,128)(2,1)}, u32[]{:S(2)}, u32[]{:S(2)}) collective-permute-start(bf16[1,2,72,1024]{3,2,1,0:T(8,128)(2,1)} %get-tuple-element.59), channel_id=1, source_target_pairs={{0,8},{8,16},{16,24},{24,32},{32,40},{40,48},{48,56},{56,64},{64,7... | collective-permute-start | bytes 884744 | tf_op jit(solution)/shard_map/ppermute | solution.py:143
  168.5 2.5 collective-permute-start.7
  173.4 3.5 %collective-permute-done.7 = bf16[1,2,72,1024]{3,2,1,0:T(8,128)(2,1)} collective-permute-done((bf16[1,2,72,1024]{3,2,1,0:T(8,128)(2,1)}, bf16[1,2,72,1024]{3,2,1,0:T(8,128)(2,1)}, u32[]{:S(2)}, u32[]{:S(2)}) %collective-permute-start.7) | collective-permute-done | bytes 294944 | tf_op jit(solution)/shard_map/ppermute | solution.py:143
  176.9 1.1 fusion.15
  178.8 1.9 convert_multiply_fusion.1
  180.6 1.4 copy.86
  183.3 2.1 fusion.18
  187.0 30.4 %all_to_all.20 = bf16[8,64,2048]{2,1,0:T(8,128)(2,1)S(1)} all-to-all(bf16[8,64,2048]{2,1,0:T(8,128)(2,1)S(1)} %pad_maximum_fusion.1), channel_id=1, replica_groups=mesh['lat'=32,'lon'=8] {'lon'}, dimensions={0} | all-to-all | bytes 4194304 | tf_op jit(solution)/shard_map/all_to_all | solution.py:156
  218.7 24.4 %all_to_all.21 = bf16[32,2,2048]{2,1,0:T(2,128)(2,1)S(1)} all-to-all(bf16[32,2,2048]{2,1,0:T(2,128)(2,1)} %reshape.380), channel_id=1, replica_groups=mesh['lat'=32,'lon'=8] {'lat'}, dimensions={0} | all-to-all | bytes 524288 | tf_op jit(solution)/shard_map/all_to_all | solution.py:156
  244.1 5.7 %all-to-all-start.3 = ((bf16[32,2,2048]{2,1,0:T(2,128)(2,1)}), bf16[32,2,2048]{2,1,0:T(2,128)(2,1)}, u32[]{:S(2)}, u32[]{:S(2)}) async-start(bf16[32,2,2048]{2,1,0:T(2,128)(2,1)} %broadcast_in_dim.5), calls=%async_computation.3 | async-start | bytes 524288 | tf_op jit(solution)/shard_map/all_to_all | solution.py:164
  250.8 1.8 fusion.7
  253.6 8.3 %all-to-all-done.3 = bf16[32,2,2048]{2,1,0:T(2,128)(2,1)} async-done(((bf16[32,2,2048]{2,1,0:T(2,128)(2,1)}), bf16[32,2,2048]{2,1,0:T(2,128)(2,1)}, u32[]{:S(2)}, u32[]{:S(2)}) %all-to-all-start.3) | async-done | bytes 262176 | tf_op jit(solution)/shard_map/all_to_all | solution.py:164
  (110 shorter events, 26.8 us)
Async XLA Ops:
  3.2 7.6 %copy-start.18 = (bf16[4,6,12,512]{3,0,2,1:T(4,128)(2,1)S(1)}, bf16[4,6,12,512]{3,0,2,1:T(4,128)(2,1)}, u32[]{:S(2)}) copy-start(bf16[4,6,12,512]{3,0,2,1:T(4,128)(2,1)} %param.19) | copy-start | bytes 884740
  3.2 7.7 %copy-start.24 = (f32[512]{0:T(512)S(1)}, f32[512]{0:T(512)}, u32[]{:S(2)}) copy-start(f32[512]{0:T(512)} %param.17) | copy-start | bytes 6148
  3.2 35.1 %all-to-all-start = ((bf16[8,64,2048]{2,1,0:T(8,128)(2,1)}), bf16[8,64,2048]{2,1,0:T(8,128)(2,1)S(1)}, u32[]{:S(2)}, u32[]{:S(2)}) async-start(bf16[8,64,2048]{2,1,0:T(8,128)(2,1)} %broadcast_in_dim.4), calls=%async_computation | async-start | bytes 4194304 | tf_op jit(solution)/shard_map/all_to_all | solution.py:149
  13.4 91.8 %copy-start.2 = (f32[288,512]{1,0:T(8,128)}, f32[288,512]{1,0:T(8,128)S(1)}, u32[]{:S(2)}) copy-start(f32[288,512]{1,0:T(8,128)S(1)} %reshape.381) | copy-start | bytes 1769476
  38.4 1.4 copy-start.8
  41.9 4.8 %copy-start.4 = (bf16[288,1536]{1,0:T(8,128)(2,1)}, bf16[288,1536]{1,0:T(8,128)(2,1)S(1)}, u32[]{:S(2)}) copy-start(bf16[288,1536]{1,0:T(8,128)(2,1)S(1)} %fusion) | copy-start | bytes 2654212
  46.7 13.5 %copy-start = (f32[288,512]{1,0:T(8,128)}, f32[288,512]{1,0:T(8,128)S(1)}, u32[]{:S(2)}) copy-start(f32[288,512]{1,0:T(8,128)S(1)} %copy.79) | copy-start | bytes 1769476
  46.8 9.0 %copy-start.6 = (bf16[288,512]{1,0:T(8,128)(2,1)}, bf16[288,512]{1,0:T(8,128)(2,1)S(1)}, u32[]{:S(2)}) copy-start(bf16[288,512]{1,0:T(8,128)(2,1)S(1)} %fusion.11) | copy-start | bytes 884740
  47.8 9.9 %collective-permute-start.1 = (bf16[1,2,72,1024]{3,2,1,0:T(8,128)(2,1)}, bf16[1,2,72,1024]{3,2,1,0:T(8,128)(2,1)S(1)}, u32[]{:S(2)}, u32[]{:S(2)}) collective-permute-start(bf16[1,2,72,1024]{3,2,1,0:T(8,128)(2,1)} %bitcast.11), channel_id=1, source_target_pairs={{8,0},{16,8},{24,16},{32,24},{40,32},{48,40},{56,48},{64,56},{72,6... | collective-permute-start | bytes 884744 | tf_op jit(solution)/shard_map/ppermute | solution.py:129
  51.6 7.4 %collective-permute-start = (bf16[1,2,72,1024]{3,2,1,0:T(8,128)(2,1)}, bf16[1,2,72,1024]{3,2,1,0:T(8,128)(2,1)}, u32[]{:S(2)}, u32[]{:S(2)}) collective-permute-start(bf16[1,2,72,1024]{3,2,1,0:T(8,128)(2,1)} %bitcast.8), channel_id=1, source_target_pairs={{0,8},{8,16},{16,24},{24,32},{32,40},{40,48},{48,56},{56,64},{64,7... | collective-permute-start | bytes 884744 | tf_op jit(solution)/shard_map/ppermute | solution.py:128
  57.7 3.6 %copy-start.13 = (bf16[1,2,72,1024]{3,2,1,0:T(8,128)(2,1)}, bf16[1,2,72,1024]{3,2,1,0:T(8,128)(2,1)S(1)}, u32[]{:S(2)}) copy-start(bf16[1,2,72,1024]{3,2,1,0:T(8,128)(2,1)S(1)} %collective-permute-done.1) | copy-start | bytes 884740
  61.3 19.2 %collective-permute-start.2 = (bf16[4,1,72,1024]{3,2,1,0:T(8,128)(2,1)}, bf16[4,1,72,1024]{3,2,1,0:T(8,128)(2,1)}, u32[]{:S(2)}, u32[]{:S(2)}) collective-permute-start(bf16[4,1,72,1024]{3,2,1,0:T(8,128)(2,1)} %get-tuple-element.60), channel_id=1, source_target_pairs={{0,1},{1,2},{2,3},{3,4},{4,5},{5,6},{6,7},{7,0},{8,9},{9,10},{10,1... | collective-permute-start | bytes 1769480 | tf_op jit(solution)/shard_map/ppermute | solution.py:128
  61.9 29.0 %collective-permute-start.3 = (bf16[4,1,72,1024]{3,2,1,0:T(8,128)(2,1)}, bf16[4,1,72,1024]{3,2,1,0:T(8,128)(2,1)}, u32[]{:S(2)}, u32[]{:S(2)}) collective-permute-start(bf16[4,1,72,1024]{3,2,1,0:T(8,128)(2,1)} %get-tuple-element.61), channel_id=1, source_target_pairs={{1,0},{2,1},{3,2},{4,3},{5,4},{6,5},{7,6},{0,7},{9,8},{10,9},{11,1... | collective-permute-start | bytes 1769480 | tf_op jit(solution)/shard_map/ppermute | solution.py:129
  66.5 4.3 %copy-start.22 = (f32[288,8]{0,1:T(8,128)}, f32[288,8]{0,1:T(8,128)S(1)}, u32[]{:S(2)}) copy-start(f32[288,8]{0,1:T(8,128)S(1)} %multiply_reduce_fusion.1) | copy-start | bytes 27652
  66.6 24.2 %copy-start.7 = (bf16[288,512]{1,0:T(8,128)(2,1)S(1)}, bf16[288,512]{1,0:T(8,128)(2,1)}, u32[]{:S(2)}) copy-start(bf16[288,512]{1,0:T(8,128)(2,1)} %copy-done.6) | copy-start | bytes 884740
  102.1 3.2 %copy-start.14 = (bf16[288,512]{1,0:T(8,128)(2,1)S(1)}, bf16[288,512]{1,0:T(8,128)(2,1)}, u32[]{:S(2)}) copy-start(bf16[288,512]{1,0:T(8,128)(2,1)} %reshape_reshape.10) | copy-start | bytes 884740
  106.3 23.7 %copy-start.17 = (bf16[288,512]{1,0:T(8,128)(2,1)}, bf16[288,512]{1,0:T(8,128)(2,1)S(1)}, u32[]{:S(2)}) copy-start(bf16[288,512]{1,0:T(8,128)(2,1)S(1)} %get-tuple-element.66) | copy-start | bytes 884740
  133.8 18.4 %collective-permute-start.4 = (bf16[4,1,72,1024]{3,2,1,0:T(8,128)(2,1)}, bf16[4,1,72,1024]{3,2,1,0:T(8,128)(2,1)}, u32[]{:S(2)}, u32[]{:S(2)}) collective-permute-start(bf16[4,1,72,1024]{3,2,1,0:T(8,128)(2,1)} %get-tuple-element.57), channel_id=1, source_target_pairs={{7,0},{0,1},{1,2},{2,3},{3,4},{4,5},{5,6},{6,7},{15,8},{8,9},{9,10... | collective-permute-start | bytes 1769480 | tf_op jit(solution)/shard_map/ppermute | solution.py:137
  134.9 28.3 %collective-permute-start.5 = (bf16[4,1,72,1024]{3,2,1,0:T(8,128)(2,1)}, bf16[4,1,72,1024]{3,2,1,0:T(8,128)(2,1)}, u32[]{:S(2)}, u32[]{:S(2)}) collective-permute-start(bf16[4,1,72,1024]{3,2,1,0:T(8,128)(2,1)} %get-tuple-element.56), channel_id=1, source_target_pairs={{1,0},{2,1},{3,2},{4,3},{5,4},{6,5},{7,6},{0,7},{9,8},{10,9},{11,1... | collective-permute-start | bytes 1769480 | tf_op jit(solution)/shard_map/ppermute | solution.py:137
  142.7 5.0 %copy-start.12 = (bf16[512,288]{1,0:T(8,128)(2,1)S(1)}, bf16[512,288]{1,0:T(8,128)(2,1)}, u32[]{:S(2)}) copy-start(bf16[512,288]{1,0:T(8,128)(2,1)} %copy.90) | copy-start | bytes 884740
  164.6 3.8 %copy-start.10 = (f32[288,8,64]{0,2,1:T(8,128)S(1)}, f32[288,8,64]{0,2,1:T(8,128)}, u32[]{:S(2)}) copy-start(f32[288,8,64]{0,2,1:T(8,128)} %copy.83) | copy-start | bytes 1769476
  164.8 6.3 %copy-start.23 = (f32[288,8]{0,1:T(8,128)S(1)}, f32[288,8]{0,1:T(8,128)}, u32[]{:S(2)}) copy-start(f32[288,8]{0,1:T(8,128)} %copy-done.22) | copy-start | bytes 27652
  165.6 6.7 %collective-permute-start.6 = (bf16[1,2,72,1024]{3,2,1,0:T(8,128)(2,1)}, bf16[1,2,72,1024]{3,2,1,0:T(8,128)(2,1)}, u32[]{:S(2)}, u32[]{:S(2)}) collective-permute-start(bf16[1,2,72,1024]{3,2,1,0:T(8,128)(2,1)} %get-tuple-element.59), channel_id=1, source_target_pairs={{0,8},{8,16},{16,24},{24,32},{32,40},{40,48},{48,56},{56,64},{64,7... | collective-permute-start | bytes 884744 | tf_op jit(solution)/shard_map/ppermute | solution.py:143
  168.5 8.4 %collective-permute-start.7 = (bf16[1,2,72,1024]{3,2,1,0:T(8,128)(2,1)}, bf16[1,2,72,1024]{3,2,1,0:T(8,128)(2,1)}, u32[]{:S(2)}, u32[]{:S(2)}) collective-permute-start(bf16[1,2,72,1024]{3,2,1,0:T(8,128)(2,1)} %get-tuple-element.58), channel_id=1, source_target_pairs={{8,0},{16,8},{24,16},{32,24},{40,32},{48,40},{56,48},{64,56},{72,6... | collective-permute-start | bytes 884744 | tf_op jit(solution)/shard_map/ppermute | solution.py:143
  180.6 2.7 %copy-start.1 = (f32[288,512]{1,0:T(8,128)S(1)}, f32[288,512]{1,0:T(8,128)}, u32[]{:S(2)}) copy-start(f32[288,512]{1,0:T(8,128)} %copy-done) | copy-start | bytes 1769476
  180.6 2.7 %copy-start.5 = (bf16[288,1536]{1,0:T(8,128)(2,1)S(1)}, bf16[288,1536]{1,0:T(8,128)(2,1)}, u32[]{:S(2)}) copy-start(bf16[288,1536]{1,0:T(8,128)(2,1)} %copy-done.4) | copy-start | bytes 2654212
  183.3 2.2 copy-start.15
  183.3 2.2 copy-start.21
  185.5 1.1 copy-start.19
  185.5 1.1 copy-start.20
  185.5 1.2 copy-start.11
  217.4 32.4 %copy-start.16 = (bf16[288,512]{1,0:T(8,128)(2,1)S(1)}, bf16[288,512]{1,0:T(8,128)(2,1)}, u32[]{:S(2)}) copy-start(bf16[288,512]{1,0:T(8,128)(2,1)} %get-tuple-element.67) | copy-start | bytes 884740
  217.8 33.0 %copy-start.3 = (f32[288,512]{1,0:T(8,128)S(1)}, f32[288,512]{1,0:T(8,128)}, u32[]{:S(2)}) copy-start(f32[288,512]{1,0:T(8,128)} %copy-done.2) | copy-start | bytes 1769476
  217.8 33.0 %copy-start.9 = (bf16[8,64,2048]{2,1,0:T(8,128)(2,1)S(1)}, bf16[8,64,2048]{2,1,0:T(8,128)(2,1)}, u32[]{:S(2)}) copy-start(bf16[8,64,2048]{2,1,0:T(8,128)(2,1)} %copy-done.8) | copy-start | bytes 6291460
  244.1 17.8 %all-to-all-start.3 = ((bf16[32,2,2048]{2,1,0:T(2,128)(2,1)}), bf16[32,2,2048]{2,1,0:T(2,128)(2,1)}, u32[]{:S(2)}, u32[]{:S(2)}) async-start(bf16[32,2,2048]{2,1,0:T(2,128)(2,1)} %broadcast_in_dim.5), calls=%async_computation.3 | async-start | bytes 524288 | tf_op jit(solution)/shard_map/all_to_all | solution.py:164
where the time goes:
time: 266 us; the launch traced here: 264 us
  waiting for transfers between devices  69.4 us (26%)
  blocking collectives  54.7 us (21%)
  local copies, waits for them, and re-layouts  36.4 us (14%)
  starting transfers between devices  35.9 us (13%)
  Pallas kernels  29.9 us (11%)
  other arithmetic  26 us (10%)
  matrix products  10.8 us (4%)
    all_to_all x2, blocking collectives, sum_rows(): spread = lax.all_to_all(chunks, axis, 0, 0, tiled=False)  54.7 us
    all_to_all x1, waiting for transfers between devices, gather_rows(): spread = lax.all_to_all(copies, axis, 0, 0, tiled=False)  24.8 us
    pallas_call x1, Pallas kernels, window_bwd(): pl.pallas_call(attn_bwd_kernel, grid=(row_units, col_units), in_specs=[pl...  21.5 us
    ppermute x2, waiting for transfers between devices, with_halo(): after = lax.ppermute(initial, axis, down)  11.9 us
    ppermute x2, waiting for transfers between devices, from_behind(): return lax.ppermute(block, axis, route)  11.7 us
    ppermute x2, waiting for transfers between devices, with_halo(): before = lax.ppermute(last, axis, up)  9.18 us
    pallas_call x1, Pallas kernels, window_fwd(): pl.pallas_call(attn_fwd_kernel, grid=(row_units, col_units), in_specs=[pl...  8.4 us
    ppermute x2, starting transfers between devices, with_halo(): after = lax.ppermute(initial, axis, down)  8.35 us
  transfers between devices with their start and end apart: 10, of which 10 were waited for; matrix products, arithmetic and copies ran while one was open for 11% of the time, Pallas kernels for 0%

commit v1 on v0

--- a/solution.py
+++ b/solution.py
@@ -165,6 +165,41 @@
     return spread.reshape((peers * own.shape[0],) + own.shape[1:])
 
 
+def chip_partner(block):
+    peers = lax.axis_size("lat")
+    return lax.ppermute(block, "lat", [(i, i ^ 1) for i in range(peers)])
+
+
+def gather_rows_paired(block, axis):
+    core = lax.axis_index("lat") % 2
+    halves = block.reshape(block.shape[0], 2, block.shape[1] // 2)
+    mine = lax.dynamic_index_in_dim(halves, core, axis=1, keepdims=False)
+    gathered = gather_rows(mine, axis)
+    other = chip_partner(gathered)
+    return jnp.where(
+        core == 0,
+        jnp.concatenate([gathered, other], axis=1),
+        jnp.concatenate([other, gathered], axis=1),
+    )
+
+
+def sum_rows_paired(partial, axis):
+    peers = lax.axis_size(axis)
+    core = lax.axis_index("lat") % 2
+    blocks = partial.reshape(peers, 2, partial.shape[0] // (2 * peers), partial.shape[1])
+    keep = lax.dynamic_index_in_dim(blocks, core, axis=1, keepdims=False)
+    give = lax.dynamic_index_in_dim(blocks, 1 - core, axis=1, keepdims=False)
+    pair = keep.astype(jnp.float32) + chip_partner(give).astype(jnp.float32)
+    own = sum_rows(pair.astype(jnp.bfloat16).reshape(-1, partial.shape[1]), axis)
+    own = own.astype(jnp.bfloat16)
+    empty = jnp.zeros_like(own)
+    return jnp.where(
+        core == 0,
+        jnp.concatenate([own, empty], axis=0),
+        jnp.concatenate([empty, own], axis=0),
+    )
+
+
 def unit_rows(vectors):
     scaling = lax.rsqrt(jnp.sum(vectors * vectors, axis=-1, keepdims=True) + UNIT_EPS)
     return (vectors * scaling, scaling)
@@ -230,7 +265,7 @@
     tok_count = row_units * col_units * query_count
     tok_flat = tok_units.reshape(tok_count, model_width)
     cot_flat = query_units(cotangent).reshape(tok_count, model_width).astype(jnp.float32)
-    weights_all = gather_rows(jnp.concatenate([w_qkv, w_out], axis=1), "lon")
+    weights_all = gather_rows_paired(jnp.concatenate([w_qkv, w_out], axis=1), "lon")
     w_qkv_all = weights_all[:, : 3 * model_width]
     w_out_all = weights_all[:, 3 * model_width :]
     projected = jnp.dot(tok_flat, w_qkv_all, preferred_element_type=jnp.float32)
@@ -291,7 +326,7 @@
     partial = jnp.concatenate(
         [cross_rows(tok_flat, grad_proj), cross_rows(attended, grad_y)], axis=1
     ).astype(jnp.bfloat16)
-    shard_sum = sum_rows(partial, "lon").astype(jnp.bfloat16)
+    shard_sum = sum_rows_paired(partial, "lon")
     summed = sum_everywhere(shard_sum, "lat").astype(jnp.float32)
     grad_qkv = summed[:, : 3 * model_width]
     grad_out = summed[:, 3 * model_width :]

time: 266 us -> 250 us (0.940)
  waiting for transfers between devices: 69.4 us -> 48.8 us
  blocking collectives: 54.7 us -> 68.6 us
  starting transfers between devices: 35.9 us -> 28.7 us
  local copies, waits for them, and re-layouts: 36.4 us -> 33.1 us
    all_to_all x1 -> x0, waiting for transfers between devices: 24.8 us -> none  [gather_rows(): spread = lax.all_to_all(copies, axis, 0, 0, tiled=False)]
    all_to_all x0 -> x1, blocking collectives: none -> 23.7 us  [gather_rows(): spread = lax.all_to_all(copies, axis, 0, 0, tiled=False)]
    all_to_all x2, blocking collectives: 54.7 us -> 44.9 us  [sum_rows(): spread = lax.all_to_all(chunks, axis, 0, 0, tiled=False)]
    all_to_all x1 -> x0, starting transfers between devices: 7.61 us -> none  [gather_rows(): spread = lax.all_to_all(copies, axis, 0, 0, tiled=False)]
    ppermute x0 -> x2, waiting for transfers between devices: none -> 3.97 us  [chip_partner(): return lax.ppermute(block, 'lat', [(i, i ^ 1) for i in range(peers)])]
  transfers between devices with their start and end apart: 10 -> 11, of which waited for: 10 -> 10; matrix products, arithmetic and copies ran while one was open for 11% -> 11% of each run, Pallas kernels for 0% -> 0%
where the time goes in v1:
time: 250 us; the launch traced here: 248 us
  blocking collectives  68.6 us (27%)
  waiting for transfers between devices  48.8 us (20%)
  local copies, waits for them, and re-layouts  33.1 us (13%)
  Pallas kernels  29.9 us (12%)
  starting transfers between devices  28.7 us (11%)
  other arithmetic  28.4 us (11%)
  matrix products  9.33 us (4%)
    all_to_all x2, blocking collectives, sum_rows(): spread = lax.all_to_all(chunks, axis, 0, 0, tiled=False)  44.9 us
    all_to_all x1, blocking collectives, gather_rows(): spread = lax.all_to_all(copies, axis, 0, 0, tiled=False)  23.7 us
    pallas_call x1, Pallas kernels, window_bwd(): pl.pallas_call(attn_bwd_kernel, grid=(row_units, col_units), in_specs=[pl...  21.5 us
    ppermute x2, waiting for transfers between devices, with_halo(): after = lax.ppermute(initial, axis, down)  11.8 us
    ppermute x2, waiting for transfers between devices, from_behind(): return lax.ppermute(block, axis, route)  11.8 us
    ppermute x2, waiting for transfers between devices, with_halo(): before = lax.ppermute(last, axis, up)  9.45 us
    pallas_call x1, Pallas kernels, window_fwd(): pl.pallas_call(attn_fwd_kernel, grid=(row_units, col_units), in_specs=[pl...  8.4 us
    all_to_all x1, waiting for transfers between devices, sum_everywhere(): spread = lax.all_to_all(copies, axis, 0, 0, tiled=False)  8.32 us
  transfers between devices with their start and end apart: 11, of which 10 were waited for; matrix products, arithmetic and copies ran while one was open for 11% of the time, Pallas kernels for 0%

profile of v1, /device:TPU:1, one launch (start us, length us, event | category | flops | bytes accessed | tf_op | source)
XLA Modules:
  0.0 248.2 jit_solution(14446554253217705486)
XLA Ops:
  2.3 23.7 %all_to_all.20 = bf16[8,64,1024]{2,1,0:T(8,128)(2,1)S(1)} all-to-all(bf16[8,64,1024]{2,1,0:T(8,128)(2,1)S(1)} %broadcast_in_dim.7), channel_id=1, replica_groups=mesh['lat'=32,'lon'=8] {'lon'}, dimensions={0} | all-to-all | bytes 2097152 | tf_op jit(solution)/shard_map/all_to_all | solution.py:149
  26.0 1.9 collective-permute-start
  29.0 1.3 collective-permute-done
  30.3 2.4 maximum_select_fusion
  35.2 1.3 copy.78
  37.5 1.4 copy.79
  40.0 2.3 collective-permute-start.2
  42.3 3.4 %collective-permute-start.1 = (bf16[1,2,72,1024]{3,2,1,0:T(8,128)(2,1)}, bf16[1,2,72,1024]{3,2,1,0:T(8,128)(2,1)}, u32[]{:S(2)}, u32[]{:S(2)}) collective-permute-start(bf16[1,2,72,1024]{3,2,1,0:T(8,128)(2,1)} %bitcast.8), channel_id=1, source_target_pairs={{0,8},{8,16},{16,24},{24,32},{32,40},{40,48},{48,56},{56,64},{64,7... | collective-permute-start | bytes 884744 | tf_op jit(solution)/shard_map/ppermute | solution.py:128
  46.8 1.6 collective-permute-done.2
  48.4 1.3 collective-permute-done.1
  49.7 1.2 pad_maximum_fusion.1
  50.9 1.1 fusion.34
  52.6 4.5 %collective-permute-start.4 = (bf16[4,1,72,1024]{3,2,1,0:T(8,128)(2,1)}, bf16[4,1,72,1024]{3,2,1,0:T(8,128)(2,1)}, u32[]{:S(2)}, u32[]{:S(2)}) collective-permute-start(bf16[4,1,72,1024]{3,2,1,0:T(8,128)(2,1)} %get-tuple-element.61), channel_id=1, source_target_pairs={{1,0},{2,1},{3,2},{4,3},{5,4},{6,5},{7,6},{0,7},{9,8},{10,9},{11,1... | collective-permute-start | bytes 1769480 | tf_op jit(solution)/shard_map/ppermute | solution.py:129
  57.3 2.1 reshape.394
  59.4 2.1 copy.93
  61.5 1.9 multiply_convert_fusion.1.q_ref
  63.4 8.2 %collective-permute-done.3 = bf16[4,1,72,1024]{3,2,1,0:T(8,128)(2,1)} collective-permute-done((bf16[4,1,72,1024]{3,2,1,0:T(8,128)(2,1)}, bf16[4,1,72,1024]{3,2,1,0:T(8,128)(2,1)}, u32[]{:S(2)}, u32[]{:S(2)}) %collective-permute-start.3) | collective-permute-done | bytes 589856 | tf_op jit(solution)/shard_map/ppermute | solution.py:128
  71.5 10.2 %collective-permute-done.4 = bf16[4,1,72,1024]{3,2,1,0:T(8,128)(2,1)} collective-permute-done((bf16[4,1,72,1024]{3,2,1,0:T(8,128)(2,1)}, bf16[4,1,72,1024]{3,2,1,0:T(8,128)(2,1)}, u32[]{:S(2)}, u32[]{:S(2)}) %collective-permute-start.4) | collective-permute-done | bytes 589856 | tf_op jit(solution)/shard_map/ppermute | solution.py:129
  81.7 2.9 %pad_maximum_fusion.kv_ref = bf16[4,4,72,1024]{3,2,1,0:T(8,128)(2,1)} fusion(bf16[4,1,72,1024]{3,2,1,0:T(8,128)(2,1)} %collective-permute-done.4, bf16[1,2,72,1024]{3,2,1,0:T(8,128)(2,1)} %copy-done.13, bf16[2,2,72,512]{3,2,1,0:T(8,128)(2,1)S(1)} %bitcast.81, bf16[2,2,72,512]{3,2,1,0:T(8,128)(2,1)S(1)} %bitcast.83, ...), kind=kLoop, calls=%fused_computation.5 | loop fusion | flops 14155776 | bytes 4718592 | tf_op jit(solution)/shard_map/concatenate | solution.py:130
  84.6 8.4 %shard_map.93 = f32[2,2,72,512]{3,2,1,0:T(8,128)} custom-call(f32[8]{0:T(128)} %tau_ref.3, bf16[2,2,72,512]{3,2,1,0:T(8,128)(2,1)} %multiply_convert_fusion.1.q_ref, bf16[4,4,72,1024]{3,2,1,0:T(8,128)(2,1)} %pad_maximum_fusion.kv_ref, f32[4,72,72]{2,1,0:T(8,128)} %and_convert_fusion.mask_ref), custom_call_target="tpu_custom_call" | custom-call | tf_op jit(solution)/shard_map/pallas_call | solution.py:84
  93.0 1.1 convert_element_type.107
  94.2 1.5 fusion.36
  97.2 2.2 convolution_convert_fusion.3
  99.4 21.5 %shard_map.94 = (f32[2,2,72,512]{3,2,1,0:T(8,128)}, f32[4,4,72,1024]{3,2,1,0:T(8,128)}) custom-call(f32[8]{0:T(128)} %tau_ref.3, bf16[2,2,72,512]{3,2,1,0:T(8,128)(2,1)} %multiply_convert_fusion.1.q_ref, bf16[4,4,72,1024]{3,2,1,0:T(8,128)(2,1)} %pad_maximum_fusion.kv_ref, bf16[2,2,72,512]{3,2,1,0:T(8,128)(2,1)} %bitcast.99, ...), custom_call_target="tpu_custom_call" | custom-call | tf_op jit(solution)/shard_map/pallas_call | solution.py:100
  120.9 2.7 %convert.35 = bf16[4,4,72,1024]{3,2,1,0:T(8,128)(2,1)S(1)} convert(f32[4,4,72,1024]{3,2,1,0:T(8,128)} %get-tuple-element.55) | non-fusion elementwise | flops 1179648 | bytes 7077888 | tf_op jit(solution)/shard_map/convert.19
  123.6 1.1 fusion.32
  125.6 4.2 %collective-permute-start.6 = (bf16[4,1,72,1024]{3,2,1,0:T(8,128)(2,1)}, bf16[4,1,72,1024]{3,2,1,0:T(8,128)(2,1)}, u32[]{:S(2)}, u32[]{:S(2)}) collective-permute-start(bf16[4,1,72,1024]{3,2,1,0:T(8,128)(2,1)} %get-tuple-element.56), channel_id=1, source_target_pairs={{1,0},{2,1},{3,2},{4,3},{5,4},{6,5},{7,6},{0,7},{9,8},{10,9},{11,1... | collective-permute-start | bytes 1769480 | tf_op jit(solution)/shard_map/ppermute | solution.py:137
  130.9 1.8 slice.197
  133.6 2.4 reshape.384
  136.0 2.6 %copy.83 = f32[288,8,64]{0,2,1:T(8,128)} copy(f32[288,8,64]{2,1,0:T(8,128)} %reshape.384) | data formatting | bytes 1179648 | tf_op jit(solution)/shard_map/reshape | solution.py:304
  138.6 2.2 convolution_convert_fusion.2
  140.8 2.8 %collective-permute-done.5 = bf16[4,1,72,1024]{3,2,1,0:T(8,128)(2,1)} collective-permute-done((bf16[4,1,72,1024]{3,2,1,0:T(8,128)(2,1)}, bf16[4,1,72,1024]{3,2,1,0:T(8,128)(2,1)}, u32[]{:S(2)}, u32[]{:S(2)}) %collective-permute-start.5) | collective-permute-done | bytes 589856 | tf_op jit(solution)/shard_map/ppermute | solution.py:137
  143.6 1.6 add_dynamic-update-slice_fusion
  145.2 9.0 %collective-permute-done.6 = bf16[4,1,72,1024]{3,2,1,0:T(8,128)(2,1)} collective-permute-done((bf16[4,1,72,1024]{3,2,1,0:T(8,128)(2,1)}, bf16[4,1,72,1024]{3,2,1,0:T(8,128)(2,1)}, u32[]{:S(2)}, u32[]{:S(2)}) %collective-permute-start.6) | collective-permute-done | bytes 589856 | tf_op jit(solution)/shard_map/ppermute | solution.py:137
  154.2 1.4 fusion.11
  156.6 2.7 %collective-permute-start.7 = (bf16[1,2,72,1024]{3,2,1,0:T(8,128)(2,1)}, bf16[1,2,72,1024]{3,2,1,0:T(8,128)(2,1)}, u32[]{:S(2)}, u32[]{:S(2)}) collective-permute-start(bf16[1,2,72,1024]{3,2,1,0:T(8,128)(2,1)} %get-tuple-element.59), channel_id=1, source_target_pairs={{0,8},{8,16},{16,24},{24,32},{32,40},{40,48},{48,56},{56,64},{64,7... | collective-permute-start | bytes 884744 | tf_op jit(solution)/shard_map/ppermute | solution.py:143
  159.5 2.6 %collective-permute-start.8 = (bf16[1,2,72,1024]{3,2,1,0:T(8,128)(2,1)}, bf16[1,2,72,1024]{3,2,1,0:T(8,128)(2,1)}, u32[]{:S(2)}, u32[]{:S(2)}) collective-permute-start(bf16[1,2,72,1024]{3,2,1,0:T(8,128)(2,1)} %get-tuple-element.58), channel_id=1, source_target_pairs={{8,0},{16,8},{24,16},{32,24},{40,32},{48,40},{56,48},{64,56},{72,6... | collective-permute-start | bytes 884744 | tf_op jit(solution)/shard_map/ppermute | solution.py:143
  164.4 3.5 %collective-permute-done.8 = bf16[1,2,72,1024]{3,2,1,0:T(8,128)(2,1)} collective-permute-done((bf16[1,2,72,1024]{3,2,1,0:T(8,128)(2,1)}, bf16[1,2,72,1024]{3,2,1,0:T(8,128)(2,1)}, u32[]{:S(2)}, u32[]{:S(2)}) %collective-permute-start.8) | collective-permute-done | bytes 294944 | tf_op jit(solution)/shard_map/ppermute | solution.py:143
  167.8 1.1 fusion.20
  169.7 1.9 convert_multiply_fusion.1
  171.6 1.4 copy.86
  174.3 2.1 fusion.23
  177.9 2.6 %collective-permute-done.9 = bf16[8,32,2048]{2,1,0:T(8,128)(2,1)S(1)} collective-permute-done((bf16[8,32,2048]{2,1,0:T(8,128)(2,1)S(1)}, bf16[8,32,2048]{2,1,0:T(8,128)(2,1)S(1)}, u32[]{:S(2)}, u32[]{:S(2)}) %collective-permute-start.9) | collective-permute-done | bytes 1048608 | tf_op jit(solution)/shard_map/ppermute | solution.py:170
  180.9 21.6 %all_to_all.21 = bf16[8,32,2048]{2,1,0:T(8,128)(2,1)S(1)} all-to-all(bf16[8,32,2048]{2,1,0:T(8,128)(2,1)S(1)} %fusion.1), channel_id=1, replica_groups=mesh['lat'=32,'lon'=8] {'lon'}, dimensions={0} | all-to-all | bytes 2097152 | tf_op jit(solution)/shard_map/all_to_all | solution.py:156
  203.6 23.3 %all_to_all.22 = bf16[32,2,2048]{2,1,0:T(2,128)(2,1)S(1)} all-to-all(bf16[32,2,2048]{2,1,0:T(2,128)(2,1)} %reshape.387), channel_id=1, replica_groups=mesh['lat'=32,'lon'=8] {'lat'}, dimensions={0} | all-to-all | bytes 524288 | tf_op jit(solution)/shard_map/all_to_all | solution.py:156
  228.0 5.7 %all-to-all-start.3 = ((bf16[32,2,2048]{2,1,0:T(2,128)(2,1)}), bf16[32,2,2048]{2,1,0:T(2,128)(2,1)}, u32[]{:S(2)}, u32[]{:S(2)}) async-start(bf16[32,2,2048]{2,1,0:T(2,128)(2,1)} %broadcast_in_dim.8), calls=%async_computation.3 | async-start | bytes 524288 | tf_op jit(solution)/shard_map/all_to_all | solution.py:164
  234.7 1.8 fusion.8
  237.4 8.3 %all-to-all-done.3 = bf16[32,2,2048]{2,1,0:T(2,128)(2,1)} async-done(((bf16[32,2,2048]{2,1,0:T(2,128)(2,1)}), bf16[32,2,2048]{2,1,0:T(2,128)(2,1)}, u32[]{:S(2)}, u32[]{:S(2)}) %all-to-all-start.3) | async-done | bytes 262176 | tf_op jit(solution)/shard_map/all_to_all | solution.py:164
  (123 shorter events, 27.0 us)
Async XLA Ops:
  1.8 26.1 %copy-start.19 = (bf16[4,6,12,512]{3,0,2,1:T(4,128)(2,1)S(1)}, bf16[4,6,12,512]{3,0,2,1:T(4,128)(2,1)}, u32[]{:S(2)}) copy-start(bf16[4,6,12,512]{3,0,2,1:T(4,128)(2,1)} %param.19) | copy-start | bytes 884740
  2.2 25.8 %copy-start.26 = (f32[512]{0:T(512)S(1)}, f32[512]{0:T(512)}, u32[]{:S(2)}) copy-start(f32[512]{0:T(512)} %param.17) | copy-start | bytes 6148
  2.3 26.3 %copy-start.23 = (bf16[4,6,12,512]{3,0,2,1:T(4,128)(2,1)S(1)}, bf16[4,6,12,512]{3,0,2,1:T(4,128)(2,1)}, u32[]{:S(2)}) copy-start(bf16[4,6,12,512]{3,0,2,1:T(4,128)(2,1)} %param.14) | copy-start | bytes 884740
  26.0 4.3 %collective-permute-start = (bf16[512,1024]{1,0:T(8,128)(2,1)S(1)}, bf16[512,1024]{1,0:T(8,128)(2,1)}, u32[]{:S(2)}, u32[]{:S(2)}) collective-permute-start(bf16[512,1024]{1,0:T(8,128)(2,1)S(1)} %bitcast.84), channel_id=1, source_target_pairs={{0,8},{8,0},{16,24},{24,16},{32,40},{40,32},{48,56},{56,48},{64,72... | collective-permute-start | bytes 3145736 | tf_op jit(solution)/shard_map/ppermute | solution.py:170
  28.8 3.9 %copy-start.14 = (bf16[288,512]{1,0:T(8,128)(2,1)}, bf16[288,512]{1,0:T(8,128)(2,1)S(1)}, u32[]{:S(2)}) copy-start(bf16[288,512]{1,0:T(8,128)(2,1)S(1)} %reshape_reshape.10) | copy-start | bytes 884740
  28.9 67.3 %copy-start.2 = (f32[288,512]{1,0:T(8,128)}, f32[288,512]{1,0:T(8,128)S(1)}, u32[]{:S(2)}) copy-start(f32[288,512]{1,0:T(8,128)S(1)} %reshape.388) | copy-start | bytes 1769476
  32.7 1.4 copy-start.9
  34.1 4.8 %copy-start.4 = (bf16[288,1536]{1,0:T(8,128)(2,1)}, bf16[288,1536]{1,0:T(8,128)(2,1)S(1)}, u32[]{:S(2)}) copy-start(bf16[288,1536]{1,0:T(8,128)(2,1)S(1)} %fusion) | copy-start | bytes 2654212
  38.9 12.0 %copy-start = (f32[288,512]{1,0:T(8,128)}, f32[288,512]{1,0:T(8,128)S(1)}, u32[]{:S(2)}) copy-start(f32[288,512]{1,0:T(8,128)S(1)} %copy.79) | copy-start | bytes 1769476
  39.0 7.5 %copy-start.6 = (bf16[288,512]{1,0:T(8,128)(2,1)}, bf16[288,512]{1,0:T(8,128)(2,1)S(1)}, u32[]{:S(2)}) copy-start(bf16[288,512]{1,0:T(8,128)(2,1)S(1)} %fusion.16) | copy-start | bytes 884740
  40.0 8.4 %collective-permute-start.2 = (bf16[1,2,72,1024]{3,2,1,0:T(8,128)(2,1)}, bf16[1,2,72,1024]{3,2,1,0:T(8,128)(2,1)S(1)}, u32[]{:S(2)}, u32[]{:S(2)}) collective-permute-start(bf16[1,2,72,1024]{3,2,1,0:T(8,128)(2,1)} %bitcast.11), channel_id=1, source_target_pairs={{8,0},{16,8},{24,16},{32,24},{40,32},{48,40},{56,48},{64,56},{72,6... | collective-permute-start | bytes 884744 | tf_op jit(solution)/shard_map/ppermute | solution.py:129
  42.3 7.4 %collective-permute-start.1 = (bf16[1,2,72,1024]{3,2,1,0:T(8,128)(2,1)}, bf16[1,2,72,1024]{3,2,1,0:T(8,128)(2,1)}, u32[]{:S(2)}, u32[]{:S(2)}) collective-permute-start(bf16[1,2,72,1024]{3,2,1,0:T(8,128)(2,1)} %bitcast.8), channel_id=1, source_target_pairs={{0,8},{8,16},{16,24},{24,32},{32,40},{40,48},{48,56},{56,64},{64,7... | collective-permute-start | bytes 884744 | tf_op jit(solution)/shard_map/ppermute | solution.py:128
  48.4 3.6 %copy-start.13 = (bf16[1,2,72,1024]{3,2,1,0:T(8,128)(2,1)}, bf16[1,2,72,1024]{3,2,1,0:T(8,128)(2,1)S(1)}, u32[]{:S(2)}) copy-start(bf16[1,2,72,1024]{3,2,1,0:T(8,128)(2,1)S(1)} %collective-permute-done.2) | copy-start | bytes 884740
  52.0 19.5 %collective-permute-start.3 = (bf16[4,1,72,1024]{3,2,1,0:T(8,128)(2,1)}, bf16[4,1,72,1024]{3,2,1,0:T(8,128)(2,1)}, u32[]{:S(2)}, u32[]{:S(2)}) collective-permute-start(bf16[4,1,72,1024]{3,2,1,0:T(8,128)(2,1)} %get-tuple-element.60), channel_id=1, source_target_pairs={{0,1},{1,2},{2,3},{3,4},{4,5},{5,6},{6,7},{7,0},{8,9},{9,10},{10,1... | collective-permute-start | bytes 1769480 | tf_op jit(solution)/shard_map/ppermute | solution.py:128
  52.6 29.1 %collective-permute-start.4 = (bf16[4,1,72,1024]{3,2,1,0:T(8,128)(2,1)}, bf16[4,1,72,1024]{3,2,1,0:T(8,128)(2,1)}, u32[]{:S(2)}, u32[]{:S(2)}) collective-permute-start(bf16[4,1,72,1024]{3,2,1,0:T(8,128)(2,1)} %get-tuple-element.61), channel_id=1, source_target_pairs={{1,0},{2,1},{3,2},{4,3},{5,4},{6,5},{7,6},{0,7},{9,8},{10,9},{11,1... | collective-permute-start | bytes 1769480 | tf_op jit(solution)/shard_map/ppermute | solution.py:129
  57.2 4.3 %copy-start.24 = (f32[288,8]{0,1:T(8,128)}, f32[288,8]{0,1:T(8,128)S(1)}, u32[]{:S(2)}) copy-start(f32[288,8]{0,1:T(8,128)S(1)} %multiply_reduce_fusion.1) | copy-start | bytes 27652
  57.3 24.5 %copy-start.7 = (bf16[288,512]{1,0:T(8,128)(2,1)S(1)}, bf16[288,512]{1,0:T(8,128)(2,1)}, u32[]{:S(2)}) copy-start(bf16[288,512]{1,0:T(8,128)(2,1)} %copy-done.6) | copy-start | bytes 884740
  93.0 3.2 %copy-start.15 = (bf16[288,512]{1,0:T(8,128)(2,1)S(1)}, bf16[288,512]{1,0:T(8,128)(2,1)}, u32[]{:S(2)}) copy-start(bf16[288,512]{1,0:T(8,128)(2,1)} %copy-done.14) | copy-start | bytes 884740
  97.2 23.7 %copy-start.18 = (bf16[288,512]{1,0:T(8,128)(2,1)}, bf16[288,512]{1,0:T(8,128)(2,1)S(1)}, u32[]{:S(2)}) copy-start(bf16[288,512]{1,0:T(8,128)(2,1)S(1)} %get-tuple-element.66) | copy-start | bytes 884740
  124.7 18.9 %collective-permute-start.5 = (bf16[4,1,72,1024]{3,2,1,0:T(8,128)(2,1)}, bf16[4,1,72,1024]{3,2,1,0:T(8,128)(2,1)}, u32[]{:S(2)}, u32[]{:S(2)}) collective-permute-start(bf16[4,1,72,1024]{3,2,1,0:T(8,128)(2,1)} %get-tuple-element.57), channel_id=1, source_target_pairs={{7,0},{0,1},{1,2},{2,3},{3,4},{4,5},{5,6},{6,7},{15,8},{8,9},{9,10... | collective-permute-start | bytes 1769480 | tf_op jit(solution)/shard_map/ppermute | solution.py:137
  125.6 28.6 %collective-permute-start.6 = (bf16[4,1,72,1024]{3,2,1,0:T(8,128)(2,1)}, bf16[4,1,72,1024]{3,2,1,0:T(8,128)(2,1)}, u32[]{:S(2)}, u32[]{:S(2)}) collective-permute-start(bf16[4,1,72,1024]{3,2,1,0:T(8,128)(2,1)} %get-tuple-element.56), channel_id=1, source_target_pairs={{1,0},{2,1},{3,2},{4,3},{5,4},{6,5},{7,6},{0,7},{9,8},{10,9},{11,1... | collective-permute-start | bytes 1769480 | tf_op jit(solution)/shard_map/ppermute | solution.py:137
  133.6 5.0 %copy-start.12 = (bf16[512,288]{1,0:T(8,128)(2,1)S(1)}, bf16[512,288]{1,0:T(8,128)(2,1)}, u32[]{:S(2)}) copy-start(bf16[512,288]{1,0:T(8,128)(2,1)} %copy.90) | copy-start | bytes 884740
  155.6 3.8 %copy-start.11 = (f32[288,8,64]{0,2,1:T(8,128)S(1)}, f32[288,8,64]{0,2,1:T(8,128)}, u32[]{:S(2)}) copy-start(f32[288,8,64]{0,2,1:T(8,128)} %copy.83) | copy-start | bytes 1769476
  155.8 6.3 %copy-start.25 = (f32[288,8]{0,1:T(8,128)S(1)}, f32[288,8]{0,1:T(8,128)}, u32[]{:S(2)}) copy-start(f32[288,8]{0,1:T(8,128)} %copy-done.24) | copy-start | bytes 27652
  156.6 6.7 %collective-permute-start.7 = (bf16[1,2,72,1024]{3,2,1,0:T(8,128)(2,1)}, bf16[1,2,72,1024]{3,2,1,0:T(8,128)(2,1)}, u32[]{:S(2)}, u32[]{:S(2)}) collective-permute-start(bf16[1,2,72,1024]{3,2,1,0:T(8,128)(2,1)} %get-tuple-element.59), channel_id=1, source_target_pairs={{0,8},{8,16},{16,24},{24,32},{32,40},{40,48},{48,56},{56,64},{64,7... | collective-permute-start | bytes 884744 | tf_op jit(solution)/shard_map/ppermute | solution.py:143
  159.5 8.4 %collective-permute-start.8 = (bf16[1,2,72,1024]{3,2,1,0:T(8,128)(2,1)}, bf16[1,2,72,1024]{3,2,1,0:T(8,128)(2,1)}, u32[]{:S(2)}, u32[]{:S(2)}) collective-permute-start(bf16[1,2,72,1024]{3,2,1,0:T(8,128)(2,1)} %get-tuple-element.58), channel_id=1, source_target_pairs={{8,0},{16,8},{24,16},{32,24},{40,32},{48,40},{56,48},{64,56},{72,6... | collective-permute-start | bytes 884744 | tf_op jit(solution)/shard_map/ppermute | solution.py:143
  171.6 2.7 %copy-start.1 = (f32[288,512]{1,0:T(8,128)S(1)}, f32[288,512]{1,0:T(8,128)}, u32[]{:S(2)}) copy-start(f32[288,512]{1,0:T(8,128)} %copy-done) | copy-start | bytes 1769476
  171.6 2.7 %copy-start.5 = (bf16[288,1536]{1,0:T(8,128)(2,1)S(1)}, bf16[288,1536]{1,0:T(8,128)(2,1)}, u32[]{:S(2)}) copy-start(bf16[288,1536]{1,0:T(8,128)(2,1)} %copy-done.4) | copy-start | bytes 2654212
  174.2 2.2 copy-start.16
  174.2 2.2 copy-start.22
  176.4 1.1 copy-start.20
  176.4 1.1 copy-start.21
  176.4 1.2 copy-start.8
  177.8 2.7 %collective-permute-start.9 = (bf16[8,32,2048]{2,1,0:T(8,128)(2,1)S(1)}, bf16[8,32,2048]{2,1,0:T(8,128)(2,1)S(1)}, u32[]{:S(2)}, u32[]{:S(2)}) collective-permute-start(bf16[8,32,2048]{2,1,0:T(8,128)(2,1)S(1)} %fusion.13), channel_id=1, source_target_pairs={{0,8},{8,0},{16,24},{24,16},{32,40},{40,32},{48,56},{56,48},{64,72... | collective-permute-start | bytes 3145736 | tf_op jit(solution)/shard_map/ppermute | solution.py:170
  202.5 31.2 %copy-start.17 = (bf16[288,512]{1,0:T(8,128)(2,1)S(1)}, bf16[288,512]{1,0:T(8,128)(2,1)}, u32[]{:S(2)}) copy-start(bf16[288,512]{1,0:T(8,128)(2,1)} %get-tuple-element.67) | copy-start | bytes 884740
  202.7 32.0 %copy-start.3 = (f32[288,512]{1,0:T(8,128)S(1)}, f32[288,512]{1,0:T(8,128)}, u32[]{:S(2)}) copy-start(f32[288,512]{1,0:T(8,128)} %copy-done.2) | copy-start | bytes 1769476
  202.7 32.0 %copy-start.10 = (bf16[512,2048]{1,0:T(8,128)(2,1)S(1)}, bf16[512,2048]{1,0:T(8,128)(2,1)}, u32[]{:S(2)}) copy-start(bf16[512,2048]{1,0:T(8,128)(2,1)} %copy-done.9) | copy-start | bytes 6291460
  228.0 17.8 %all-to-all-start.3 = ((bf16[32,2,2048]{2,1,0:T(2,128)(2,1)}), bf16[32,2,2048]{2,1,0:T(2,128)(2,1)}, u32[]{:S(2)}, u32[]{:S(2)}) async-start(bf16[32,2,2048]{2,1,0:T(2,128)(2,1)} %broadcast_in_dim.8), calls=%async_computation.3 | async-start | bytes 524288 | tf_op jit(solution)/shard_map/all_to_all | solution.py:164

commit v2 on v1

--- a/solution.py
+++ b/solution.py
@@ -118,31 +118,6 @@
     )(tau, query, ext_kv, grad, mask)
 
 
-def with_halo(shard, sides, width, wrap):
-    for axis, dim in sides:
-        peers, length = (lax.axis_size(axis), shard.shape[dim])
-        up = [(i, (i + 1) % peers) for i in range(peers if wrap else peers - 1)]
-        down = [(j, i) for i, j in up]
-        last = lax.slice_in_dim(shard, length - width, length, axis=dim)
-        initial = lax.slice_in_dim(shard, 0, width, axis=dim)
-        before = lax.ppermute(last, axis, up)
-        after = lax.ppermute(initial, axis, down)
-        shard = jnp.concatenate([before, shard, after], axis=dim)
-    return shard
-
-
-def from_behind(block, axis, distance):
-    devices = range(lax.axis_size(axis))
-    route = [((i - distance) % len(devices), i) for i in devices]
-    return lax.ppermute(block, axis, route)
-
-
-def from_behind_2(block, axis, distance):
-    devices = range(lax.axis_size(axis))
-    route = [(i - distance, i) for i in devices if i - distance in devices]
-    return lax.ppermute(block, axis, route)
-
-
 def gather_rows(block, axis):
     peers = lax.axis_size(axis)
     copies = jnp.broadcast_to(block[None], (peers,) + block.shape)
@@ -163,6 +138,43 @@
     copies = jnp.broadcast_to(own[None], (peers,) + own.shape)
     spread = lax.all_to_all(copies, axis, 0, 0, tiled=False)
     return spread.reshape((peers * own.shape[0],) + own.shape[1:])
+
+
+def shift_grid(block, down, right):
+    rows, cols = lax.axis_size("lat"), lax.axis_size("lon")
+    if down == 0:
+        return lax.ppermute(block, "lon", [(j, (j + right) % cols) for j in range(cols)])
+    pairs = [
+        (i * cols + j, (i + down) * cols + (j + right) % cols)
+        for i in range(rows)
+        if 0 <= i + down < rows
+        for j in range(cols)
+    ]
+    if right == 0:
+        return lax.ppermute(block, "lat", [(i, i + down) for i in range(rows) if 0 <= i + down < rows])
+    return lax.ppermute(block, ("lat", "lon"), pairs)
+
+
+def with_ring(units):
+    up = shift_grid(units[1], 1, 0)
+    down = shift_grid(units[0], -1, 0)
+    left = shift_grid(units[:, 1], 0, 1)
+    right = shift_grid(units[:, 0], 0, -1)
+    top = [shift_grid(units[1, 1], 1, 1), up[0], up[1], shift_grid(units[1, 0], 1, -1)]
+    bottom = [shift_grid(units[0, 1], -1, 1), down[0], down[1], shift_grid(units[0, 0], -1, -1)]
+    middle = [[left[r], units[r, 0], units[r, 1], right[r]] for r in range(2)]
+    return jnp.stack([jnp.stack(row) for row in [top] + middle + [bottom]])
+
+
+def fold_ring(ext):
+    def back(block, down, right):
+        return shift_grid(block.astype(jnp.bfloat16), down, right).astype(ext.dtype)
+
+    own = ext[1:3, 1:3]
+    own = own.at[0].add(back(ext[3, 1:3], 1, 0)).at[1].add(back(ext[0, 1:3], -1, 0))
+    own = own.at[:, 0].add(back(ext[1:3, 3], 0, 1)).at[:, 1].add(back(ext[1:3, 0], 0, -1))
+    own = own.at[0, 0].add(back(ext[3, 3], 1, 1)).at[0, 1].add(back(ext[3, 0], 1, -1))
+    return own.at[1, 0].add(back(ext[0, 3], -1, 1)).at[1, 1].add(back(ext[0, 0], -1, -1))
 
 
 def chip_partner(block):
@@ -283,8 +295,7 @@
     kv_source = jnp.concatenate([key_b, proj_b[:, 2 * model_width :]], axis=1).reshape(
         row_units, col_units, query_count, 2 * model_width
     )
-    ext_rows = with_halo(kv_source, (("lat", 0),), 1, False)
-    ext_kv = with_halo(ext_rows, (("lon", 1),), 1, True)
+    ext_kv = with_ring(kv_source)
     level_win = (jnp.arange(query_count) // (half_h * half_w) + WL // 2) // WL
     same_level = level_win[:, None] == level_win[None, :]
     block_row = jnp.arange(row_units + 2)
@@ -303,18 +314,7 @@
     grad_q = unit_back(
         query_f, query_scale, dquery.reshape(tok_count, head_count, head_dim)
     ).reshape(tok_count, model_width)
-    west_rim = ext_grad[:, :1]
-    east_rim = ext_grad[:, col_units + 1 :]
-    center = ext_grad[:, 1 : col_units + 1]
-    from_east = from_behind(west_rim.astype(jnp.bfloat16), "lon", -1).astype(west_rim.dtype)
-    from_west = from_behind(east_rim.astype(jnp.bfloat16), "lon", 1).astype(east_rim.dtype)
-    center = center.at[:, :1].add(from_west).at[:, col_units - 1 :].add(from_east)
-    north_rim = center[:1]
-    south_rim = center[row_units + 1 :]
-    middle = center[1 : row_units + 1]
-    from_south = from_behind_2(north_rim.astype(jnp.bfloat16), "lat", -1).astype(north_rim.dtype)
-    from_north = from_behind_2(south_rim.astype(jnp.bfloat16), "lat", 1).astype(south_rim.dtype)
-    middle = middle.at[:1].add(from_north).at[row_units - 1 :].add(from_south)
+    middle = fold_ring(ext_grad)
     own_grads = middle.reshape(tok_count, 2 * model_width)
     grad_k = unit_back(
         key_f, key_scale, own_grads[:, :model_width].reshape(tok_count, head_count, head_dim)

time: 250 us -> 268 us (1.072)
  starting transfers between devices: 28.7 us -> 72.4 us
  waiting for transfers between devices: 48.8 us -> 17.5 us
  local copies, waits for them, and re-layouts: 33.1 us -> 36.7 us
    ppermute x8 -> x16, starting transfers between devices: 21.1 us -> 64.8 us  [the longest x8 41.4 us: shift_grid(): return lax.ppermute(block, ('lat', 'lon'), pairs)]
    ppermute x8 -> x16, waiting for transfers between devices: 36.6 us -> 6.55 us  [the longest x4 3.61 us: shift_grid(): lax.ppermute(block, 'lon', [(j, (j + right) % cols) for j in range(cols)])]
    another operation x3 -> x6, other arithmetic: 5.02 us -> 9.79 us  [the longest x4 4.96 us: with_ring(): return jnp.stack([jnp.stack(row) for row in [top] + middle + [bottom]])]
    concatenate x2 -> x0, other arithmetic: 4.05 us -> none  [with_halo(): shard = jnp.concatenate([before, shard, after], axis=dim)]
  transfers between devices with their start and end apart: 11 -> 19, of which waited for: 10 -> 5; matrix products, arithmetic and copies ran while one was open for 11% -> 11% of each run, Pallas kernels for 0% -> 0%
where the time goes in v2:
time: 268 us; the launch traced here: 266 us
  starting transfers between devices  72.4 us (27%)
  blocking collectives  69.3 us (26%)
  local copies, waits for them, and re-layouts  36.7 us (14%)
  other arithmetic  30.6 us (11%)
  Pallas kernels  29.9 us (11%)
  waiting for transfers between devices  17.5 us (7%)
  matrix products  8.23 us (3%)
    all_to_all x2, blocking collectives, sum_rows(): spread = lax.all_to_all(chunks, axis, 0, 0, tiled=False)  45.7 us
    ppermute x8, starting transfers between devices, shift_grid(): return lax.ppermute(block, ('lat', 'lon'), pairs)  41.4 us
    all_to_all x1, blocking collectives, gather_rows(): spread = lax.all_to_all(copies, axis, 0, 0, tiled=False)  23.6 us
    pallas_call x1, Pallas kernels, window_bwd(): pl.pallas_call(attn_bwd_kernel, grid=(row_units, col_units), in_specs=[pl...  21.5 us
    ppermute x4, starting transfers between devices, shift_grid(): lax.ppermute(block, 'lat', [(i, i + down) for i in range(rows) if 0 <= i...  13 us
    ppermute x4, starting transfers between devices, shift_grid(): lax.ppermute(block, 'lon', [(j, (j + right) % cols) for j in range(cols)])  10.4 us
    pallas_call x1, Pallas kernels, window_fwd(): pl.pallas_call(attn_fwd_kernel, grid=(row_units, col_units), in_specs=[pl...  8.4 us
    all_to_all x1, waiting for transfers between devices, sum_everywhere(): spread = lax.all_to_all(copies, axis, 0, 0, tiled=False)  8.32 us
  transfers between devices with their start and end apart: 19, of which 5 were waited for; matrix products, arithmetic and copies ran while one was open for 11% of the time, Pallas kernels for 0%

profile of v2, /device:TPU:1, one launch (start us, length us, event | category | flops | bytes accessed | tf_op | source)
XLA Modules:
  0.0 266.0 jit_solution(17043204030180744235)
XLA Ops:
  2.3 23.6 %all_to_all.20 = bf16[8,64,1024]{2,1,0:T(8,128)(2,1)S(1)} all-to-all(bf16[8,64,1024]{2,1,0:T(8,128)(2,1)S(1)} %broadcast_in_dim.7), channel_id=1, replica_groups=mesh['lat'=32,'lon'=8] {'lon'}, dimensions={0} | all-to-all | bytes 2097152 | tf_op jit(solution)/shard_map/all_to_all | solution.py:124
  25.9 1.9 collective-permute-start
  38.3 1.4 copy.89
  41.5 3.1 %collective-permute-start.8 = (bf16[72,1024]{1,0:T(8,128)(2,1)}, bf16[72,1024]{1,0:T(8,128)(2,1)}, u32[]{:S(2)}, u32[]{:S(2)}) collective-permute-start(bf16[72,1024]{1,0:T(8,128)(2,1)} %bitcast.27), channel_id=1, source_target_pairs={{8,7},{9,0},{10,1},{11,2},{12,3},{13,4},{14,5},{15,6},{16,15},{17,... | collective-permute-start | bytes 442376 | tf_op jit(solution)/shard_map/ppermute | solution.py:155
  44.6 4.9 %collective-permute-start.1 = (bf16[72,1024]{1,0:T(8,128)(2,1)}, bf16[72,1024]{1,0:T(8,128)(2,1)}, u32[]{:S(2)}, u32[]{:S(2)}) collective-permute-start(bf16[72,1024]{1,0:T(8,128)(2,1)} %bitcast.10), channel_id=1, source_target_pairs={{0,9},{1,10},{2,11},{3,12},{4,13},{5,14},{6,15},{7,8},{8,17},{9,18... | collective-permute-start | bytes 442376 | tf_op jit(solution)/shard_map/ppermute | solution.py:155
  49.5 1.6 collective-permute-start.4
  51.1 3.6 %collective-permute-start.5 = (bf16[2,72,1024]{2,1,0:T(8,128)(2,1)}, bf16[2,72,1024]{2,1,0:T(8,128)(2,1)}, u32[]{:S(2)}, u32[]{:S(2)}) collective-permute-start(bf16[2,72,1024]{2,1,0:T(8,128)(2,1)} %get-tuple-element.121), channel_id=1, source_target_pairs={{0,7},{1,0},{2,1},{3,2},{4,3},{5,4},{6,5},{7,6},{8,15},{9,8},{10,9... | collective-permute-start | bytes 884744 | tf_op jit(solution)/shard_map/ppermute | solution.py:146
  55.1 2.1 reshape.588
  57.2 2.1 copy.105
  59.4 1.9 multiply_convert_fusion.1.q_ref
  61.2 1.9 fusion.28
  63.1 1.9 collective-permute-start.6
  66.1 1.9 collective-permute-start.7
  69.1 3.6 %collective-permute-start.2 = (bf16[2,72,1024]{2,1,0:T(8,128)(2,1)S(1)}, bf16[2,72,1024]{2,1,0:T(8,128)(2,1)S(1)}, u32[]{:S(2)}, u32[]{:S(2)}) collective-permute-start(bf16[2,72,1024]{2,1,0:T(8,128)(2,1)S(1)} %bitcast.173), channel_id=1, source_target_pairs={{0,8},{8,16},{16,24},{24,32},{32,40},{40,48},{48,56},{56,64},{64,7... | collective-permute-start | bytes 884744 | tf_op jit(solution)/shard_map/ppermute | solution.py:154
  74.5 6.3 %collective-permute-start.3 = (bf16[72,1024]{1,0:T(8,128)(2,1)S(1)}, bf16[72,1024]{1,0:T(8,128)(2,1)S(1)}, u32[]{:S(2)}, u32[]{:S(2)}) collective-permute-start(bf16[72,1024]{1,0:T(8,128)(2,1)S(1)} %bitcast.168), channel_id=1, source_target_pairs={{0,15},{1,8},{2,9},{3,10},{4,11},{5,12},{6,13},{7,14},{8,23},{9,16... | collective-permute-start | bytes 442376 | tf_op jit(solution)/shard_map/ppermute | solution.py:155
  81.9 1.2 maximum_bitcast_fusion.1
  84.1 1.7 pad_maximum_fusion.kv_ref
  85.9 8.4 %shard_map.93 = f32[2,2,72,512]{3,2,1,0:T(8,128)} custom-call(f32[8]{0:T(128)} %tau_ref.3, bf16[2,2,72,512]{3,2,1,0:T(8,128)(2,1)} %multiply_convert_fusion.1.q_ref, bf16[4,4,72,1024]{3,2,1,0:T(8,128)(2,1)} %pad_maximum_fusion.kv_ref, f32[4,72,72]{2,1,0:T(8,128)} %and_convert_fusion.mask_ref), custom_call_target="tpu_custom_call" | custom-call | tf_op jit(solution)/shard_map/pallas_call | solution.py:84
  95.4 1.5 fusion.48
  98.4 2.1 convolution_convert_fusion.3
  100.5 21.5 %shard_map.94 = (f32[2,2,72,512]{3,2,1,0:T(8,128)}, f32[4,4,72,1024]{3,2,1,0:T(8,128)}) custom-call(f32[8]{0:T(128)} %tau_ref.3, bf16[2,2,72,512]{3,2,1,0:T(8,128)(2,1)} %multiply_convert_fusion.1.q_ref, bf16[4,4,72,1024]{3,2,1,0:T(8,128)(2,1)} %pad_maximum_fusion.kv_ref, bf16[2,2,72,512]{3,2,1,0:T(8,128)(2,1)} %bitcast.171, ...), custom_call_target="tpu_custom_call" | custom-call | tf_op jit(solution)/shard_map/pallas_call | solution.py:100
  122.0 2.7 %convert.61 = bf16[4,4,72,1024]{3,2,1,0:T(8,128)(2,1)S(1)} convert(f32[4,4,72,1024]{3,2,1,0:T(8,128)} %get-tuple-element.103) | non-fusion elementwise | flops 1179648 | bytes 7077888 | tf_op jit(solution)/shard_map/convert.31
  127.5 1.2 convolution_convert_fusion.2
  128.7 1.3 reshape.560
  130.0 1.4 copy.93
  131.4 4.5 %collective-permute-start.9 = (bf16[2,72,1024]{2,1,0:T(8,128)(2,1)}, bf16[2,72,1024]{2,1,0:T(8,128)(2,1)}, u32[]{:S(2)}, u32[]{:S(2)}) collective-permute-start(bf16[2,72,1024]{2,1,0:T(8,128)(2,1)} %get-tuple-element.111), channel_id=1, source_target_pairs={{0,8},{8,16},{16,24},{24,32},{32,40},{40,48},{48,56},{56,64},{64,7... | collective-permute-start | bytes 884744 | tf_op jit(solution)/shard_map/ppermute | solution.py:154
  136.0 1.2 multiply_reduce_fusion
  137.2 2.9 %collective-permute-start.10 = (bf16[2,72,1024]{2,1,0:T(8,128)(2,1)}, bf16[2,72,1024]{2,1,0:T(8,128)(2,1)}, u32[]{:S(2)}, u32[]{:S(2)}) collective-permute-start(bf16[2,72,1024]{2,1,0:T(8,128)(2,1)} %get-tuple-element.110), channel_id=1, source_target_pairs={{8,0},{16,8},{24,16},{32,24},{40,32},{48,40},{56,48},{64,56},{72,6... | collective-permute-start | bytes 884744 | tf_op jit(solution)/shard_map/ppermute | solution.py:154
  140.1 1.4 slice.359
  142.6 7.6 %collective-permute-start.16 = (bf16[72,1024]{1,0:T(8,128)(2,1)}, bf16[72,1024]{1,0:T(8,128)(2,1)S(1)}, u32[]{:S(2)}, u32[]{:S(2)}) collective-permute-start(bf16[72,1024]{1,0:T(8,128)(2,1)} %get-tuple-element.104), channel_id=1, source_target_pairs={{8,7},{9,0},{10,1},{11,2},{12,3},{13,4},{14,5},{15,6},{16,15},{17,... | collective-permute-start | bytes 442376 | tf_op jit(solution)/shard_map/ppermute | solution.py:155
  150.2 1.9 collective-permute-start.15
  152.1 8.2 %collective-permute-start.14 = (bf16[72,1024]{1,0:T(8,128)(2,1)}, bf16[72,1024]{1,0:T(8,128)(2,1)S(1)}, u32[]{:S(2)}, u32[]{:S(2)}) collective-permute-start(bf16[72,1024]{1,0:T(8,128)(2,1)} %get-tuple-element.106), channel_id=1, source_target_pairs={{0,15},{1,8},{2,9},{3,10},{4,11},{5,12},{6,13},{7,14},{8,23},{9,16... | collective-permute-start | bytes 442376 | tf_op jit(solution)/shard_map/ppermute | solution.py:155
  160.4 1.2 fusion.22
  161.6 5.1 %collective-permute-start.12 = (bf16[2,72,1024]{2,1,0:T(8,128)(2,1)}, bf16[2,72,1024]{2,1,0:T(8,128)(2,1)S(1)}, u32[]{:S(2)}, u32[]{:S(2)}) collective-permute-start(bf16[2,72,1024]{2,1,0:T(8,128)(2,1)} %get-tuple-element.108), channel_id=1, source_target_pairs={{0,7},{1,0},{2,1},{3,2},{4,3},{5,4},{6,5},{7,6},{8,15},{9,8},{10,9... | collective-permute-start | bytes 884744 | tf_op jit(solution)/shard_map/ppermute | solution.py:146
  167.8 3.6 %collective-permute-done.11 = bf16[2,72,1024]{2,1,0:T(8,128)(2,1)S(1)} collective-permute-done((bf16[2,72,1024]{2,1,0:T(8,128)(2,1)}, bf16[2,72,1024]{2,1,0:T(8,128)(2,1)S(1)}, u32[]{:S(2)}, u32[]{:S(2)}) %collective-permute-start.11) | collective-permute-done | bytes 294944 | tf_op jit(solution)/shard_map/ppermute | solution.py:146
  171.4 7.6 %collective-permute-start.13 = (bf16[72,1024]{1,0:T(8,128)(2,1)S(1)}, bf16[72,1024]{1,0:T(8,128)(2,1)S(1)}, u32[]{:S(2)}, u32[]{:S(2)}) collective-permute-start(bf16[72,1024]{1,0:T(8,128)(2,1)S(1)} %copy-done.14), channel_id=1, source_target_pairs={{0,9},{1,10},{2,11},{3,12},{4,13},{5,14},{6,15},{7,8},{8,17},{9,18... | collective-permute-start | bytes 442376 | tf_op jit(solution)/shard_map/ppermute | solution.py:155
  179.4 2.1 collective-permute-done.13
  181.6 1.2 fusion.36
  184.7 2.2 copy.98
  186.9 1.2 bitcast_reduce_fusion
  189.0 2.2 copy.99
  191.3 2.1 fusion.24
  194.9 2.6 collective-permute-done.17
  197.9 20.5 %all_to_all.21 = bf16[8,32,2048]{2,1,0:T(8,128)(2,1)S(1)} all-to-all(bf16[8,32,2048]{2,1,0:T(8,128)(2,1)S(1)} %fusion.1), channel_id=1, replica_groups=mesh['lat'=32,'lon'=8] {'lon'}, dimensions={0} | all-to-all | bytes 2097152 | tf_op jit(solution)/shard_map/all_to_all | solution.py:131
  219.5 25.1 %all_to_all.22 = bf16[32,2,2048]{2,1,0:T(2,128)(2,1)S(1)} all-to-all(bf16[32,2,2048]{2,1,0:T(2,128)(2,1)} %reshape.573), channel_id=1, replica_groups=mesh['lat'=32,'lon'=8] {'lat'}, dimensions={0} | all-to-all | bytes 524288 | tf_op jit(solution)/shard_map/all_to_all | solution.py:131
  245.7 5.7 %all-to-all-start.3 = ((bf16[32,2,2048]{2,1,0:T(2,128)(2,1)}), bf16[32,2,2048]{2,1,0:T(2,128)(2,1)}, u32[]{:S(2)}, u32[]{:S(2)}) async-start(bf16[32,2,2048]{2,1,0:T(2,128)(2,1)} %broadcast_in_dim.8), calls=%async_computation.3 | async-start | bytes 524288 | tf_op jit(solution)/shard_map/all_to_all | solution.py:139
  252.4 1.8 fusion.8
  255.2 8.3 %all-to-all-done.3 = bf16[32,2,2048]{2,1,0:T(2,128)(2,1)} async-done(((bf16[32,2,2048]{2,1,0:T(2,128)(2,1)}), bf16[32,2,2048]{2,1,0:T(2,128)(2,1)}, u32[]{:S(2)}, u32[]{:S(2)}) %all-to-all-start.3) | async-done | bytes 262176 | tf_op jit(solution)/shard_map/all_to_all | solution.py:139
  (133 shorter events, 39.5 us)
Async XLA Ops:
  1.8 25.9 %copy-start.10 = (bf16[4,6,12,512]{3,0,2,1:T(4,128)(2,1)S(1)}, bf16[4,6,12,512]{3,0,2,1:T(4,128)(2,1)}, u32[]{:S(2)}) copy-start(bf16[4,6,12,512]{3,0,2,1:T(4,128)(2,1)} %param.27) | copy-start | bytes 884740
  1.8 25.9 %copy-start.17 = (f32[512]{0:T(512)S(1)}, f32[512]{0:T(512)}, u32[]{:S(2)}) copy-start(f32[512]{0:T(512)} %param.25) | copy-start | bytes 6148
  25.9 6.6 %collective-permute-start = (bf16[512,1024]{1,0:T(8,128)(2,1)S(1)}, bf16[512,1024]{1,0:T(8,128)(2,1)S(1)}, u32[]{:S(2)}, u32[]{:S(2)}) collective-permute-start(bf16[512,1024]{1,0:T(8,128)(2,1)S(1)} %bitcast.154), channel_id=1, source_target_pairs={{0,8},{8,0},{16,24},{24,16},{32,40},{40,32},{48,56},{56,48},{64,72... | collective-permute-start | bytes 3145736 | tf_op jit(solution)/shard_map/ppermute | solution.py:182
  32.5 1.0 copy-start.7
  33.4 1.4 copy-start.5
  34.8 4.8 %copy-start = (bf16[288,1536]{1,0:T(8,128)(2,1)}, bf16[288,1536]{1,0:T(8,128)(2,1)S(1)}, u32[]{:S(2)}) copy-start(bf16[288,1536]{1,0:T(8,128)(2,1)S(1)} %fusion) | copy-start | bytes 2654212
  35.0 5.6 %copy-start.3 = (bf16[288,512]{1,0:T(8,128)(2,1)}, bf16[288,512]{1,0:T(8,128)(2,1)S(1)}, u32[]{:S(2)}) copy-start(bf16[288,512]{1,0:T(8,128)(2,1)S(1)} %get-tuple-element.114) | copy-start | bytes 884740
  39.8 14.9 %copy-start.4 = (bf16[288,512]{1,0:T(8,128)(2,1)}, bf16[288,512]{1,0:T(8,128)(2,1)S(1)}, u32[]{:S(2)}) copy-start(bf16[288,512]{1,0:T(8,128)(2,1)S(1)} %fusion.15) | copy-start | bytes 884740
  41.5 39.3 %collective-permute-start.8 = (bf16[72,1024]{1,0:T(8,128)(2,1)}, bf16[72,1024]{1,0:T(8,128)(2,1)}, u32[]{:S(2)}, u32[]{:S(2)}) collective-permute-start(bf16[72,1024]{1,0:T(8,128)(2,1)} %bitcast.27), channel_id=1, source_target_pairs={{8,7},{9,0},{10,1},{11,2},{12,3},{13,4},{14,5},{15,6},{16,15},{17,... | collective-permute-start | bytes 442376 | tf_op jit(solution)/shard_map/ppermute | solution.py:155
  44.6 38.5 %collective-permute-start.1 = (bf16[72,1024]{1,0:T(8,128)(2,1)}, bf16[72,1024]{1,0:T(8,128)(2,1)}, u32[]{:S(2)}, u32[]{:S(2)}) collective-permute-start(bf16[72,1024]{1,0:T(8,128)(2,1)} %bitcast.10), channel_id=1, source_target_pairs={{0,9},{1,10},{2,11},{3,12},{4,13},{5,14},{6,15},{7,8},{8,17},{9,18... | collective-permute-start | bytes 442376 | tf_op jit(solution)/shard_map/ppermute | solution.py:155
  49.5 16.6 %collective-permute-start.4 = (bf16[2,72,1024]{2,1,0:T(8,128)(2,1)}, bf16[2,72,1024]{2,1,0:T(8,128)(2,1)}, u32[]{:S(2)}, u32[]{:S(2)}) collective-permute-start(bf16[2,72,1024]{2,1,0:T(8,128)(2,1)} %get-tuple-element.120), channel_id=1, source_target_pairs={{0,1},{1,2},{2,3},{3,4},{4,5},{5,6},{6,7},{7,0},{8,9},{9,10},{10,1... | collective-permute-start | bytes 884744 | tf_op jit(solution)/shard_map/ppermute | solution.py:146
  51.1 18.0 %collective-permute-start.5 = (bf16[2,72,1024]{2,1,0:T(8,128)(2,1)}, bf16[2,72,1024]{2,1,0:T(8,128)(2,1)}, u32[]{:S(2)}, u32[]{:S(2)}) collective-permute-start(bf16[2,72,1024]{2,1,0:T(8,128)(2,1)} %get-tuple-element.121), channel_id=1, source_target_pairs={{0,7},{1,0},{2,1},{3,2},{4,3},{5,4},{6,5},{7,6},{8,15},{9,8},{10,9... | collective-permute-start | bytes 884744 | tf_op jit(solution)/shard_map/ppermute | solution.py:146
  55.0 4.3 %copy-start.15 = (f32[288,8]{0,1:T(8,128)}, f32[288,8]{0,1:T(8,128)S(1)}, u32[]{:S(2)}) copy-start(f32[288,8]{0,1:T(8,128)S(1)} %multiply_reduce_fusion.1) | copy-start | bytes 27652
  63.1 11.4 %collective-permute-start.6 = (bf16[72,1024]{1,0:T(8,128)(2,1)}, bf16[72,1024]{1,0:T(8,128)(2,1)}, u32[]{:S(2)}, u32[]{:S(2)}) collective-permute-start(bf16[72,1024]{1,0:T(8,128)(2,1)} %bitcast.24), channel_id=1, source_target_pairs={{8,1},{9,2},{10,3},{11,4},{12,5},{13,6},{14,7},{15,0},{16,9},{17,1... | collective-permute-start | bytes 442376 | tf_op jit(solution)/shard_map/ppermute | solution.py:155
  66.1 14.7 %collective-permute-start.7 = (bf16[2,72,1024]{2,1,0:T(8,128)(2,1)}, bf16[2,72,1024]{2,1,0:T(8,128)(2,1)S(1)}, u32[]{:S(2)}, u32[]{:S(2)}) collective-permute-start(bf16[2,72,1024]{2,1,0:T(8,128)(2,1)} %bitcast.26), channel_id=1, source_target_pairs={{8,0},{16,8},{24,16},{32,24},{40,32},{48,40},{56,48},{64,56},{72,6... | collective-permute-start | bytes 884744 | tf_op jit(solution)/shard_map/ppermute | solution.py:154
  69.1 14.1 %collective-permute-start.2 = (bf16[2,72,1024]{2,1,0:T(8,128)(2,1)S(1)}, bf16[2,72,1024]{2,1,0:T(8,128)(2,1)S(1)}, u32[]{:S(2)}, u32[]{:S(2)}) collective-permute-start(bf16[2,72,1024]{2,1,0:T(8,128)(2,1)S(1)} %bitcast.173), channel_id=1, source_target_pairs={{0,8},{8,16},{16,24},{24,32},{32,40},{40,48},{48,56},{56,64},{64,7... | collective-permute-start | bytes 884744 | tf_op jit(solution)/shard_map/ppermute | solution.py:154
  74.5 8.6 %collective-permute-start.3 = (bf16[72,1024]{1,0:T(8,128)(2,1)S(1)}, bf16[72,1024]{1,0:T(8,128)(2,1)S(1)}, u32[]{:S(2)}, u32[]{:S(2)}) collective-permute-start(bf16[72,1024]{1,0:T(8,128)(2,1)S(1)} %bitcast.168), channel_id=1, source_target_pairs={{0,15},{1,8},{2,9},{3,10},{4,11},{5,12},{6,13},{7,14},{8,23},{9,16... | collective-permute-start | bytes 442376 | tf_op jit(solution)/shard_map/ppermute | solution.py:155
  94.3 3.2 %copy-start.8 = (bf16[288,512]{1,0:T(8,128)(2,1)S(1)}, bf16[288,512]{1,0:T(8,128)(2,1)}, u32[]{:S(2)}) copy-start(bf16[288,512]{1,0:T(8,128)(2,1)} %reshape_reshape.10) | copy-start | bytes 884740
  94.3 3.2 %copy-start.18 = (f32[288]{0:T(512)S(1)}, f32[288]{0:T(512)}, u32[]{:S(2)}) copy-start(f32[288]{0:T(512)} %div.46) | copy-start | bytes 3460
  130.0 10.1 %copy-start.16 = (f32[288,8]{0,1:T(8,128)S(1)}, f32[288,8]{0,1:T(8,128)}, u32[]{:S(2)}) copy-start(f32[288,8]{0,1:T(8,128)} %copy-done.15) | copy-start | bytes 27652
  131.4 28.8 %collective-permute-start.9 = (bf16[2,72,1024]{2,1,0:T(8,128)(2,1)}, bf16[2,72,1024]{2,1,0:T(8,128)(2,1)}, u32[]{:S(2)}, u32[]{:S(2)}) collective-permute-start(bf16[2,72,1024]{2,1,0:T(8,128)(2,1)} %get-tuple-element.111), channel_id=1, source_target_pairs={{0,8},{8,16},{16,24},{24,32},{32,40},{40,48},{48,56},{56,64},{64,7... | collective-permute-start | bytes 884744 | tf_op jit(solution)/shard_map/ppermute | solution.py:154
  137.2 24.4 %collective-permute-start.10 = (bf16[2,72,1024]{2,1,0:T(8,128)(2,1)}, bf16[2,72,1024]{2,1,0:T(8,128)(2,1)}, u32[]{:S(2)}, u32[]{:S(2)}) collective-permute-start(bf16[2,72,1024]{2,1,0:T(8,128)(2,1)} %get-tuple-element.110), channel_id=1, source_target_pairs={{8,0},{16,8},{24,16},{32,24},{40,32},{48,40},{56,48},{64,56},{72,6... | collective-permute-start | bytes 884744 | tf_op jit(solution)/shard_map/ppermute | solution.py:154
  142.6 28.8 %copy-start.14 = (bf16[72,1024]{1,0:T(8,128)(2,1)S(1)}, bf16[72,1024]{1,0:T(8,128)(2,1)}, u32[]{:S(2)}) copy-start(bf16[72,1024]{1,0:T(8,128)(2,1)} %get-tuple-element.107) | copy-start | bytes 442372
  142.6 40.3 %collective-permute-start.16 = (bf16[72,1024]{1,0:T(8,128)(2,1)}, bf16[72,1024]{1,0:T(8,128)(2,1)S(1)}, u32[]{:S(2)}, u32[]{:S(2)}) collective-permute-start(bf16[72,1024]{1,0:T(8,128)(2,1)} %get-tuple-element.104), channel_id=1, source_target_pairs={{8,7},{9,0},{10,1},{11,2},{12,3},{13,4},{14,5},{15,6},{16,15},{17,... | collective-permute-start | bytes 442376 | tf_op jit(solution)/shard_map/ppermute | solution.py:155
  150.2 32.7 %collective-permute-start.15 = (bf16[72,1024]{1,0:T(8,128)(2,1)}, bf16[72,1024]{1,0:T(8,128)(2,1)S(1)}, u32[]{:S(2)}, u32[]{:S(2)}) collective-permute-start(bf16[72,1024]{1,0:T(8,128)(2,1)} %get-tuple-element.105), channel_id=1, source_target_pairs={{8,1},{9,2},{10,3},{11,4},{12,5},{13,6},{14,7},{15,0},{16,9},{17,1... | collective-permute-start | bytes 442376 | tf_op jit(solution)/shard_map/ppermute | solution.py:155
  152.1 29.5 %collective-permute-start.14 = (bf16[72,1024]{1,0:T(8,128)(2,1)}, bf16[72,1024]{1,0:T(8,128)(2,1)S(1)}, u32[]{:S(2)}, u32[]{:S(2)}) collective-permute-start(bf16[72,1024]{1,0:T(8,128)(2,1)} %get-tuple-element.106), channel_id=1, source_target_pairs={{0,15},{1,8},{2,9},{3,10},{4,11},{5,12},{6,13},{7,14},{8,23},{9,16... | collective-permute-start | bytes 442376 | tf_op jit(solution)/shard_map/ppermute | solution.py:155
  160.3 11.2 %collective-permute-start.11 = (bf16[2,72,1024]{2,1,0:T(8,128)(2,1)}, bf16[2,72,1024]{2,1,0:T(8,128)(2,1)S(1)}, u32[]{:S(2)}, u32[]{:S(2)}) collective-permute-start(bf16[2,72,1024]{2,1,0:T(8,128)(2,1)} %get-tuple-element.109), channel_id=1, source_target_pairs={{0,1},{1,2},{2,3},{3,4},{4,5},{5,6},{6,7},{7,0},{8,9},{9,10},{10,1... | collective-permute-start | bytes 884744 | tf_op jit(solution)/shard_map/ppermute | solution.py:146
  161.6 17.6 %collective-permute-start.12 = (bf16[2,72,1024]{2,1,0:T(8,128)(2,1)}, bf16[2,72,1024]{2,1,0:T(8,128)(2,1)S(1)}, u32[]{:S(2)}, u32[]{:S(2)}) collective-permute-start(bf16[2,72,1024]{2,1,0:T(8,128)(2,1)} %get-tuple-element.108), channel_id=1, source_target_pairs={{0,7},{1,0},{2,1},{3,2},{4,3},{5,4},{6,5},{7,6},{8,15},{9,8},{10,9... | collective-permute-start | bytes 884744 | tf_op jit(solution)/shard_map/ppermute | solution.py:146
  171.4 10.1 %collective-permute-start.13 = (bf16[72,1024]{1,0:T(8,128)(2,1)S(1)}, bf16[72,1024]{1,0:T(8,128)(2,1)S(1)}, u32[]{:S(2)}, u32[]{:S(2)}) collective-permute-start(bf16[72,1024]{1,0:T(8,128)(2,1)S(1)} %copy-done.14), channel_id=1, source_target_pairs={{0,9},{1,10},{2,11},{3,12},{4,13},{5,14},{6,15},{7,8},{8,17},{9,18... | collective-permute-start | bytes 442376 | tf_op jit(solution)/shard_map/ppermute | solution.py:155
  179.3 4.4 %copy-start.1 = (bf16[288,1536]{1,0:T(8,128)(2,1)S(1)}, bf16[288,1536]{1,0:T(8,128)(2,1)}, u32[]{:S(2)}) copy-start(bf16[288,1536]{1,0:T(8,128)(2,1)} %copy-done) | copy-start | bytes 2654212
  191.3 2.1 copy-start.13
  193.4 1.1 copy-start.11
  193.4 1.1 copy-start.12
  193.4 1.2 copy-start.2
  194.8 2.7 %collective-permute-start.17 = (bf16[8,32,2048]{2,1,0:T(8,128)(2,1)S(1)}, bf16[8,32,2048]{2,1,0:T(8,128)(2,1)S(1)}, u32[]{:S(2)}, u32[]{:S(2)}) collective-permute-start(bf16[8,32,2048]{2,1,0:T(8,128)(2,1)S(1)} %fusion.12), channel_id=1, source_target_pairs={{0,8},{8,0},{16,24},{24,16},{32,40},{40,32},{48,56},{56,48},{64,72... | collective-permute-start | bytes 3145736 | tf_op jit(solution)/shard_map/ppermute | solution.py:182
  218.4 33.0 %copy-start.9 = (bf16[288,512]{1,0:T(8,128)(2,1)S(1)}, bf16[288,512]{1,0:T(8,128)(2,1)}, u32[]{:S(2)}) copy-start(bf16[288,512]{1,0:T(8,128)(2,1)} %get-tuple-element.117) | copy-start | bytes 884740
  218.6 33.8 %copy-start.6 = (bf16[512,2048]{1,0:T(8,128)(2,1)S(1)}, bf16[512,2048]{1,0:T(8,128)(2,1)}, u32[]{:S(2)}) copy-start(bf16[512,2048]{1,0:T(8,128)(2,1)} %copy-done.5) | copy-start | bytes 6291460
  245.7 17.8 %all-to-all-start.3 = ((bf16[32,2,2048]{2,1,0:T(2,128)(2,1)}), bf16[32,2,2048]{2,1,0:T(2,128)(2,1)}, u32[]{:S(2)}, u32[]{:S(2)}) async-start(bf16[32,2,2048]{2,1,0:T(2,128)(2,1)} %broadcast_in_dim.8), calls=%async_computation.3 | async-start | bytes 524288 | tf_op jit(solution)/shard_map/all_to_all | solution.py:139

commit v3 on v1

--- a/solution.py
+++ b/solution.py
@@ -26,53 +26,49 @@
     return lax.dot_general(a, b, (((0,), (0,)), ((), ())), preferred_element_type=jnp.float32)
 
 
-def _block_probs(tau_ref, head, query, kv_ref, mask_ref):
-    lanes = pl.ds(head * HD_K, HD_K)
-    weights = []
-    for r in range(2):
-        for c in range(2):
-            scores = _nt(query, kv_ref[r, c, :, lanes]) * tau_ref[head]
-            weights.append(jnp.exp(scores) * mask_ref[r])
-    total = sum(jnp.sum(w, axis=-1, keepdims=True) for w in weights)
-    return [w / total for w in weights]
+def _window_probs(tau_ref, head, query, keys, mask):
+    scores = _nt(query, keys) * tau_ref[head]
+    weights = jnp.exp(scores) * mask
+    return weights / jnp.sum(weights, axis=-1, keepdims=True)
+
+
+def _head_keys(kv_ref, lanes):
+    rows, cols, block = kv_ref.shape[:3]
+    return kv_ref[:, :, :, lanes].reshape(rows * cols * block, HD_K)
 
 
 def attn_fwd_kernel(tau_ref, q_ref, kv_ref, mask_ref, out_ref):
     width = q_ref.shape[3]
+    mask = mask_ref[0]
     for head in range(HEADS_K):
         lanes = pl.ds(head * HD_K, HD_K)
         value_lanes = pl.ds(width + head * HD_K, HD_K)
-        probs = _block_probs(tau_ref, head, q_ref[0, 0, :, lanes], kv_ref, mask_ref)
-        mixed = None
-        for n, p in enumerate(probs):
-            part = jnp.dot(
-                p.astype(jnp.bfloat16),
-                kv_ref[n // 2, n % 2, :, value_lanes],
-                preferred_element_type=jnp.float32,
-            )
-            mixed = part if mixed is None else mixed + part
-        out_ref[0, 0, :, lanes] = mixed
+        probs = _window_probs(tau_ref, head, q_ref[0, 0, :, lanes], _head_keys(kv_ref, lanes), mask)
+        out_ref[0, 0, :, lanes] = jnp.dot(
+            probs.astype(jnp.bfloat16),
+            _head_keys(kv_ref, value_lanes),
+            preferred_element_type=jnp.float32,
+        )
 
 
 def attn_bwd_kernel(tau_ref, q_ref, kv_ref, g_ref, mask_ref, dq_ref, dkv_ref):
     width = q_ref.shape[3]
+    mask = mask_ref[0]
     for head in range(HEADS_K):
         lanes = pl.ds(head * HD_K, HD_K)
         value_lanes = pl.ds(width + head * HD_K, HD_K)
         query = q_ref[0, 0, :, lanes]
         grad = g_ref[0, 0, :, lanes]
-        probs = _block_probs(tau_ref, head, query, kv_ref, mask_ref)
-        dprobs = [_nt(grad, kv_ref[n // 2, n % 2, :, value_lanes]) for n in range(4)]
-        total = sum(jnp.sum(p * d, axis=-1, keepdims=True) for p, d in zip(probs, dprobs))
-        dquery = None
-        for n in range(4):
-            r, c = n // 2, n % 2
-            dscore = (tau_ref[head] * (probs[n] * (dprobs[n] - total))).astype(jnp.bfloat16)
-            part = jnp.dot(dscore, kv_ref[r, c, :, lanes], preferred_element_type=jnp.float32)
-            dquery = part if dquery is None else dquery + part
-            dkv_ref[r, c, :, lanes] = _tn(dscore, query)
-            dkv_ref[r, c, :, value_lanes] = _tn(probs[n].astype(jnp.bfloat16), grad)
-        dq_ref[0, 0, :, lanes] = dquery
+        keys = _head_keys(kv_ref, lanes)
+        probs = _window_probs(tau_ref, head, query, keys, mask)
+        dprob = _nt(grad, _head_keys(kv_ref, value_lanes))
+        total = jnp.sum(probs * dprob, axis=-1, keepdims=True)
+        dscore = (tau_ref[head] * (probs * (dprob - total))).astype(jnp.bfloat16)
+        dq_ref[0, 0, :, lanes] = jnp.dot(dscore, keys, preferred_element_type=jnp.float32)
+        dkv_ref[:, :, :, lanes] = _tn(dscore, query).reshape(dkv_ref.shape[:3] + (HD_K,))
+        dkv_ref[:, :, :, value_lanes] = _tn(probs.astype(jnp.bfloat16), grad).reshape(
+            dkv_ref.shape[:3] + (HD_K,)
+        )
 
 
 def _window_of(i, j):
@@ -81,14 +77,15 @@
 
 def window_fwd(tau, query, ext_kv, mask):
     row_units, col_units, queries, width = query.shape
+    block = ext_kv.shape[2]
     return pl.pallas_call(
         attn_fwd_kernel,
         grid=(row_units, col_units),
         in_specs=[
             pl.BlockSpec(memory_space=pltpu.SMEM),
             pl.BlockSpec((1, 1, queries, width), lambda i, j: (i, j, 0, 0)),
-            pl.BlockSpec((2, 2, queries, 2 * width), _window_of),
-            pl.BlockSpec((2, queries, queries), lambda i, j: ((i + 1) // 2, 0, 0)),
+            pl.BlockSpec((2, 2, block, 2 * width), _window_of),
+            pl.BlockSpec((1, queries, mask.shape[2]), lambda i, j: ((i + 1) // 2, 0, 0)),
         ],
         out_specs=pl.BlockSpec((1, 1, queries, width), lambda i, j: (i, j, 0, 0)),
         out_shape=jax.ShapeDtypeStruct(query.shape, jnp.float32),
@@ -97,19 +94,20 @@
 
 def window_bwd(tau, query, ext_kv, grad, mask):
     row_units, col_units, queries, width = query.shape
+    block = ext_kv.shape[2]
     return pl.pallas_call(
         attn_bwd_kernel,
         grid=(row_units, col_units),
         in_specs=[
             pl.BlockSpec(memory_space=pltpu.SMEM),
             pl.BlockSpec((1, 1, queries, width), lambda i, j: (i, j, 0, 0)),
-            pl.BlockSpec((2, 2, queries, 2 * width), _window_of),
+            pl.BlockSpec((2, 2, block, 2 * width), _window_of),
             pl.BlockSpec((1, 1, queries, width), lambda i, j: (i, j, 0, 0)),
-            pl.BlockSpec((2, queries, queries), lambda i, j: ((i + 1) // 2, 0, 0)),
+            pl.BlockSpec((1, queries, mask.shape[2]), lambda i, j: ((i + 1) // 2, 0, 0)),
         ],
         out_specs=[
             pl.BlockSpec((1, 1, queries, width), lambda i, j: (i, j, 0, 0)),
-            pl.BlockSpec((2, 2, queries, 2 * width), _window_of),
+            pl.BlockSpec((2, 2, block, 2 * width), _window_of),
         ],
         out_shape=[
             jax.ShapeDtypeStruct(query.shape, jnp.float32),
@@ -285,12 +283,20 @@
     )
     ext_rows = with_halo(kv_source, (("lat", 0),), 1, False)
     ext_kv = with_halo(ext_rows, (("lon", 1),), 1, True)
-    level_win = (jnp.arange(query_count) // (half_h * half_w) + WL // 2) // WL
-    same_level = level_win[:, None] == level_win[None, :]
+    block = 16 * pl.cdiv(query_count, 16)
+    ext_kv = jnp.pad(ext_kv, ((0, 0), (0, 0), (0, block - query_count), (0, 0)))
+    level_win = (jnp.arange(block) // (half_h * half_w) + WL // 2) // WL
+    same_level = (level_win[:query_count, None] == level_win[None, :]) & (
+        jnp.arange(block) < query_count
+    )
     block_row = jnp.arange(row_units + 2)
     first_row = lax.axis_index("lat") * lat_rows - half_h + half_h * block_row
     inside = (first_row >= 0) & (first_row < lat_rows * lax.axis_size("lat"))
-    allowed = (same_level[None, :, :] & inside[:, None, None]).astype(jnp.float32)
+    allowed = same_level[None, :, :] & inside[:, None, None]
+    allowed = allowed.reshape(-1, 2, 1, query_count, block)
+    allowed = jnp.broadcast_to(allowed, allowed.shape[:2] + (2, query_count, block))
+    allowed = allowed.transpose(0, 3, 1, 2, 4).reshape(-1, query_count, 4 * block)
+    allowed = allowed.astype(jnp.float32)
     mixed = window_fwd(tau, query_u, ext_kv, allowed)
     attended = mixed.astype(jnp.bfloat16).reshape(tok_count, model_width)
     y_rows = jnp.dot(attended, w_out_all, preferred_element_type=jnp.float32)
@@ -300,6 +306,7 @@
     grad_att = jnp.dot(grad_y, w_out_all.T, preferred_element_type=jnp.float32)
     grad_u = grad_att.astype(jnp.bfloat16).reshape(row_units, col_units, query_count, model_width)
     dquery, ext_grad = window_bwd(tau, query_u, ext_kv, grad_u, allowed)
+    ext_grad = ext_grad[:, :, :query_count]
     grad_q = unit_back(
         query_f, query_scale, dquery.reshape(tok_count, head_count, head_dim)
     ).reshape(tok_count, model_width)

time: 250 us -> 244 us (0.976)
    pallas_call x1, Pallas kernels: 21.5 us -> 17.8 us  [window_bwd(): pl.pallas_call(attn_bwd_kernel, grid=(row_units, col_units), in_specs=[pl...]
    pallas_call x1, Pallas kernels: 8.4 us -> 11.9 us  [window_fwd(): pl.pallas_call(attn_fwd_kernel, grid=(row_units, col_units), in_specs=[pl...]
  transfers between devices with their start and end apart: 11 -> 11, of which waited for: 10 -> 9; matrix products, arithmetic and copies ran while one was open for 11% -> 12% of each run, Pallas kernels for 0% -> 0%
where the time goes in v3:
time: 244 us; the launch traced here: 242 us
  blocking collectives  68.1 us (28%)
  waiting for transfers between devices  46.8 us (19%)
  local copies, waits for them, and re-layouts  32.2 us (13%)
  Pallas kernels  29.7 us (12%)
  starting transfers between devices  28.8 us (12%)
  other arithmetic  26 us (11%)
  matrix products  9.35 us (4%)
    all_to_all x2, blocking collectives, sum_rows(): spread = lax.all_to_all(chunks, axis, 0, 0, tiled=False)  44.5 us
    all_to_all x1, blocking collectives, gather_rows(): spread = lax.all_to_all(copies, axis, 0, 0, tiled=False)  23.6 us
    pallas_call x1, Pallas kernels, window_bwd(): pl.pallas_call(attn_bwd_kernel, grid=(row_units, col_units), in_specs=[pl...  17.8 us
    pallas_call x1, Pallas kernels, window_fwd(): pl.pallas_call(attn_fwd_kernel, grid=(row_units, col_units), in_specs=[pl...  11.9 us
    ppermute x2, waiting for transfers between devices, with_halo(): after = lax.ppermute(initial, axis, down)  11.9 us
    ppermute x2, waiting for transfers between devices, from_behind(): return lax.ppermute(block, axis, route)  11.2 us
    ppermute x2, waiting for transfers between devices, with_halo(): before = lax.ppermute(last, axis, up)  9.17 us
    all_to_all x1, waiting for transfers between devices, sum_everywhere(): spread = lax.all_to_all(copies, axis, 0, 0, tiled=False)  8.32 us
  transfers between devices with their start and end apart: 11, of which 9 were waited for; matrix products, arithmetic and copies ran while one was open for 12% of the time, Pallas kernels for 0%

profile of v3, /device:TPU:1, one launch (start us, length us, event | category | flops | bytes accessed | tf_op | source)
XLA Modules:
  0.0 242.4 jit_solution(15554165027846228027)
XLA Ops:
  2.3 23.6 %all_to_all.20 = bf16[8,64,1024]{2,1,0:T(8,128)(2,1)S(1)} all-to-all(bf16[8,64,1024]{2,1,0:T(8,128)(2,1)S(1)} %broadcast_in_dim.9), channel_id=1, replica_groups=mesh['lat'=32,'lon'=8] {'lon'}, dimensions={0} | all-to-all | bytes 2097152 | tf_op jit(solution)/shard_map/all_to_all | solution.py:147
  25.9 1.9 collective-permute-start
  34.2 2.3 collective-permute-start.2
  36.4 3.4 %collective-permute-start.1 = (bf16[1,2,72,1024]{3,2,1,0:T(8,128)(2,1)}, bf16[1,2,72,1024]{3,2,1,0:T(8,128)(2,1)}, u32[]{:S(2)}, u32[]{:S(2)}) collective-permute-start(bf16[1,2,72,1024]{3,2,1,0:T(8,128)(2,1)} %bitcast.8), channel_id=1, source_target_pairs={{0,8},{8,16},{16,24},{24,32},{32,40},{40,48},{48,56},{56,64},{64,7... | collective-permute-start | bytes 884744 | tf_op jit(solution)/shard_map/ppermute | solution.py:126
  39.9 1.1 copy.99
  42.8 1.1 collective-permute-done.1
  43.9 1.3 pad_maximum_fusion
  45.1 1.1 fusion.45
  46.8 4.5 %collective-permute-start.4 = (bf16[4,1,72,1024]{3,2,1,0:T(8,128)(2,1)}, bf16[4,1,72,1024]{3,2,1,0:T(8,128)(2,1)}, u32[]{:S(2)}, u32[]{:S(2)}) collective-permute-start(bf16[4,1,72,1024]{3,2,1,0:T(8,128)(2,1)} %get-tuple-element.61), channel_id=1, source_target_pairs={{1,0},{2,1},{3,2},{4,3},{5,4},{6,5},{7,6},{0,7},{9,8},{10,9},{11,1... | collective-permute-start | bytes 1769480 | tf_op jit(solution)/shard_map/ppermute | solution.py:127
  51.5 2.1 reshape.389
  53.6 2.1 copy.93
  55.7 1.9 multiply_convert_fusion.1.q_ref
  57.6 8.1 %collective-permute-done.3 = bf16[4,1,72,1024]{3,2,1,0:T(8,128)(2,1)} collective-permute-done((bf16[4,1,72,1024]{3,2,1,0:T(8,128)(2,1)}, bf16[4,1,72,1024]{3,2,1,0:T(8,128)(2,1)}, u32[]{:S(2)}, u32[]{:S(2)}) %collective-permute-start.3) | collective-permute-done | bytes 589856 | tf_op jit(solution)/shard_map/ppermute | solution.py:126
  65.7 11.9 %collective-permute-done.4 = bf16[4,1,72,1024]{3,2,1,0:T(8,128)(2,1)} collective-permute-done((bf16[4,1,72,1024]{3,2,1,0:T(8,128)(2,1)}, bf16[4,1,72,1024]{3,2,1,0:T(8,128)(2,1)}, u32[]{:S(2)}, u32[]{:S(2)}) %collective-permute-start.4) | collective-permute-done | bytes 589856 | tf_op jit(solution)/shard_map/ppermute | solution.py:127
  77.6 2.9 %fusion.7.kv_ref = bf16[4,4,80,1024]{3,2,1,0:T(8,128)(2,1)} fusion(bf16[4,1,72,1024]{3,2,1,0:T(8,128)(2,1)} %collective-permute-done.4, bf16[4,1,72,1024]{3,2,1,0:T(8,128)(2,1)} %collective-permute-done.3, bf16[1,2,72,1024]{3,2,1,0:T(8,128)(2,1)} %collective-permute-done.2, bf16[1,2,72,1024]{3,2,1,0:T(8,128)(2,1)} %collective-permute-done.1, ...), kind=kLoop, calls=%fused_computation.12 | loop fusion | flops 24903680 | bytes 4980736 | tf_op jit(solution)/shard_map/concatenate | solution.py:128
  80.5 11.9 %shard_map.93 = f32[2,2,72,512]{3,2,1,0:T(8,128)} custom-call(f32[8]{0:T(128)} %tau_ref.3, bf16[2,2,72,512]{3,2,1,0:T(8,128)(2,1)} %multiply_convert_fusion.1.q_ref, bf16[4,4,80,1024]{3,2,1,0:T(8,128)(2,1)} %fusion.7.kv_ref, f32[2,72,320]{2,1,0:T(8,128)} %convert_element_type.114.mask_ref), custom_call_target="tpu_custom_call" | custom-call | tf_op jit(solution)/shard_map/pallas_call | solution.py:81
  92.4 1.1 convert_element_type.115
  93.5 1.5 fusion.47
  96.6 2.2 convolution_convert_fusion.3
  98.8 17.8 %shard_map.94 = (f32[2,2,72,512]{3,2,1,0:T(8,128)}, f32[4,4,80,1024]{3,2,1,0:T(8,128)}) custom-call(f32[8]{0:T(128)} %tau_ref.3, bf16[2,2,72,512]{3,2,1,0:T(8,128)(2,1)} %multiply_convert_fusion.1.q_ref, bf16[4,4,80,1024]{3,2,1,0:T(8,128)(2,1)} %fusion.7.kv_ref, bf16[2,2,72,512]{3,2,1,0:T(8,128)(2,1)} %bitcast.102, f32[2,72,320]{2,1,0:T(8,128)} %convert_element_type.114.mask_ref), custom_call_target="tpu_custom_call" | custom-call | tf_op jit(solution)/shard_map/pallas_call | solution.py:98
  116.6 2.9 %convert.35 = bf16[4,4,80,1024]{3,2,1,0:T(8,128)(2,1)S(1)} convert(f32[4,4,80,1024]{3,2,1,0:T(8,128)} %get-tuple-element.55) | non-fusion elementwise | flops 1310720 | bytes 7864320 | tf_op jit(solution)/shard_map/convert.19
  119.5 1.2 fusion.43
  121.6 4.1 %collective-permute-start.6 = (bf16[4,1,72,1024]{3,2,1,0:T(8,128)(2,1)}, bf16[4,1,72,1024]{3,2,1,0:T(8,128)(2,1)}, u32[]{:S(2)}, u32[]{:S(2)}) collective-permute-start(bf16[4,1,72,1024]{3,2,1,0:T(8,128)(2,1)} %get-tuple-element.56), channel_id=1, source_target_pairs={{1,0},{2,1},{3,2},{4,3},{5,4},{6,5},{7,6},{0,7},{9,8},{10,9},{11,1... | collective-permute-start | bytes 1769480 | tf_op jit(solution)/shard_map/ppermute | solution.py:135
  125.7 1.1 copy.85
  126.8 1.8 slice.205
  129.5 2.4 reshape.379
  131.9 2.6 %copy.83 = f32[288,8,64]{0,2,1:T(8,128)} copy(f32[288,8,64]{2,1,0:T(8,128)} %reshape.379) | data formatting | bytes 1179648 | tf_op jit(solution)/shard_map/reshape | solution.py:311
  134.6 2.2 convolution_convert_fusion.2
  136.8 2.3 collective-permute-done.5
  139.1 1.6 add_dynamic-update-slice_fusion
  140.7 8.9 %collective-permute-done.6 = bf16[4,1,72,1024]{3,2,1,0:T(8,128)(2,1)} collective-permute-done((bf16[4,1,72,1024]{3,2,1,0:T(8,128)(2,1)}, bf16[4,1,72,1024]{3,2,1,0:T(8,128)(2,1)}, u32[]{:S(2)}, u32[]{:S(2)}) %collective-permute-start.6) | collective-permute-done | bytes 589856 | tf_op jit(solution)/shard_map/ppermute | solution.py:135
  149.6 1.4 fusion.22
  152.0 1.9 collective-permute-start.7
  154.1 3.4 %collective-permute-start.8 = (bf16[1,2,72,1024]{3,2,1,0:T(8,128)(2,1)}, bf16[1,2,72,1024]{3,2,1,0:T(8,128)(2,1)}, u32[]{:S(2)}, u32[]{:S(2)}) collective-permute-start(bf16[1,2,72,1024]{3,2,1,0:T(8,128)(2,1)} %get-tuple-element.58), channel_id=1, source_target_pairs={{8,0},{16,8},{24,16},{32,24},{40,32},{48,40},{56,48},{64,56},{72,6... | collective-permute-start | bytes 884744 | tf_op jit(solution)/shard_map/ppermute | solution.py:141
  157.6 1.1 copy.84
  158.8 1.0 fusion.32
  159.9 2.6 %collective-permute-done.8 = bf16[1,2,72,1024]{3,2,1,0:T(8,128)(2,1)} collective-permute-done((bf16[1,2,72,1024]{3,2,1,0:T(8,128)(2,1)}, bf16[1,2,72,1024]{3,2,1,0:T(8,128)(2,1)}, u32[]{:S(2)}, u32[]{:S(2)}) %collective-permute-start.8) | collective-permute-done | bytes 294944 | tf_op jit(solution)/shard_map/ppermute | solution.py:141
  162.5 1.1 fusion.31
  164.3 1.9 convert_multiply_fusion.1
  166.2 1.4 copy.86
  167.8 1.1 copy.87
  168.9 2.1 fusion.34
  172.5 2.6 %collective-permute-done.9 = bf16[8,32,2048]{2,1,0:T(8,128)(2,1)S(1)} collective-permute-done((bf16[8,32,2048]{2,1,0:T(8,128)(2,1)S(1)}, bf16[8,32,2048]{2,1,0:T(8,128)(2,1)S(1)}, u32[]{:S(2)}, u32[]{:S(2)}) %collective-permute-start.9) | collective-permute-done | bytes 1048608 | tf_op jit(solution)/shard_map/ppermute | solution.py:168
  175.5 22.5 %all_to_all.21 = bf16[8,32,2048]{2,1,0:T(8,128)(2,1)S(1)} all-to-all(bf16[8,32,2048]{2,1,0:T(8,128)(2,1)S(1)} %fusion.12), channel_id=1, replica_groups=mesh['lat'=32,'lon'=8] {'lon'}, dimensions={0} | all-to-all | bytes 2097152 | tf_op jit(solution)/shard_map/all_to_all | solution.py:154
  199.2 22.0 %all_to_all.22 = bf16[32,2,2048]{2,1,0:T(2,128)(2,1)S(1)} all-to-all(bf16[32,2,2048]{2,1,0:T(2,128)(2,1)} %reshape.382), channel_id=1, replica_groups=mesh['lat'=32,'lon'=8] {'lat'}, dimensions={0} | all-to-all | bytes 524288 | tf_op jit(solution)/shard_map/all_to_all | solution.py:154
  222.2 5.7 %all-to-all-start.3 = ((bf16[32,2,2048]{2,1,0:T(2,128)(2,1)}), bf16[32,2,2048]{2,1,0:T(2,128)(2,1)}, u32[]{:S(2)}, u32[]{:S(2)}) async-start(bf16[32,2,2048]{2,1,0:T(2,128)(2,1)} %broadcast_in_dim.11), calls=%async_computation.3 | async-start | bytes 524288 | tf_op jit(solution)/shard_map/all_to_all | solution.py:162
  228.9 1.8 fusion.19
  231.6 8.3 %all-to-all-done.3 = bf16[32,2,2048]{2,1,0:T(2,128)(2,1)} async-done(((bf16[32,2,2048]{2,1,0:T(2,128)(2,1)}), bf16[32,2,2048]{2,1,0:T(2,128)(2,1)}, u32[]{:S(2)}, u32[]{:S(2)}) %all-to-all-start.3) | async-done | bytes 262176 | tf_op jit(solution)/shard_map/all_to_all | solution.py:162
  (126 shorter events, 24.3 us)
Async XLA Ops:
  1.8 25.9 %copy-start.23 = (bf16[4,6,12,512]{3,0,2,1:T(4,128)(2,1)S(1)}, bf16[4,6,12,512]{3,0,2,1:T(4,128)(2,1)}, u32[]{:S(2)}) copy-start(bf16[4,6,12,512]{3,0,2,1:T(4,128)(2,1)} %param.14) | copy-start | bytes 884740
  2.2 25.8 %copy-start.18 = (bf16[4,6,12,512]{3,0,2,1:T(4,128)(2,1)S(1)}, bf16[4,6,12,512]{3,0,2,1:T(4,128)(2,1)}, u32[]{:S(2)}) copy-start(bf16[4,6,12,512]{3,0,2,1:T(4,128)(2,1)} %param.19) | copy-start | bytes 884740
  2.2 25.8 %copy-start.26 = (f32[512]{0:T(512)S(1)}, f32[512]{0:T(512)}, u32[]{:S(2)}) copy-start(f32[512]{0:T(512)} %param.17) | copy-start | bytes 6148
  25.9 4.2 %collective-permute-start = (bf16[512,1024]{1,0:T(8,128)(2,1)S(1)}, bf16[512,1024]{1,0:T(8,128)(2,1)S(1)}, u32[]{:S(2)}, u32[]{:S(2)}) collective-permute-start(bf16[512,1024]{1,0:T(8,128)(2,1)S(1)} %bitcast.87), channel_id=1, source_target_pairs={{0,8},{8,0},{16,24},{24,16},{32,40},{40,32},{48,56},{56,48},{64,72... | collective-permute-start | bytes 3145736 | tf_op jit(solution)/shard_map/ppermute | solution.py:168
  27.9 2.9 %copy-start.13 = (bf16[288,512]{1,0:T(8,128)(2,1)}, bf16[288,512]{1,0:T(8,128)(2,1)S(1)}, u32[]{:S(2)}) copy-start(bf16[288,512]{1,0:T(8,128)(2,1)S(1)} %reshape_reshape.10) | copy-start | bytes 884740
  30.8 1.4 copy-start.9
  32.2 0.9 copy-start.4
  33.2 9.2 %copy-start = (f32[288,512]{1,0:T(8,128)}, f32[288,512]{1,0:T(8,128)S(1)}, u32[]{:S(2)}) copy-start(f32[288,512]{1,0:T(8,128)S(1)} %copy.79) | copy-start | bytes 1769476
  33.2 8.1 %copy-start.19 = (f32[2,2,72,80]{3,1,2,0:T(2,128)S(1)}, f32[2,2,72,80]{3,1,2,0:T(2,128)}, u32[]{:S(2)}) copy-start(f32[2,2,72,80]{3,1,2,0:T(2,128)} %and_convert_fusion) | copy-start | bytes 276484
  33.3 9.2 %copy-start.6 = (bf16[288,512]{1,0:T(8,128)(2,1)}, bf16[288,512]{1,0:T(8,128)(2,1)S(1)}, u32[]{:S(2)}) copy-start(bf16[288,512]{1,0:T(8,128)(2,1)S(1)} %fusion.27) | copy-start | bytes 884740
  34.2 8.6 %collective-permute-start.2 = (bf16[1,2,72,1024]{3,2,1,0:T(8,128)(2,1)}, bf16[1,2,72,1024]{3,2,1,0:T(8,128)(2,1)}, u32[]{:S(2)}, u32[]{:S(2)}) collective-permute-start(bf16[1,2,72,1024]{3,2,1,0:T(8,128)(2,1)} %bitcast.11), channel_id=1, source_target_pairs={{8,0},{16,8},{24,16},{32,24},{40,32},{48,40},{56,48},{64,56},{72,6... | collective-permute-start | bytes 884744 | tf_op jit(solution)/shard_map/ppermute | solution.py:127
  36.4 7.4 %collective-permute-start.1 = (bf16[1,2,72,1024]{3,2,1,0:T(8,128)(2,1)}, bf16[1,2,72,1024]{3,2,1,0:T(8,128)(2,1)}, u32[]{:S(2)}, u32[]{:S(2)}) collective-permute-start(bf16[1,2,72,1024]{3,2,1,0:T(8,128)(2,1)} %bitcast.8), channel_id=1, source_target_pairs={{0,8},{8,16},{16,24},{24,32},{32,40},{40,48},{48,56},{56,64},{64,7... | collective-permute-start | bytes 884744 | tf_op jit(solution)/shard_map/ppermute | solution.py:126
  42.5 53.1 %copy-start.2 = (f32[288,512]{1,0:T(8,128)}, f32[288,512]{1,0:T(8,128)S(1)}, u32[]{:S(2)}) copy-start(f32[288,512]{1,0:T(8,128)S(1)} %reshape.383) | copy-start | bytes 1769476
  46.3 19.4 %collective-permute-start.3 = (bf16[4,1,72,1024]{3,2,1,0:T(8,128)(2,1)}, bf16[4,1,72,1024]{3,2,1,0:T(8,128)(2,1)}, u32[]{:S(2)}, u32[]{:S(2)}) collective-permute-start(bf16[4,1,72,1024]{3,2,1,0:T(8,128)(2,1)} %get-tuple-element.60), channel_id=1, source_target_pairs={{0,1},{1,2},{2,3},{3,4},{4,5},{5,6},{6,7},{7,0},{8,9},{9,10},{10,1... | collective-permute-start | bytes 1769480 | tf_op jit(solution)/shard_map/ppermute | solution.py:126
  46.8 30.8 %collective-permute-start.4 = (bf16[4,1,72,1024]{3,2,1,0:T(8,128)(2,1)}, bf16[4,1,72,1024]{3,2,1,0:T(8,128)(2,1)}, u32[]{:S(2)}, u32[]{:S(2)}) collective-permute-start(bf16[4,1,72,1024]{3,2,1,0:T(8,128)(2,1)} %get-tuple-element.61), channel_id=1, source_target_pairs={{1,0},{2,1},{3,2},{4,3},{5,4},{6,5},{7,6},{0,7},{9,8},{10,9},{11,1... | collective-permute-start | bytes 1769480 | tf_op jit(solution)/shard_map/ppermute | solution.py:127
  51.4 4.3 %copy-start.24 = (f32[288,8]{0,1:T(8,128)}, f32[288,8]{0,1:T(8,128)S(1)}, u32[]{:S(2)}) copy-start(f32[288,8]{0,1:T(8,128)S(1)} %multiply_reduce_fusion.1) | copy-start | bytes 27652
  51.5 26.1 %copy-start.7 = (bf16[288,512]{1,0:T(8,128)(2,1)S(1)}, bf16[288,512]{1,0:T(8,128)(2,1)}, u32[]{:S(2)}) copy-start(bf16[288,512]{1,0:T(8,128)(2,1)} %copy-done.6) | copy-start | bytes 884740
  92.4 3.2 %copy-start.14 = (bf16[288,512]{1,0:T(8,128)(2,1)S(1)}, bf16[288,512]{1,0:T(8,128)(2,1)}, u32[]{:S(2)}) copy-start(bf16[288,512]{1,0:T(8,128)(2,1)} %copy-done.13) | copy-start | bytes 884740
  96.6 20.0 %copy-start.17 = (bf16[288,512]{1,0:T(8,128)(2,1)}, bf16[288,512]{1,0:T(8,128)(2,1)S(1)}, u32[]{:S(2)}) copy-start(bf16[288,512]{1,0:T(8,128)(2,1)S(1)} %get-tuple-element.66) | copy-start | bytes 884740
  120.7 18.4 %collective-permute-start.5 = (bf16[4,1,72,1024]{3,2,1,0:T(8,128)(2,1)}, bf16[4,1,72,1024]{3,2,1,0:T(8,128)(2,1)}, u32[]{:S(2)}, u32[]{:S(2)}) collective-permute-start(bf16[4,1,72,1024]{3,2,1,0:T(8,128)(2,1)} %get-tuple-element.57), channel_id=1, source_target_pairs={{7,0},{0,1},{1,2},{2,3},{3,4},{4,5},{5,6},{6,7},{15,8},{8,9},{9,10... | collective-permute-start | bytes 1769480 | tf_op jit(solution)/shard_map/ppermute | solution.py:135
  121.6 28.0 %collective-permute-start.6 = (bf16[4,1,72,1024]{3,2,1,0:T(8,128)(2,1)}, bf16[4,1,72,1024]{3,2,1,0:T(8,128)(2,1)}, u32[]{:S(2)}, u32[]{:S(2)}) collective-permute-start(bf16[4,1,72,1024]{3,2,1,0:T(8,128)(2,1)} %get-tuple-element.56), channel_id=1, source_target_pairs={{1,0},{2,1},{3,2},{4,3},{5,4},{6,5},{7,6},{0,7},{9,8},{10,9},{11,1... | collective-permute-start | bytes 1769480 | tf_op jit(solution)/shard_map/ppermute | solution.py:135
  129.5 5.0 %copy-start.12 = (bf16[512,288]{1,0:T(8,128)(2,1)S(1)}, bf16[512,288]{1,0:T(8,128)(2,1)}, u32[]{:S(2)}) copy-start(bf16[512,288]{1,0:T(8,128)(2,1)} %copy.90) | copy-start | bytes 884740
  151.0 3.0 %copy-start.11 = (f32[288,8,64]{0,2,1:T(8,128)S(1)}, f32[288,8,64]{0,2,1:T(8,128)}, u32[]{:S(2)}) copy-start(f32[288,8,64]{0,2,1:T(8,128)} %copy.83) | copy-start | bytes 1769476
  151.2 6.4 %copy-start.25 = (f32[288,8]{0,1:T(8,128)S(1)}, f32[288,8]{0,1:T(8,128)}, u32[]{:S(2)}) copy-start(f32[288,8]{0,1:T(8,128)} %copy-done.24) | copy-start | bytes 27652
  152.0 6.8 %collective-permute-start.7 = (bf16[1,2,72,1024]{3,2,1,0:T(8,128)(2,1)}, bf16[1,2,72,1024]{3,2,1,0:T(8,128)(2,1)}, u32[]{:S(2)}, u32[]{:S(2)}) collective-permute-start(bf16[1,2,72,1024]{3,2,1,0:T(8,128)(2,1)} %get-tuple-element.59), channel_id=1, source_target_pairs={{0,8},{8,16},{16,24},{24,32},{32,40},{40,48},{48,56},{56,64},{64,7... | collective-permute-start | bytes 884744 | tf_op jit(solution)/shard_map/ppermute | solution.py:141
  154.1 8.4 %collective-permute-start.8 = (bf16[1,2,72,1024]{3,2,1,0:T(8,128)(2,1)}, bf16[1,2,72,1024]{3,2,1,0:T(8,128)(2,1)}, u32[]{:S(2)}, u32[]{:S(2)}) collective-permute-start(bf16[1,2,72,1024]{3,2,1,0:T(8,128)(2,1)} %get-tuple-element.58), channel_id=1, source_target_pairs={{8,0},{16,8},{24,16},{32,24},{40,32},{48,40},{56,48},{64,56},{72,6... | collective-permute-start | bytes 884744 | tf_op jit(solution)/shard_map/ppermute | solution.py:141
  166.2 2.7 %copy-start.1 = (f32[288,512]{1,0:T(8,128)S(1)}, f32[288,512]{1,0:T(8,128)}, u32[]{:S(2)}) copy-start(f32[288,512]{1,0:T(8,128)} %copy-done) | copy-start | bytes 1769476
  166.2 2.7 %copy-start.5 = (bf16[288,1536]{1,0:T(8,128)(2,1)S(1)}, bf16[288,1536]{1,0:T(8,128)(2,1)}, u32[]{:S(2)}) copy-start(bf16[288,1536]{1,0:T(8,128)(2,1)} %copy-done.4) | copy-start | bytes 2654212
  168.9 2.2 copy-start.15
  168.9 2.2 copy-start.22
  171.0 1.1 copy-start.20
  171.0 1.1 copy-start.21
  171.1 1.2 copy-start.8
  172.4 2.7 %collective-permute-start.9 = (bf16[8,32,2048]{2,1,0:T(8,128)(2,1)S(1)}, bf16[8,32,2048]{2,1,0:T(8,128)(2,1)S(1)}, u32[]{:S(2)}, u32[]{:S(2)}) collective-permute-start(bf16[8,32,2048]{2,1,0:T(8,128)(2,1)S(1)} %fusion.24), channel_id=1, source_target_pairs={{0,8},{8,0},{16,24},{24,16},{32,40},{40,32},{48,56},{56,48},{64,72... | collective-permute-start | bytes 3145736 | tf_op jit(solution)/shard_map/ppermute | solution.py:168
  198.1 29.8 %copy-start.16 = (bf16[288,512]{1,0:T(8,128)(2,1)S(1)}, bf16[288,512]{1,0:T(8,128)(2,1)}, u32[]{:S(2)}) copy-start(bf16[288,512]{1,0:T(8,128)(2,1)} %get-tuple-element.67) | copy-start | bytes 884740
  198.2 30.6 %copy-start.3 = (f32[288,512]{1,0:T(8,128)S(1)}, f32[288,512]{1,0:T(8,128)}, u32[]{:S(2)}) copy-start(f32[288,512]{1,0:T(8,128)} %copy-done.2) | copy-start | bytes 1769476
  198.2 30.6 %copy-start.10 = (bf16[512,2048]{1,0:T(8,128)(2,1)S(1)}, bf16[512,2048]{1,0:T(8,128)(2,1)}, u32[]{:S(2)}) copy-start(bf16[512,2048]{1,0:T(8,128)(2,1)} %copy-done.9) | copy-start | bytes 6291460
  222.2 17.8 %all-to-all-start.3 = ((bf16[32,2,2048]{2,1,0:T(2,128)(2,1)}), bf16[32,2,2048]{2,1,0:T(2,128)(2,1)}, u32[]{:S(2)}, u32[]{:S(2)}) async-start(bf16[32,2,2048]{2,1,0:T(2,128)(2,1)} %broadcast_in_dim.11), calls=%async_computation.3 | async-start | bytes 524288 | tf_op jit(solution)/shard_map/all_to_all | solution.py:162

commit v4 on v3

--- a/solution.py
+++ b/solution.py
@@ -281,8 +281,8 @@
     kv_source = jnp.concatenate([key_b, proj_b[:, 2 * model_width :]], axis=1).reshape(
         row_units, col_units, query_count, 2 * model_width
     )
-    ext_rows = with_halo(kv_source, (("lat", 0),), 1, False)
-    ext_kv = with_halo(ext_rows, (("lon", 1),), 1, True)
+    ext_cols = with_halo(kv_source, (("lon", 1),), 1, True)
+    ext_kv = with_halo(ext_cols, (("lat", 0),), 1, False)
     block = 16 * pl.cdiv(query_count, 16)
     ext_kv = jnp.pad(ext_kv, ((0, 0), (0, 0), (0, block - query_count), (0, 0)))
     level_win = (jnp.arange(block) // (half_h * half_w) + WL // 2) // WL
@@ -310,18 +310,18 @@
     grad_q = unit_back(
         query_f, query_scale, dquery.reshape(tok_count, head_count, head_dim)
     ).reshape(tok_count, model_width)
-    west_rim = ext_grad[:, :1]
-    east_rim = ext_grad[:, col_units + 1 :]
-    center = ext_grad[:, 1 : col_units + 1]
+    north_rim = ext_grad[:1]
+    south_rim = ext_grad[row_units + 1 :]
+    rows = ext_grad[1 : row_units + 1]
+    from_south = from_behind_2(north_rim.astype(jnp.bfloat16), "lat", -1).astype(north_rim.dtype)
+    from_north = from_behind_2(south_rim.astype(jnp.bfloat16), "lat", 1).astype(south_rim.dtype)
+    rows = rows.at[:1].add(from_north).at[row_units - 1 :].add(from_south)
+    west_rim = rows[:, :1]
+    east_rim = rows[:, col_units + 1 :]
+    middle = rows[:, 1 : col_units + 1]
     from_east = from_behind(west_rim.astype(jnp.bfloat16), "lon", -1).astype(west_rim.dtype)
     from_west = from_behind(east_rim.astype(jnp.bfloat16), "lon", 1).astype(east_rim.dtype)
-    center = center.at[:, :1].add(from_west).at[:, col_units - 1 :].add(from_east)
-    north_rim = center[:1]
-    south_rim = center[row_units + 1 :]
-    middle = center[1 : row_units + 1]
-    from_south = from_behind_2(north_rim.astype(jnp.bfloat16), "lat", -1).astype(north_rim.dtype)
-    from_north = from_behind_2(south_rim.astype(jnp.bfloat16), "lat", 1).astype(south_rim.dtype)
-    middle = middle.at[:1].add(from_north).at[row_units - 1 :].add(from_south)
+    middle = middle.at[:, :1].add(from_west).at[:, col_units - 1 :].add(from_east)
     own_grads = middle.reshape(tok_count, 2 * model_width)
     grad_k = unit_back(
         key_f, key_scale, own_grads[:, :model_width].reshape(tok_count, head_count, head_dim)

time: 244 us -> 229 us (0.939)
  waiting for transfers between devices: 46.8 us -> 32.1 us
    ppermute x2, waiting for transfers between devices: 9.17 us -> 4.22 us  [with_halo(): before = lax.ppermute(last, axis, up)]
    ppermute x2, waiting for transfers between devices: 11.9 us -> 7.04 us  [with_halo(): after = lax.ppermute(initial, axis, down)]
    ppermute x2, waiting for transfers between devices: 2.59 us -> 0.01 us  [from_behind_2(): return lax.ppermute(block, axis, route)]
  transfers between devices with their start and end apart: 11 -> 11, of which waited for: 9 -> 8; matrix products, arithmetic and copies ran while one was open for 12% -> 13% of each run, Pallas kernels for 0% -> 0%
where the time goes in v4:
time: 229 us; the launch traced here: 227 us
  blocking collectives  66.4 us (29%)
  local copies, waits for them, and re-layouts  32.2 us (14%)
  waiting for transfers between devices  32.1 us (14%)
  starting transfers between devices  30.3 us (13%)
  Pallas kernels  29.7 us (13%)
  other arithmetic  26 us (11%)
  matrix products  9.36 us (4%)
    all_to_all x2, blocking collectives, sum_rows(): spread = lax.all_to_all(chunks, axis, 0, 0, tiled=False)  42.8 us
    all_to_all x1, blocking collectives, gather_rows(): spread = lax.all_to_all(copies, axis, 0, 0, tiled=False)  23.6 us
    pallas_call x1, Pallas kernels, window_bwd(): pl.pallas_call(attn_bwd_kernel, grid=(row_units, col_units), in_specs=[pl...  17.8 us
    pallas_call x1, Pallas kernels, window_fwd(): pl.pallas_call(attn_fwd_kernel, grid=(row_units, col_units), in_specs=[pl...  11.9 us
    ppermute x2, waiting for transfers between devices, from_behind(): return lax.ppermute(block, axis, route)  9.26 us
    all_to_all x1, waiting for transfers between devices, sum_everywhere(): spread = lax.all_to_all(copies, axis, 0, 0, tiled=False)  8.32 us
    ppermute x2, waiting for transfers between devices, with_halo(): after = lax.ppermute(initial, axis, down)  7.04 us
    ppermute x2, starting transfers between devices, with_halo(): after = lax.ppermute(initial, axis, down)  6.6 us
  transfers between devices with their start and end apart: 11, of which 8 were waited for; matrix products, arithmetic and copies ran while one was open for 13% of the time, Pallas kernels for 0%

profile of v4, /device:TPU:1, one launch (start us, length us, event | category | flops | bytes accessed | tf_op | source)
XLA Modules:
  0.0 227.4 jit_solution(7631536418526609053)
XLA Ops:
  2.3 23.6 %all_to_all.20 = bf16[8,64,1024]{2,1,0:T(8,128)(2,1)S(1)} all-to-all(bf16[8,64,1024]{2,1,0:T(8,128)(2,1)S(1)} %broadcast_in_dim.9), channel_id=1, replica_groups=mesh['lat'=32,'lon'=8] {'lon'}, dimensions={0} | all-to-all | bytes 2097152 | tf_op jit(solution)/shard_map/all_to_all | solution.py:147
  25.9 1.9 collective-permute-start
  34.7 4.5 %collective-permute-start.2 = (bf16[2,1,72,1024]{3,2,1,0:T(8,128)(2,1)}, bf16[2,1,72,1024]{3,2,1,0:T(8,128)(2,1)}, u32[]{:S(2)}, u32[]{:S(2)}) collective-permute-start(bf16[2,1,72,1024]{3,2,1,0:T(8,128)(2,1)} %get-tuple-element.69), channel_id=1, source_target_pairs={{1,0},{2,1},{3,2},{4,3},{5,4},{6,5},{7,6},{0,7},{9,8},{10,9},{11,1... | collective-permute-start | bytes 884744 | tf_op jit(solution)/shard_map/ppermute | solution.py:127
  39.3 1.1 copy.99
  42.1 4.2 %collective-permute-done.1 = bf16[2,1,72,1024]{3,2,1,0:T(8,128)(2,1)} collective-permute-done((bf16[2,1,72,1024]{3,2,1,0:T(8,128)(2,1)}, bf16[2,1,72,1024]{3,2,1,0:T(8,128)(2,1)}, u32[]{:S(2)}, u32[]{:S(2)}) %collective-permute-start.1) | collective-permute-done | bytes 294944 | tf_op jit(solution)/shard_map/ppermute | solution.py:126
  46.3 3.9 %collective-permute-done.2 = bf16[2,1,72,1024]{3,2,1,0:T(8,128)(2,1)} collective-permute-done((bf16[2,1,72,1024]{3,2,1,0:T(8,128)(2,1)}, bf16[2,1,72,1024]{3,2,1,0:T(8,128)(2,1)}, u32[]{:S(2)}, u32[]{:S(2)}) %collective-permute-start.2) | collective-permute-done | bytes 294944 | tf_op jit(solution)/shard_map/ppermute | solution.py:127
  50.2 1.2 pad_maximum_fusion
  51.5 1.1 fusion.45
  52.6 4.6 %collective-permute-start.3 = (bf16[1,4,72,1024]{3,2,1,0:T(8,128)(2,1)}, bf16[1,4,72,1024]{3,2,1,0:T(8,128)(2,1)}, u32[]{:S(2)}, u32[]{:S(2)}) collective-permute-start(bf16[1,4,72,1024]{3,2,1,0:T(8,128)(2,1)} %get-tuple-element.60), channel_id=1, source_target_pairs={{0,8},{8,16},{16,24},{24,32},{32,40},{40,48},{48,56},{56,64},{64,7... | collective-permute-start | bytes 1769480 | tf_op jit(solution)/shard_map/ppermute | solution.py:126
  57.2 2.1 collective-permute-start.4
  59.5 2.1 reshape.387
  61.6 2.1 copy.93
  63.7 1.9 multiply_convert_fusion.1.q_ref
  65.6 3.1 %collective-permute-done.4 = bf16[1,4,72,1024]{3,2,1,0:T(8,128)(2,1)} collective-permute-done((bf16[1,4,72,1024]{3,2,1,0:T(8,128)(2,1)}, bf16[1,4,72,1024]{3,2,1,0:T(8,128)(2,1)}, u32[]{:S(2)}, u32[]{:S(2)}) %collective-permute-start.4) | collective-permute-done | bytes 589856 | tf_op jit(solution)/shard_map/ppermute | solution.py:127
  68.7 2.9 %fusion.7.kv_ref = bf16[4,4,80,1024]{3,2,1,0:T(8,128)(2,1)} fusion(bf16[1,4,72,1024]{3,2,1,0:T(8,128)(2,1)} %collective-permute-done.4, bf16[1,4,72,1024]{3,2,1,0:T(8,128)(2,1)} %collective-permute-done.3, bf16[2,1,72,1024]{3,2,1,0:T(8,128)(2,1)} %collective-permute-done.2, bf16[2,1,72,1024]{3,2,1,0:T(8,128)(2,1)} %collective-permute-done.1, ...), kind=kLoop, calls=%fused_computation.12 | loop fusion | flops 24903680 | bytes 4980736 | tf_op jit(solution)/shard_map/concatenate | solution.py:128
  71.6 11.9 %shard_map.93 = f32[2,2,72,512]{3,2,1,0:T(8,128)} custom-call(f32[8]{0:T(128)} %tau_ref.3, bf16[2,2,72,512]{3,2,1,0:T(8,128)(2,1)} %multiply_convert_fusion.1.q_ref, bf16[4,4,80,1024]{3,2,1,0:T(8,128)(2,1)} %fusion.7.kv_ref, f32[2,72,320]{2,1,0:T(8,128)} %convert_element_type.114.mask_ref), custom_call_target="tpu_custom_call" | custom-call | tf_op jit(solution)/shard_map/pallas_call | solution.py:81
  83.5 1.1 convert_element_type.115
  84.7 1.5 fusion.47
  87.7 2.2 convolution_convert_fusion.3
  89.9 17.8 %shard_map.94 = (f32[2,2,72,512]{3,2,1,0:T(8,128)}, f32[4,4,80,1024]{3,2,1,0:T(8,128)}) custom-call(f32[8]{0:T(128)} %tau_ref.3, bf16[2,2,72,512]{3,2,1,0:T(8,128)(2,1)} %multiply_convert_fusion.1.q_ref, bf16[4,4,80,1024]{3,2,1,0:T(8,128)(2,1)} %fusion.7.kv_ref, bf16[2,2,72,512]{3,2,1,0:T(8,128)(2,1)} %bitcast.102, f32[2,72,320]{2,1,0:T(8,128)} %convert_element_type.114.mask_ref), custom_call_target="tpu_custom_call" | custom-call | tf_op jit(solution)/shard_map/pallas_call | solution.py:98
  107.7 2.9 %convert.35 = bf16[4,4,80,1024]{3,2,1,0:T(8,128)(2,1)S(1)} convert(f32[4,4,80,1024]{3,2,1,0:T(8,128)} %get-tuple-element.55) | non-fusion elementwise | flops 1310720 | bytes 7864320 | tf_op jit(solution)/shard_map/convert.19
  110.6 1.2 fusion.43
  111.8 1.9 collective-permute-start.5
  113.7 3.2 %collective-permute-start.6 = (bf16[1,4,72,1024]{3,2,1,0:T(8,128)(2,1)}, bf16[1,4,72,1024]{3,2,1,0:T(8,128)(2,1)}, u32[]{:S(2)}, u32[]{:S(2)}) collective-permute-start(bf16[1,4,72,1024]{3,2,1,0:T(8,128)(2,1)} %get-tuple-element.56), channel_id=1, source_target_pairs={{8,0},{16,8},{24,16},{32,24},{40,32},{48,40},{56,48},{64,56},{72,6... | collective-permute-start | bytes 1769480 | tf_op jit(solution)/shard_map/ppermute | solution.py:141
  117.0 1.1 copy.85
  118.0 1.8 slice.197
  120.8 2.4 %reshape.377 = f32[288,8,64]{2,1,0:T(8,128)} reshape(f32[2,2,72,512]{3,2,1,0:T(8,128)} %get-tuple-element.54) | data formatting | bytes 1179648 | tf_op jit(solution)/shard_map/reshape | solution.py:311
  123.2 2.6 %copy.83 = f32[288,8,64]{0,2,1:T(8,128)} copy(f32[288,8,64]{2,1,0:T(8,128)} %reshape.377) | data formatting | bytes 1179648 | tf_op jit(solution)/shard_map/reshape | solution.py:311
  125.8 2.2 convolution_convert_fusion.2
  128.0 1.6 add_dynamic-update-slice_fusion
  129.6 1.4 fusion.22
  133.1 4.5 %collective-permute-start.8 = (bf16[2,1,72,1024]{3,2,1,0:T(8,128)(2,1)}, bf16[2,1,72,1024]{3,2,1,0:T(8,128)(2,1)}, u32[]{:S(2)}, u32[]{:S(2)}) collective-permute-start(bf16[2,1,72,1024]{3,2,1,0:T(8,128)(2,1)} %get-tuple-element.58), channel_id=1, source_target_pairs={{1,0},{2,1},{3,2},{4,3},{5,4},{6,5},{7,6},{0,7},{9,8},{10,9},{11,1... | collective-permute-start | bytes 884744 | tf_op jit(solution)/shard_map/ppermute | solution.py:135
  137.6 1.1 copy.84
  138.8 5.9 %collective-permute-done.7 = bf16[2,1,72,1024]{3,2,1,0:T(8,128)(2,1)} collective-permute-done((bf16[2,1,72,1024]{3,2,1,0:T(8,128)(2,1)}, bf16[2,1,72,1024]{3,2,1,0:T(8,128)(2,1)}, u32[]{:S(2)}, u32[]{:S(2)}) %collective-permute-start.7) | collective-permute-done | bytes 294944 | tf_op jit(solution)/shard_map/ppermute | solution.py:135
  144.7 1.0 fusion.32
  145.8 3.4 %collective-permute-done.8 = bf16[2,1,72,1024]{3,2,1,0:T(8,128)(2,1)} collective-permute-done((bf16[2,1,72,1024]{3,2,1,0:T(8,128)(2,1)}, bf16[2,1,72,1024]{3,2,1,0:T(8,128)(2,1)}, u32[]{:S(2)}, u32[]{:S(2)}) %collective-permute-start.8) | collective-permute-done | bytes 294944 | tf_op jit(solution)/shard_map/ppermute | solution.py:135
  149.1 1.1 fusion.31
  151.0 1.9 convert_multiply_fusion.1
  152.9 1.4 copy.86
  154.5 1.1 copy.87
  155.6 2.1 fusion.34
  159.6 2.3 %collective-permute-done.9 = bf16[8,32,2048]{2,1,0:T(8,128)(2,1)S(1)} collective-permute-done((bf16[8,32,2048]{2,1,0:T(8,128)(2,1)S(1)}, bf16[8,32,2048]{2,1,0:T(8,128)(2,1)S(1)}, u32[]{:S(2)}, u32[]{:S(2)}) %collective-permute-start.9) | collective-permute-done | bytes 1048608 | tf_op jit(solution)/shard_map/ppermute | solution.py:168
  162.2 21.1 %all_to_all.21 = bf16[8,32,2048]{2,1,0:T(8,128)(2,1)S(1)} all-to-all(bf16[8,32,2048]{2,1,0:T(8,128)(2,1)S(1)} %fusion.12), channel_id=1, replica_groups=mesh['lat'=32,'lon'=8] {'lon'}, dimensions={0} | all-to-all | bytes 2097152 | tf_op jit(solution)/shard_map/all_to_all | solution.py:154
  184.4 21.7 %all_to_all.22 = bf16[32,2,2048]{2,1,0:T(2,128)(2,1)S(1)} all-to-all(bf16[32,2,2048]{2,1,0:T(2,128)(2,1)} %reshape.380), channel_id=1, replica_groups=mesh['lat'=32,'lon'=8] {'lat'}, dimensions={0} | all-to-all | bytes 524288 | tf_op jit(solution)/shard_map/all_to_all | solution.py:154
  207.2 5.7 %all-to-all-start.3 = ((bf16[32,2,2048]{2,1,0:T(2,128)(2,1)}), bf16[32,2,2048]{2,1,0:T(2,128)(2,1)}, u32[]{:S(2)}, u32[]{:S(2)}) async-start(bf16[32,2,2048]{2,1,0:T(2,128)(2,1)} %broadcast_in_dim.11), calls=%async_computation.3 | async-start | bytes 524288 | tf_op jit(solution)/shard_map/all_to_all | solution.py:162
  213.9 1.8 fusion.19
  216.6 8.3 %all-to-all-done.3 = bf16[32,2,2048]{2,1,0:T(2,128)(2,1)} async-done(((bf16[32,2,2048]{2,1,0:T(2,128)(2,1)}), bf16[32,2,2048]{2,1,0:T(2,128)(2,1)}, u32[]{:S(2)}, u32[]{:S(2)}) %all-to-all-start.3) | async-done | bytes 262176 | tf_op jit(solution)/shard_map/all_to_all | solution.py:162
  225.0 1.0 reshape.383
  (126 shorter events, 23.6 us)
Async XLA Ops:
  1.8 25.9 %copy-start.23 = (bf16[4,6,12,512]{3,0,2,1:T(4,128)(2,1)S(1)}, bf16[4,6,12,512]{3,0,2,1:T(4,128)(2,1)}, u32[]{:S(2)}) copy-start(bf16[4,6,12,512]{3,0,2,1:T(4,128)(2,1)} %param.14) | copy-start | bytes 884740
  2.2 25.8 %copy-start.18 = (bf16[4,6,12,512]{3,0,2,1:T(4,128)(2,1)S(1)}, bf16[4,6,12,512]{3,0,2,1:T(4,128)(2,1)}, u32[]{:S(2)}) copy-start(bf16[4,6,12,512]{3,0,2,1:T(4,128)(2,1)} %param.19) | copy-start | bytes 884740
  2.2 25.8 %copy-start.26 = (f32[512]{0:T(512)S(1)}, f32[512]{0:T(512)}, u32[]{:S(2)}) copy-start(f32[512]{0:T(512)} %param.17) | copy-start | bytes 6148
  25.9 4.2 %collective-permute-start = (bf16[512,1024]{1,0:T(8,128)(2,1)S(1)}, bf16[512,1024]{1,0:T(8,128)(2,1)S(1)}, u32[]{:S(2)}, u32[]{:S(2)}) collective-permute-start(bf16[512,1024]{1,0:T(8,128)(2,1)S(1)} %bitcast.87), channel_id=1, source_target_pairs={{0,8},{8,0},{16,24},{24,16},{32,40},{40,32},{48,56},{56,48},{64,72... | collective-permute-start | bytes 3145736 | tf_op jit(solution)/shard_map/ppermute | solution.py:168
  27.9 2.9 %copy-start.13 = (bf16[288,512]{1,0:T(8,128)(2,1)}, bf16[288,512]{1,0:T(8,128)(2,1)S(1)}, u32[]{:S(2)}) copy-start(bf16[288,512]{1,0:T(8,128)(2,1)S(1)} %reshape_reshape.10) | copy-start | bytes 884740
  30.8 1.4 copy-start.9
  32.2 0.9 copy-start.4
  33.2 8.6 %copy-start = (f32[288,512]{1,0:T(8,128)}, f32[288,512]{1,0:T(8,128)S(1)}, u32[]{:S(2)}) copy-start(f32[288,512]{1,0:T(8,128)S(1)} %copy.79) | copy-start | bytes 1769476
  33.2 7.5 %copy-start.19 = (f32[2,2,72,80]{3,1,2,0:T(2,128)S(1)}, f32[2,2,72,80]{3,1,2,0:T(2,128)}, u32[]{:S(2)}) copy-start(f32[2,2,72,80]{3,1,2,0:T(2,128)} %and_convert_fusion) | copy-start | bytes 276484
  33.3 8.6 %copy-start.6 = (bf16[288,512]{1,0:T(8,128)(2,1)}, bf16[288,512]{1,0:T(8,128)(2,1)S(1)}, u32[]{:S(2)}) copy-start(bf16[288,512]{1,0:T(8,128)(2,1)S(1)} %fusion.27) | copy-start | bytes 884740
  34.2 12.2 %collective-permute-start.1 = (bf16[2,1,72,1024]{3,2,1,0:T(8,128)(2,1)}, bf16[2,1,72,1024]{3,2,1,0:T(8,128)(2,1)}, u32[]{:S(2)}, u32[]{:S(2)}) collective-permute-start(bf16[2,1,72,1024]{3,2,1,0:T(8,128)(2,1)} %get-tuple-element.68), channel_id=1, source_target_pairs={{0,1},{1,2},{2,3},{3,4},{4,5},{5,6},{6,7},{7,0},{8,9},{9,10},{10,1... | collective-permute-start | bytes 884744 | tf_op jit(solution)/shard_map/ppermute | solution.py:126
  34.7 15.5 %collective-permute-start.2 = (bf16[2,1,72,1024]{3,2,1,0:T(8,128)(2,1)}, bf16[2,1,72,1024]{3,2,1,0:T(8,128)(2,1)}, u32[]{:S(2)}, u32[]{:S(2)}) collective-permute-start(bf16[2,1,72,1024]{3,2,1,0:T(8,128)(2,1)} %get-tuple-element.69), channel_id=1, source_target_pairs={{1,0},{2,1},{3,2},{4,3},{5,4},{6,5},{7,6},{0,7},{9,8},{10,9},{11,1... | collective-permute-start | bytes 884744 | tf_op jit(solution)/shard_map/ppermute | solution.py:127
  41.8 44.9 %copy-start.2 = (f32[288,512]{1,0:T(8,128)}, f32[288,512]{1,0:T(8,128)S(1)}, u32[]{:S(2)}) copy-start(f32[288,512]{1,0:T(8,128)S(1)} %reshape.381) | copy-start | bytes 1769476
  52.6 13.0 %collective-permute-start.3 = (bf16[1,4,72,1024]{3,2,1,0:T(8,128)(2,1)}, bf16[1,4,72,1024]{3,2,1,0:T(8,128)(2,1)}, u32[]{:S(2)}, u32[]{:S(2)}) collective-permute-start(bf16[1,4,72,1024]{3,2,1,0:T(8,128)(2,1)} %get-tuple-element.60), channel_id=1, source_target_pairs={{0,8},{8,16},{16,24},{24,32},{32,40},{40,48},{48,56},{56,64},{64,7... | collective-permute-start | bytes 1769480 | tf_op jit(solution)/shard_map/ppermute | solution.py:126
  57.2 11.5 %collective-permute-start.4 = (bf16[1,4,72,1024]{3,2,1,0:T(8,128)(2,1)}, bf16[1,4,72,1024]{3,2,1,0:T(8,128)(2,1)}, u32[]{:S(2)}, u32[]{:S(2)}) collective-permute-start(bf16[1,4,72,1024]{3,2,1,0:T(8,128)(2,1)} %get-tuple-element.61), channel_id=1, source_target_pairs={{8,0},{16,8},{24,16},{32,24},{40,32},{48,40},{56,48},{64,56},{72,6... | collective-permute-start | bytes 1769480 | tf_op jit(solution)/shard_map/ppermute | solution.py:127
  59.4 4.3 %copy-start.24 = (f32[288,8]{0,1:T(8,128)}, f32[288,8]{0,1:T(8,128)S(1)}, u32[]{:S(2)}) copy-start(f32[288,8]{0,1:T(8,128)S(1)} %multiply_reduce_fusion.1) | copy-start | bytes 27652
  59.5 9.2 %copy-start.7 = (bf16[288,512]{1,0:T(8,128)(2,1)S(1)}, bf16[288,512]{1,0:T(8,128)(2,1)}, u32[]{:S(2)}) copy-start(bf16[288,512]{1,0:T(8,128)(2,1)} %copy-done.6) | copy-start | bytes 884740
  83.5 3.2 %copy-start.14 = (bf16[288,512]{1,0:T(8,128)(2,1)S(1)}, bf16[288,512]{1,0:T(8,128)(2,1)}, u32[]{:S(2)}) copy-start(bf16[288,512]{1,0:T(8,128)(2,1)} %copy-done.13) | copy-start | bytes 884740
  87.7 20.0 %copy-start.17 = (bf16[288,512]{1,0:T(8,128)(2,1)}, bf16[288,512]{1,0:T(8,128)(2,1)S(1)}, u32[]{:S(2)}) copy-start(bf16[288,512]{1,0:T(8,128)(2,1)S(1)} %get-tuple-element.66) | copy-start | bytes 884740
  111.8 16.2 %collective-permute-start.5 = (bf16[1,4,72,1024]{3,2,1,0:T(8,128)(2,1)}, bf16[1,4,72,1024]{3,2,1,0:T(8,128)(2,1)}, u32[]{:S(2)}, u32[]{:S(2)}) collective-permute-start(bf16[1,4,72,1024]{3,2,1,0:T(8,128)(2,1)} %get-tuple-element.57), channel_id=1, source_target_pairs={{0,8},{8,16},{16,24},{24,32},{32,40},{40,48},{48,56},{56,64},{64,7... | collective-permute-start | bytes 1769480 | tf_op jit(solution)/shard_map/ppermute | solution.py:141
  113.7 15.9 %collective-permute-start.6 = (bf16[1,4,72,1024]{3,2,1,0:T(8,128)(2,1)}, bf16[1,4,72,1024]{3,2,1,0:T(8,128)(2,1)}, u32[]{:S(2)}, u32[]{:S(2)}) collective-permute-start(bf16[1,4,72,1024]{3,2,1,0:T(8,128)(2,1)} %get-tuple-element.56), channel_id=1, source_target_pairs={{8,0},{16,8},{24,16},{32,24},{40,32},{48,40},{56,48},{64,56},{72,6... | collective-permute-start | bytes 1769480 | tf_op jit(solution)/shard_map/ppermute | solution.py:141
  120.8 5.0 %copy-start.12 = (bf16[512,288]{1,0:T(8,128)(2,1)S(1)}, bf16[512,288]{1,0:T(8,128)(2,1)}, u32[]{:S(2)}) copy-start(bf16[512,288]{1,0:T(8,128)(2,1)} %copy.90) | copy-start | bytes 884740
  131.0 2.0 copy-start.11
  131.2 6.4 %copy-start.25 = (f32[288,8]{0,1:T(8,128)S(1)}, f32[288,8]{0,1:T(8,128)}, u32[]{:S(2)}) copy-start(f32[288,8]{0,1:T(8,128)} %copy-done.24) | copy-start | bytes 27652
  132.1 12.7 %collective-permute-start.7 = (bf16[2,1,72,1024]{3,2,1,0:T(8,128)(2,1)}, bf16[2,1,72,1024]{3,2,1,0:T(8,128)(2,1)}, u32[]{:S(2)}, u32[]{:S(2)}) collective-permute-start(bf16[2,1,72,1024]{3,2,1,0:T(8,128)(2,1)} %get-tuple-element.59), channel_id=1, source_target_pairs={{7,0},{0,1},{1,2},{2,3},{3,4},{4,5},{5,6},{6,7},{15,8},{8,9},{9,10... | collective-permute-start | bytes 884744 | tf_op jit(solution)/shard_map/ppermute | solution.py:135
  133.1 16.1 %collective-permute-start.8 = (bf16[2,1,72,1024]{3,2,1,0:T(8,128)(2,1)}, bf16[2,1,72,1024]{3,2,1,0:T(8,128)(2,1)}, u32[]{:S(2)}, u32[]{:S(2)}) collective-permute-start(bf16[2,1,72,1024]{3,2,1,0:T(8,128)(2,1)} %get-tuple-element.58), channel_id=1, source_target_pairs={{1,0},{2,1},{3,2},{4,3},{5,4},{6,5},{7,6},{0,7},{9,8},{10,9},{11,1... | collective-permute-start | bytes 884744 | tf_op jit(solution)/shard_map/ppermute | solution.py:135
  152.9 2.7 %copy-start.1 = (f32[288,512]{1,0:T(8,128)S(1)}, f32[288,512]{1,0:T(8,128)}, u32[]{:S(2)}) copy-start(f32[288,512]{1,0:T(8,128)} %copy-done) | copy-start | bytes 1769476
  152.9 2.7 %copy-start.5 = (bf16[288,1536]{1,0:T(8,128)(2,1)S(1)}, bf16[288,1536]{1,0:T(8,128)(2,1)}, u32[]{:S(2)}) copy-start(bf16[288,1536]{1,0:T(8,128)(2,1)} %copy-done.4) | copy-start | bytes 2654212
  155.5 2.2 copy-start.15
  155.5 2.2 copy-start.22
  157.7 1.1 copy-start.20
  157.7 1.1 copy-start.21
  157.7 1.2 copy-start.8
  159.1 2.8 %collective-permute-start.9 = (bf16[8,32,2048]{2,1,0:T(8,128)(2,1)S(1)}, bf16[8,32,2048]{2,1,0:T(8,128)(2,1)S(1)}, u32[]{:S(2)}, u32[]{:S(2)}) collective-permute-start(bf16[8,32,2048]{2,1,0:T(8,128)(2,1)S(1)} %fusion.24), channel_id=1, source_target_pairs={{0,8},{8,0},{16,24},{24,16},{32,40},{40,32},{48,56},{56,48},{64,72... | collective-permute-start | bytes 3145736 | tf_op jit(solution)/shard_map/ppermute | solution.py:168
  183.3 29.6 %copy-start.16 = (bf16[288,512]{1,0:T(8,128)(2,1)S(1)}, bf16[288,512]{1,0:T(8,128)(2,1)}, u32[]{:S(2)}) copy-start(bf16[288,512]{1,0:T(8,128)(2,1)} %get-tuple-element.67) | copy-start | bytes 884740
  183.4 30.4 %copy-start.3 = (f32[288,512]{1,0:T(8,128)S(1)}, f32[288,512]{1,0:T(8,128)}, u32[]{:S(2)}) copy-start(f32[288,512]{1,0:T(8,128)} %copy-done.2) | copy-start | bytes 1769476
  183.4 30.4 %copy-start.10 = (bf16[512,2048]{1,0:T(8,128)(2,1)S(1)}, bf16[512,2048]{1,0:T(8,128)(2,1)}, u32[]{:S(2)}) copy-start(bf16[512,2048]{1,0:T(8,128)(2,1)} %copy-done.9) | copy-start | bytes 6291460
  207.2 17.8 %all-to-all-start.3 = ((bf16[32,2,2048]{2,1,0:T(2,128)(2,1)}), bf16[32,2,2048]{2,1,0:T(2,128)(2,1)}, u32[]{:S(2)}, u32[]{:S(2)}) async-start(bf16[32,2,2048]{2,1,0:T(2,128)(2,1)} %broadcast_in_dim.11), calls=%async_computation.3 | async-start | bytes 524288 | tf_op jit(solution)/shard_map/all_to_all | solution.py:162

commit v5 on v4

--- a/solution.py
+++ b/solution.py
@@ -26,49 +26,71 @@
     return lax.dot_general(a, b, (((0,), (0,)), ((), ())), preferred_element_type=jnp.float32)
 
 
-def _window_probs(tau_ref, head, query, keys, mask):
-    scores = _nt(query, keys) * tau_ref[head]
+def _window_probs(tau, query, keys, mask):
+    scores = _nt(query, keys) * tau
     weights = jnp.exp(scores) * mask
     return weights / jnp.sum(weights, axis=-1, keepdims=True)
 
 
-def _head_keys(kv_ref, lanes):
+def _pair_lanes(pair, width=0):
+    return pl.ds(width + 2 * pair * HD_K, 2 * HD_K)
+
+
+def _pair_keys(kv_ref, lanes):
     rows, cols, block = kv_ref.shape[:3]
-    return kv_ref[:, :, :, lanes].reshape(rows * cols * block, HD_K)
+    return kv_ref[:, :, :, lanes].reshape(rows * cols * block, 2 * HD_K)
+
+
+def _split_pair(block, low):
+    zero = jnp.zeros_like(block)
+    return jnp.where(low, block, zero), jnp.where(low, zero, block)
 
 
 def attn_fwd_kernel(tau_ref, q_ref, kv_ref, mask_ref, out_ref):
     width = q_ref.shape[3]
     mask = mask_ref[0]
-    for head in range(HEADS_K):
-        lanes = pl.ds(head * HD_K, HD_K)
-        value_lanes = pl.ds(width + head * HD_K, HD_K)
-        probs = _window_probs(tau_ref, head, q_ref[0, 0, :, lanes], _head_keys(kv_ref, lanes), mask)
-        out_ref[0, 0, :, lanes] = jnp.dot(
-            probs.astype(jnp.bfloat16),
-            _head_keys(kv_ref, value_lanes),
-            preferred_element_type=jnp.float32,
-        )
+    for pair in range(HEADS_K // 2):
+        lanes, value_lanes = _pair_lanes(pair), _pair_lanes(pair, width)
+        query = q_ref[0, 0, :, lanes]
+        low = lax.broadcasted_iota(jnp.int32, query.shape, 1) < HD_K
+        keys = _pair_keys(kv_ref, lanes)
+        values = _pair_keys(kv_ref, value_lanes)
+        mixed = []
+        for half, part in enumerate(_split_pair(query, low)):
+            probs = _window_probs(tau_ref[2 * pair + half], part, keys, mask)
+            mixed.append(
+                jnp.dot(probs.astype(jnp.bfloat16), values, preferred_element_type=jnp.float32)
+            )
+        out_ref[0, 0, :, lanes] = jnp.where(low, mixed[0], mixed[1])
 
 
 def attn_bwd_kernel(tau_ref, q_ref, kv_ref, g_ref, mask_ref, dq_ref, dkv_ref):
     width = q_ref.shape[3]
     mask = mask_ref[0]
-    for head in range(HEADS_K):
-        lanes = pl.ds(head * HD_K, HD_K)
-        value_lanes = pl.ds(width + head * HD_K, HD_K)
+    for pair in range(HEADS_K // 2):
+        lanes, value_lanes = _pair_lanes(pair), _pair_lanes(pair, width)
         query = q_ref[0, 0, :, lanes]
         grad = g_ref[0, 0, :, lanes]
-        keys = _head_keys(kv_ref, lanes)
-        probs = _window_probs(tau_ref, head, query, keys, mask)
-        dprob = _nt(grad, _head_keys(kv_ref, value_lanes))
-        total = jnp.sum(probs * dprob, axis=-1, keepdims=True)
-        dscore = (tau_ref[head] * (probs * (dprob - total))).astype(jnp.bfloat16)
-        dq_ref[0, 0, :, lanes] = jnp.dot(dscore, keys, preferred_element_type=jnp.float32)
-        dkv_ref[:, :, :, lanes] = _tn(dscore, query).reshape(dkv_ref.shape[:3] + (HD_K,))
-        dkv_ref[:, :, :, value_lanes] = _tn(probs.astype(jnp.bfloat16), grad).reshape(
-            dkv_ref.shape[:3] + (HD_K,)
-        )
+        low = lax.broadcasted_iota(jnp.int32, query.shape, 1) < HD_K
+        keys = _pair_keys(kv_ref, lanes)
+        values = _pair_keys(kv_ref, value_lanes)
+        queries = _split_pair(query, low)
+        grads = _split_pair(grad, low)
+        dq, dk, dv = [], [], []
+        for half in range(2):
+            tau = tau_ref[2 * pair + half]
+            probs = _window_probs(tau, queries[half], keys, mask)
+            dprob = _nt(grads[half], values)
+            total = jnp.sum(probs * dprob, axis=-1, keepdims=True)
+            dscore = (tau * (probs * (dprob - total))).astype(jnp.bfloat16)
+            dq.append(jnp.dot(dscore, keys, preferred_element_type=jnp.float32))
+            dk.append(_tn(dscore, query))
+            dv.append(_tn(probs.astype(jnp.bfloat16), grad))
+        dq_ref[0, 0, :, lanes] = jnp.where(low, dq[0], dq[1])
+        key_low = lax.broadcasted_iota(jnp.int32, keys.shape, 1) < HD_K
+        out_shape = dkv_ref.shape[:3] + (2 * HD_K,)
+        dkv_ref[:, :, :, lanes] = jnp.where(key_low, dk[0], dk[1]).reshape(out_shape)
+        dkv_ref[:, :, :, value_lanes] = jnp.where(key_low, dv[0], dv[1]).reshape(out_shape)
 
 
 def _window_of(i, j):

time: 229 us -> 226 us (0.987)
  Pallas kernels: 29.7 us -> 27.4 us
where the time goes in v5:
time: 226 us; the launch traced here: 225 us
  blocking collectives  66.4 us (29%)
  local copies, waits for them, and re-layouts  32.2 us (14%)
  waiting for transfers between devices  32.1 us (14%)
  starting transfers between devices  30.3 us (13%)
  Pallas kernels  27.4 us (12%)
  other arithmetic  26 us (12%)
  matrix products  9.34 us (4%)
    all_to_all x2, blocking collectives, sum_rows(): spread = lax.all_to_all(chunks, axis, 0, 0, tiled=False)  42.8 us
    all_to_all x1, blocking collectives, gather_rows(): spread = lax.all_to_all(copies, axis, 0, 0, tiled=False)  23.6 us
    pallas_call x1, Pallas kernels, window_bwd(): pl.pallas_call(attn_bwd_kernel, grid=(row_units, col_units), in_specs=[pl...  16.5 us
    pallas_call x1, Pallas kernels, window_fwd(): pl.pallas_call(attn_fwd_kernel, grid=(row_units, col_units), in_specs=[pl...  10.8 us
    ppermute x2, waiting for transfers between devices, from_behind(): return lax.ppermute(block, axis, route)  9.31 us
    all_to_all x1, waiting for transfers between devices, sum_everywhere(): spread = lax.all_to_all(copies, axis, 0, 0, tiled=False)  8.32 us
    ppermute x2, waiting for transfers between devices, with_halo(): after = lax.ppermute(initial, axis, down)  7.04 us
    ppermute x2, starting transfers between devices, with_halo(): after = lax.ppermute(initial, axis, down)  6.6 us
  transfers between devices with their start and end apart: 11, of which 8 were waited for; matrix products, arithmetic and copies ran while one was open for 13% of the time, Pallas kernels for 0%

profile of v5, /device:TPU:1, one launch (start us, length us, event | category | flops | bytes accessed | tf_op | source)
XLA Modules:
  0.0 225.0 jit_solution(10397143071499699583)
XLA Ops:
  2.3 23.6 %all_to_all.20 = bf16[8,64,1024]{2,1,0:T(8,128)(2,1)S(1)} all-to-all(bf16[8,64,1024]{2,1,0:T(8,128)(2,1)S(1)} %broadcast_in_dim.9), channel_id=1, replica_groups=mesh['lat'=32,'lon'=8] {'lon'}, dimensions={0} | all-to-all | bytes 2097152 | tf_op jit(solution)/shard_map/all_to_all | solution.py:169
  25.9 1.9 collective-permute-start
  34.7 4.5 %collective-permute-start.2 = (bf16[2,1,72,1024]{3,2,1,0:T(8,128)(2,1)}, bf16[2,1,72,1024]{3,2,1,0:T(8,128)(2,1)}, u32[]{:S(2)}, u32[]{:S(2)}) collective-permute-start(bf16[2,1,72,1024]{3,2,1,0:T(8,128)(2,1)} %get-tuple-element.69), channel_id=1, source_target_pairs={{1,0},{2,1},{3,2},{4,3},{5,4},{6,5},{7,6},{0,7},{9,8},{10,9},{11,1... | collective-permute-start | bytes 884744 | tf_op jit(solution)/shard_map/ppermute | solution.py:149
  39.3 1.1 copy.99
  42.1 4.2 %collective-permute-done.1 = bf16[2,1,72,1024]{3,2,1,0:T(8,128)(2,1)} collective-permute-done((bf16[2,1,72,1024]{3,2,1,0:T(8,128)(2,1)}, bf16[2,1,72,1024]{3,2,1,0:T(8,128)(2,1)}, u32[]{:S(2)}, u32[]{:S(2)}) %collective-permute-start.1) | collective-permute-done | bytes 294944 | tf_op jit(solution)/shard_map/ppermute | solution.py:148
  46.3 3.9 %collective-permute-done.2 = bf16[2,1,72,1024]{3,2,1,0:T(8,128)(2,1)} collective-permute-done((bf16[2,1,72,1024]{3,2,1,0:T(8,128)(2,1)}, bf16[2,1,72,1024]{3,2,1,0:T(8,128)(2,1)}, u32[]{:S(2)}, u32[]{:S(2)}) %collective-permute-start.2) | collective-permute-done | bytes 294944 | tf_op jit(solution)/shard_map/ppermute | solution.py:149
  50.2 1.2 pad_maximum_fusion
  51.5 1.1 fusion.45
  52.6 4.6 %collective-permute-start.3 = (bf16[1,4,72,1024]{3,2,1,0:T(8,128)(2,1)}, bf16[1,4,72,1024]{3,2,1,0:T(8,128)(2,1)}, u32[]{:S(2)}, u32[]{:S(2)}) collective-permute-start(bf16[1,4,72,1024]{3,2,1,0:T(8,128)(2,1)} %get-tuple-element.60), channel_id=1, source_target_pairs={{0,8},{8,16},{16,24},{24,32},{32,40},{40,48},{48,56},{56,64},{64,7... | collective-permute-start | bytes 1769480 | tf_op jit(solution)/shard_map/ppermute | solution.py:148
  57.2 2.1 collective-permute-start.4
  59.5 2.1 reshape.387
  61.6 2.1 copy.93
  63.7 1.9 multiply_convert_fusion.1.q_ref
  65.6 3.1 %collective-permute-done.4 = bf16[1,4,72,1024]{3,2,1,0:T(8,128)(2,1)} collective-permute-done((bf16[1,4,72,1024]{3,2,1,0:T(8,128)(2,1)}, bf16[1,4,72,1024]{3,2,1,0:T(8,128)(2,1)}, u32[]{:S(2)}, u32[]{:S(2)}) %collective-permute-start.4) | collective-permute-done | bytes 589856 | tf_op jit(solution)/shard_map/ppermute | solution.py:149
  68.7 2.9 %fusion.7.kv_ref = bf16[4,4,80,1024]{3,2,1,0:T(8,128)(2,1)} fusion(bf16[1,4,72,1024]{3,2,1,0:T(8,128)(2,1)} %collective-permute-done.4, bf16[1,4,72,1024]{3,2,1,0:T(8,128)(2,1)} %collective-permute-done.3, bf16[2,1,72,1024]{3,2,1,0:T(8,128)(2,1)} %collective-permute-done.2, bf16[2,1,72,1024]{3,2,1,0:T(8,128)(2,1)} %collective-permute-done.1, ...), kind=kLoop, calls=%fused_computation.12 | loop fusion | flops 24903680 | bytes 4980736 | tf_op jit(solution)/shard_map/concatenate | solution.py:150
  71.6 10.8 %shard_map.93 = f32[2,2,72,512]{3,2,1,0:T(8,128)} custom-call(f32[8]{0:T(128)} %tau_ref.3, bf16[2,2,72,512]{3,2,1,0:T(8,128)(2,1)} %multiply_convert_fusion.1.q_ref, bf16[4,4,80,1024]{3,2,1,0:T(8,128)(2,1)} %fusion.7.kv_ref, f32[2,72,320]{2,1,0:T(8,128)} %convert_element_type.114.mask_ref), custom_call_target="tpu_custom_call" | custom-call | tf_op jit(solution)/shard_map/pallas_call | solution.py:103
  82.4 1.1 convert_element_type.115
  83.6 1.5 fusion.47
  86.6 2.2 convolution_convert_fusion.3
  88.8 16.5 %shard_map.94 = (f32[2,2,72,512]{3,2,1,0:T(8,128)}, f32[4,4,80,1024]{3,2,1,0:T(8,128)}) custom-call(f32[8]{0:T(128)} %tau_ref.3, bf16[2,2,72,512]{3,2,1,0:T(8,128)(2,1)} %multiply_convert_fusion.1.q_ref, bf16[4,4,80,1024]{3,2,1,0:T(8,128)(2,1)} %fusion.7.kv_ref, bf16[2,2,72,512]{3,2,1,0:T(8,128)(2,1)} %bitcast.102, f32[2,72,320]{2,1,0:T(8,128)} %convert_element_type.114.mask_ref), custom_call_target="tpu_custom_call" | custom-call | tf_op jit(solution)/shard_map/pallas_call | solution.py:120
  105.4 2.9 %convert.35 = bf16[4,4,80,1024]{3,2,1,0:T(8,128)(2,1)S(1)} convert(f32[4,4,80,1024]{3,2,1,0:T(8,128)} %get-tuple-element.55) | non-fusion elementwise | flops 1310720 | bytes 7864320 | tf_op jit(solution)/shard_map/convert.19
  108.2 1.2 fusion.43
  109.4 1.9 collective-permute-start.5
  111.3 3.2 %collective-permute-start.6 = (bf16[1,4,72,1024]{3,2,1,0:T(8,128)(2,1)}, bf16[1,4,72,1024]{3,2,1,0:T(8,128)(2,1)}, u32[]{:S(2)}, u32[]{:S(2)}) collective-permute-start(bf16[1,4,72,1024]{3,2,1,0:T(8,128)(2,1)} %get-tuple-element.56), channel_id=1, source_target_pairs={{8,0},{16,8},{24,16},{32,24},{40,32},{48,40},{56,48},{64,56},{72,6... | collective-permute-start | bytes 1769480 | tf_op jit(solution)/shard_map/ppermute | solution.py:163
  114.6 1.1 copy.85
  115.6 1.8 slice.197
  118.4 2.4 %reshape.377 = f32[288,8,64]{2,1,0:T(8,128)} reshape(f32[2,2,72,512]{3,2,1,0:T(8,128)} %get-tuple-element.54) | data formatting | bytes 1179648 | tf_op jit(solution)/shard_map/reshape | solution.py:333
  120.8 2.6 %copy.83 = f32[288,8,64]{0,2,1:T(8,128)} copy(f32[288,8,64]{2,1,0:T(8,128)} %reshape.377) | data formatting | bytes 1179648 | tf_op jit(solution)/shard_map/reshape | solution.py:333
  123.4 2.2 convolution_convert_fusion.2
  125.6 1.6 add_dynamic-update-slice_fusion
  127.2 1.4 fusion.22
  130.7 4.5 %collective-permute-start.8 = (bf16[2,1,72,1024]{3,2,1,0:T(8,128)(2,1)}, bf16[2,1,72,1024]{3,2,1,0:T(8,128)(2,1)}, u32[]{:S(2)}, u32[]{:S(2)}) collective-permute-start(bf16[2,1,72,1024]{3,2,1,0:T(8,128)(2,1)} %get-tuple-element.58), channel_id=1, source_target_pairs={{1,0},{2,1},{3,2},{4,3},{5,4},{6,5},{7,6},{0,7},{9,8},{10,9},{11,1... | collective-permute-start | bytes 884744 | tf_op jit(solution)/shard_map/ppermute | solution.py:157
  135.2 1.1 copy.84
  136.4 5.9 %collective-permute-done.7 = bf16[2,1,72,1024]{3,2,1,0:T(8,128)(2,1)} collective-permute-done((bf16[2,1,72,1024]{3,2,1,0:T(8,128)(2,1)}, bf16[2,1,72,1024]{3,2,1,0:T(8,128)(2,1)}, u32[]{:S(2)}, u32[]{:S(2)}) %collective-permute-start.7) | collective-permute-done | bytes 294944 | tf_op jit(solution)/shard_map/ppermute | solution.py:157
  142.3 1.0 fusion.32
  143.4 3.4 %collective-permute-done.8 = bf16[2,1,72,1024]{3,2,1,0:T(8,128)(2,1)} collective-permute-done((bf16[2,1,72,1024]{3,2,1,0:T(8,128)(2,1)}, bf16[2,1,72,1024]{3,2,1,0:T(8,128)(2,1)}, u32[]{:S(2)}, u32[]{:S(2)}) %collective-permute-start.8) | collective-permute-done | bytes 294944 | tf_op jit(solution)/shard_map/ppermute | solution.py:157
  146.8 1.1 fusion.31
  148.6 1.9 convert_multiply_fusion.1
  150.5 1.4 copy.86
  152.1 1.1 copy.87
  153.2 2.1 fusion.34
  157.2 2.3 %collective-permute-done.9 = bf16[8,32,2048]{2,1,0:T(8,128)(2,1)S(1)} collective-permute-done((bf16[8,32,2048]{2,1,0:T(8,128)(2,1)S(1)}, bf16[8,32,2048]{2,1,0:T(8,128)(2,1)S(1)}, u32[]{:S(2)}, u32[]{:S(2)}) %collective-permute-start.9) | collective-permute-done | bytes 1048608 | tf_op jit(solution)/shard_map/ppermute | solution.py:190
  159.9 21.1 %all_to_all.21 = bf16[8,32,2048]{2,1,0:T(8,128)(2,1)S(1)} all-to-all(bf16[8,32,2048]{2,1,0:T(8,128)(2,1)S(1)} %fusion.12), channel_id=1, replica_groups=mesh['lat'=32,'lon'=8] {'lon'}, dimensions={0} | all-to-all | bytes 2097152 | tf_op jit(solution)/shard_map/all_to_all | solution.py:176
  182.0 21.7 %all_to_all.22 = bf16[32,2,2048]{2,1,0:T(2,128)(2,1)S(1)} all-to-all(bf16[32,2,2048]{2,1,0:T(2,128)(2,1)} %reshape.380), channel_id=1, replica_groups=mesh['lat'=32,'lon'=8] {'lat'}, dimensions={0} | all-to-all | bytes 524288 | tf_op jit(solution)/shard_map/all_to_all | solution.py:176
  204.8 5.7 %all-to-all-start.3 = ((bf16[32,2,2048]{2,1,0:T(2,128)(2,1)}), bf16[32,2,2048]{2,1,0:T(2,128)(2,1)}, u32[]{:S(2)}, u32[]{:S(2)}) async-start(bf16[32,2,2048]{2,1,0:T(2,128)(2,1)} %broadcast_in_dim.11), calls=%async_computation.3 | async-start | bytes 524288 | tf_op jit(solution)/shard_map/all_to_all | solution.py:184
  211.5 1.8 fusion.19
  214.3 8.3 %all-to-all-done.3 = bf16[32,2,2048]{2,1,0:T(2,128)(2,1)} async-done(((bf16[32,2,2048]{2,1,0:T(2,128)(2,1)}), bf16[32,2,2048]{2,1,0:T(2,128)(2,1)}, u32[]{:S(2)}, u32[]{:S(2)}) %all-to-all-start.3) | async-done | bytes 262176 | tf_op jit(solution)/shard_map/all_to_all | solution.py:184
  222.6 1.0 reshape.383
  (126 shorter events, 23.6 us)
Async XLA Ops:
  1.8 25.9 %copy-start.23 = (bf16[4,6,12,512]{3,0,2,1:T(4,128)(2,1)S(1)}, bf16[4,6,12,512]{3,0,2,1:T(4,128)(2,1)}, u32[]{:S(2)}) copy-start(bf16[4,6,12,512]{3,0,2,1:T(4,128)(2,1)} %param.14) | copy-start | bytes 884740
  2.2 25.8 %copy-start.18 = (bf16[4,6,12,512]{3,0,2,1:T(4,128)(2,1)S(1)}, bf16[4,6,12,512]{3,0,2,1:T(4,128)(2,1)}, u32[]{:S(2)}) copy-start(bf16[4,6,12,512]{3,0,2,1:T(4,128)(2,1)} %param.19) | copy-start | bytes 884740
  2.2 25.8 %copy-start.26 = (f32[512]{0:T(512)S(1)}, f32[512]{0:T(512)}, u32[]{:S(2)}) copy-start(f32[512]{0:T(512)} %param.17) | copy-start | bytes 6148
  25.9 4.2 %collective-permute-start = (bf16[512,1024]{1,0:T(8,128)(2,1)S(1)}, bf16[512,1024]{1,0:T(8,128)(2,1)S(1)}, u32[]{:S(2)}, u32[]{:S(2)}) collective-permute-start(bf16[512,1024]{1,0:T(8,128)(2,1)S(1)} %bitcast.87), channel_id=1, source_target_pairs={{0,8},{8,0},{16,24},{24,16},{32,40},{40,32},{48,56},{56,48},{64,72... | collective-permute-start | bytes 3145736 | tf_op jit(solution)/shard_map/ppermute | solution.py:190
  27.9 2.9 %copy-start.13 = (bf16[288,512]{1,0:T(8,128)(2,1)}, bf16[288,512]{1,0:T(8,128)(2,1)S(1)}, u32[]{:S(2)}) copy-start(bf16[288,512]{1,0:T(8,128)(2,1)S(1)} %reshape_reshape.10) | copy-start | bytes 884740
  30.8 1.4 copy-start.9
  32.2 0.9 copy-start.4
  33.2 8.6 %copy-start = (f32[288,512]{1,0:T(8,128)}, f32[288,512]{1,0:T(8,128)S(1)}, u32[]{:S(2)}) copy-start(f32[288,512]{1,0:T(8,128)S(1)} %copy.79) | copy-start | bytes 1769476
  33.2 7.5 %copy-start.19 = (f32[2,2,72,80]{3,1,2,0:T(2,128)S(1)}, f32[2,2,72,80]{3,1,2,0:T(2,128)}, u32[]{:S(2)}) copy-start(f32[2,2,72,80]{3,1,2,0:T(2,128)} %and_convert_fusion) | copy-start | bytes 276484
  33.3 8.6 %copy-start.6 = (bf16[288,512]{1,0:T(8,128)(2,1)}, bf16[288,512]{1,0:T(8,128)(2,1)S(1)}, u32[]{:S(2)}) copy-start(bf16[288,512]{1,0:T(8,128)(2,1)S(1)} %fusion.27) | copy-start | bytes 884740
  34.2 12.2 %collective-permute-start.1 = (bf16[2,1,72,1024]{3,2,1,0:T(8,128)(2,1)}, bf16[2,1,72,1024]{3,2,1,0:T(8,128)(2,1)}, u32[]{:S(2)}, u32[]{:S(2)}) collective-permute-start(bf16[2,1,72,1024]{3,2,1,0:T(8,128)(2,1)} %get-tuple-element.68), channel_id=1, source_target_pairs={{0,1},{1,2},{2,3},{3,4},{4,5},{5,6},{6,7},{7,0},{8,9},{9,10},{10,1... | collective-permute-start | bytes 884744 | tf_op jit(solution)/shard_map/ppermute | solution.py:148
  34.7 15.5 %collective-permute-start.2 = (bf16[2,1,72,1024]{3,2,1,0:T(8,128)(2,1)}, bf16[2,1,72,1024]{3,2,1,0:T(8,128)(2,1)}, u32[]{:S(2)}, u32[]{:S(2)}) collective-permute-start(bf16[2,1,72,1024]{3,2,1,0:T(8,128)(2,1)} %get-tuple-element.69), channel_id=1, source_target_pairs={{1,0},{2,1},{3,2},{4,3},{5,4},{6,5},{7,6},{0,7},{9,8},{10,9},{11,1... | collective-permute-start | bytes 884744 | tf_op jit(solution)/shard_map/ppermute | solution.py:149
  41.8 43.8 %copy-start.2 = (f32[288,512]{1,0:T(8,128)}, f32[288,512]{1,0:T(8,128)S(1)}, u32[]{:S(2)}) copy-start(f32[288,512]{1,0:T(8,128)S(1)} %reshape.381) | copy-start | bytes 1769476
  52.6 13.0 %collective-permute-start.3 = (bf16[1,4,72,1024]{3,2,1,0:T(8,128)(2,1)}, bf16[1,4,72,1024]{3,2,1,0:T(8,128)(2,1)}, u32[]{:S(2)}, u32[]{:S(2)}) collective-permute-start(bf16[1,4,72,1024]{3,2,1,0:T(8,128)(2,1)} %get-tuple-element.60), channel_id=1, source_target_pairs={{0,8},{8,16},{16,24},{24,32},{32,40},{40,48},{48,56},{56,64},{64,7... | collective-permute-start | bytes 1769480 | tf_op jit(solution)/shard_map/ppermute | solution.py:148
  57.2 11.5 %collective-permute-start.4 = (bf16[1,4,72,1024]{3,2,1,0:T(8,128)(2,1)}, bf16[1,4,72,1024]{3,2,1,0:T(8,128)(2,1)}, u32[]{:S(2)}, u32[]{:S(2)}) collective-permute-start(bf16[1,4,72,1024]{3,2,1,0:T(8,128)(2,1)} %get-tuple-element.61), channel_id=1, source_target_pairs={{8,0},{16,8},{24,16},{32,24},{40,32},{48,40},{56,48},{64,56},{72,6... | collective-permute-start | bytes 1769480 | tf_op jit(solution)/shard_map/ppermute | solution.py:149
  59.4 4.3 %copy-start.24 = (f32[288,8]{0,1:T(8,128)}, f32[288,8]{0,1:T(8,128)S(1)}, u32[]{:S(2)}) copy-start(f32[288,8]{0,1:T(8,128)S(1)} %multiply_reduce_fusion.1) | copy-start | bytes 27652
  59.5 9.2 %copy-start.7 = (bf16[288,512]{1,0:T(8,128)(2,1)S(1)}, bf16[288,512]{1,0:T(8,128)(2,1)}, u32[]{:S(2)}) copy-start(bf16[288,512]{1,0:T(8,128)(2,1)} %copy-done.6) | copy-start | bytes 884740
  82.4 3.2 %copy-start.14 = (bf16[288,512]{1,0:T(8,128)(2,1)S(1)}, bf16[288,512]{1,0:T(8,128)(2,1)}, u32[]{:S(2)}) copy-start(bf16[288,512]{1,0:T(8,128)(2,1)} %copy-done.13) | copy-start | bytes 884740
  86.6 18.7 %copy-start.17 = (bf16[288,512]{1,0:T(8,128)(2,1)}, bf16[288,512]{1,0:T(8,128)(2,1)S(1)}, u32[]{:S(2)}) copy-start(bf16[288,512]{1,0:T(8,128)(2,1)S(1)} %get-tuple-element.66) | copy-start | bytes 884740
  109.4 16.2 %collective-permute-start.5 = (bf16[1,4,72,1024]{3,2,1,0:T(8,128)(2,1)}, bf16[1,4,72,1024]{3,2,1,0:T(8,128)(2,1)}, u32[]{:S(2)}, u32[]{:S(2)}) collective-permute-start(bf16[1,4,72,1024]{3,2,1,0:T(8,128)(2,1)} %get-tuple-element.57), channel_id=1, source_target_pairs={{0,8},{8,16},{16,24},{24,32},{32,40},{40,48},{48,56},{56,64},{64,7... | collective-permute-start | bytes 1769480 | tf_op jit(solution)/shard_map/ppermute | solution.py:163
  111.3 15.9 %collective-permute-start.6 = (bf16[1,4,72,1024]{3,2,1,0:T(8,128)(2,1)}, bf16[1,4,72,1024]{3,2,1,0:T(8,128)(2,1)}, u32[]{:S(2)}, u32[]{:S(2)}) collective-permute-start(bf16[1,4,72,1024]{3,2,1,0:T(8,128)(2,1)} %get-tuple-element.56), channel_id=1, source_target_pairs={{8,0},{16,8},{24,16},{32,24},{40,32},{48,40},{56,48},{64,56},{72,6... | collective-permute-start | bytes 1769480 | tf_op jit(solution)/shard_map/ppermute | solution.py:163
  118.4 5.0 %copy-start.12 = (bf16[512,288]{1,0:T(8,128)(2,1)S(1)}, bf16[512,288]{1,0:T(8,128)(2,1)}, u32[]{:S(2)}) copy-start(bf16[512,288]{1,0:T(8,128)(2,1)} %copy.90) | copy-start | bytes 884740
  128.6 2.0 copy-start.11
  128.8 6.4 %copy-start.25 = (f32[288,8]{0,1:T(8,128)S(1)}, f32[288,8]{0,1:T(8,128)}, u32[]{:S(2)}) copy-start(f32[288,8]{0,1:T(8,128)} %copy-done.24) | copy-start | bytes 27652
  129.7 12.7 %collective-permute-start.7 = (bf16[2,1,72,1024]{3,2,1,0:T(8,128)(2,1)}, bf16[2,1,72,1024]{3,2,1,0:T(8,128)(2,1)}, u32[]{:S(2)}, u32[]{:S(2)}) collective-permute-start(bf16[2,1,72,1024]{3,2,1,0:T(8,128)(2,1)} %get-tuple-element.59), channel_id=1, source_target_pairs={{7,0},{0,1},{1,2},{2,3},{3,4},{4,5},{5,6},{6,7},{15,8},{8,9},{9,10... | collective-permute-start | bytes 884744 | tf_op jit(solution)/shard_map/ppermute | solution.py:157
  130.7 16.1 %collective-permute-start.8 = (bf16[2,1,72,1024]{3,2,1,0:T(8,128)(2,1)}, bf16[2,1,72,1024]{3,2,1,0:T(8,128)(2,1)}, u32[]{:S(2)}, u32[]{:S(2)}) collective-permute-start(bf16[2,1,72,1024]{3,2,1,0:T(8,128)(2,1)} %get-tuple-element.58), channel_id=1, source_target_pairs={{1,0},{2,1},{3,2},{4,3},{5,4},{6,5},{7,6},{0,7},{9,8},{10,9},{11,1... | collective-permute-start | bytes 884744 | tf_op jit(solution)/shard_map/ppermute | solution.py:157
  150.5 2.7 %copy-start.1 = (f32[288,512]{1,0:T(8,128)S(1)}, f32[288,512]{1,0:T(8,128)}, u32[]{:S(2)}) copy-start(f32[288,512]{1,0:T(8,128)} %copy-done) | copy-start | bytes 1769476
  150.5 2.7 %copy-start.5 = (bf16[288,1536]{1,0:T(8,128)(2,1)S(1)}, bf16[288,1536]{1,0:T(8,128)(2,1)}, u32[]{:S(2)}) copy-start(bf16[288,1536]{1,0:T(8,128)(2,1)} %copy-done.4) | copy-start | bytes 2654212
  153.2 2.2 copy-start.15
  153.2 2.2 copy-start.22
  155.4 1.1 copy-start.20
  155.4 1.1 copy-start.21
  155.4 1.2 copy-start.8
  156.7 2.8 %collective-permute-start.9 = (bf16[8,32,2048]{2,1,0:T(8,128)(2,1)S(1)}, bf16[8,32,2048]{2,1,0:T(8,128)(2,1)S(1)}, u32[]{:S(2)}, u32[]{:S(2)}) collective-permute-start(bf16[8,32,2048]{2,1,0:T(8,128)(2,1)S(1)} %fusion.24), channel_id=1, source_target_pairs={{0,8},{8,0},{16,24},{24,16},{32,40},{40,32},{48,56},{56,48},{64,72... | collective-permute-start | bytes 3145736 | tf_op jit(solution)/shard_map/ppermute | solution.py:190
  180.9 29.6 %copy-start.16 = (bf16[288,512]{1,0:T(8,128)(2,1)S(1)}, bf16[288,512]{1,0:T(8,128)(2,1)}, u32[]{:S(2)}) copy-start(bf16[288,512]{1,0:T(8,128)(2,1)} %get-tuple-element.67) | copy-start | bytes 884740
  181.1 30.4 %copy-start.3 = (f32[288,512]{1,0:T(8,128)S(1)}, f32[288,512]{1,0:T(8,128)}, u32[]{:S(2)}) copy-start(f32[288,512]{1,0:T(8,128)} %copy-done.2) | copy-start | bytes 1769476
  181.1 30.4 %copy-start.10 = (bf16[512,2048]{1,0:T(8,128)(2,1)S(1)}, bf16[512,2048]{1,0:T(8,128)(2,1)}, u32[]{:S(2)}) copy-start(bf16[512,2048]{1,0:T(8,128)(2,1)} %copy-done.9) | copy-start | bytes 6291460
  204.8 17.8 %all-to-all-start.3 = ((bf16[32,2,2048]{2,1,0:T(2,128)(2,1)}), bf16[32,2,2048]{2,1,0:T(2,128)(2,1)}, u32[]{:S(2)}, u32[]{:S(2)}) async-start(bf16[32,2,2048]{2,1,0:T(2,128)(2,1)} %broadcast_in_dim.11), calls=%async_computation.3 | async-start | bytes 524288 | tf_op jit(solution)/shard_map/all_to_all | solution.py:184

commit v6 on v5

--- a/solution.py
+++ b/solution.py
@@ -210,13 +210,25 @@
     keep = lax.dynamic_index_in_dim(blocks, core, axis=1, keepdims=False)
     give = lax.dynamic_index_in_dim(blocks, 1 - core, axis=1, keepdims=False)
     pair = keep.astype(jnp.float32) + chip_partner(give).astype(jnp.float32)
-    own = sum_rows(pair.astype(jnp.bfloat16).reshape(-1, partial.shape[1]), axis)
-    own = own.astype(jnp.bfloat16)
-    empty = jnp.zeros_like(own)
+    return sum_rows(pair.astype(jnp.bfloat16).reshape(-1, partial.shape[1]), axis)
+
+
+def sum_lat_paired(own):
+    peers = lax.axis_size("lat")
+    total = own
+    bit = 2
+    while bit < peers:
+        sent = total.astype(jnp.bfloat16)
+        got = lax.ppermute(sent, "lat", [(i, i ^ bit) for i in range(peers)])
+        total = sent.astype(jnp.float32) + got.astype(jnp.float32)
+        bit *= 2
+    final = total.astype(jnp.bfloat16)
+    other = chip_partner(final)
+    core = lax.axis_index("lat") % 2
     return jnp.where(
         core == 0,
-        jnp.concatenate([own, empty], axis=0),
-        jnp.concatenate([empty, own], axis=0),
+        jnp.concatenate([final, other], axis=0),
+        jnp.concatenate([other, final], axis=0),
     )
 
 
@@ -356,7 +368,7 @@
         [cross_rows(tok_flat, grad_proj), cross_rows(attended, grad_y)], axis=1
     ).astype(jnp.bfloat16)
     shard_sum = sum_rows_paired(partial, "lon")
-    summed = sum_everywhere(shard_sum, "lat").astype(jnp.float32)
+    summed = sum_lat_paired(shard_sum).astype(jnp.float32)
     grad_qkv = summed[:, : 3 * model_width]
     grad_out = summed[:, 3 * model_width :]
     unit_shape = (row_units, col_units, query_count, model_width)

time: 226 us -> 217 us (0.960)
  blocking collectives: 66.4 us -> 44.8 us
  starting transfers between devices: 30.3 us -> 39.5 us
  waiting for transfers between devices: 32.1 us -> 37.6 us
  local copies, waits for them, and re-layouts: 32.2 us -> 29.4 us
    all_to_all x2 -> x1, blocking collectives: 42.8 us -> 21.2 us  [sum_rows(): spread = lax.all_to_all(chunks, axis, 0, 0, tiled=False)]
    ppermute x0 -> x4, waiting for transfers between devices: none -> 13.9 us  [sum_lat_paired(): got = lax.ppermute(sent, 'lat', [(i, i ^ bit) for i in range(peers)])]
    ppermute x0 -> x4, starting transfers between devices: none -> 10 us  [sum_lat_paired(): got = lax.ppermute(sent, 'lat', [(i, i ^ bit) for i in range(peers)])]
    all_to_all x1 -> x0, waiting for transfers between devices: 8.32 us -> none  [sum_everywhere(): spread = lax.all_to_all(copies, axis, 0, 0, tiled=False)]
    all_to_all x1 -> x0, starting transfers between devices: 5.67 us -> none  [sum_everywhere(): spread = lax.all_to_all(copies, axis, 0, 0, tiled=False)]
    ppermute x2 -> x3, starting transfers between devices: 2.35 us -> 7.1 us  [chip_partner(): return lax.ppermute(block, 'lat', [(i, i ^ 1) for i in range(peers)])]
  transfers between devices with their start and end apart: 11 -> 15, of which waited for: 8 -> 11; matrix products, arithmetic and copies ran while one was open for 13% -> 13% of each run, Pallas kernels for 0% -> 0%
where the time goes in v6:
time: 217 us; the launch traced here: 216 us
  blocking collectives  44.8 us (21%)
  starting transfers between devices  39.5 us (18%)
  waiting for transfers between devices  37.6 us (17%)
  local copies, waits for them, and re-layouts  29.4 us (14%)
  Pallas kernels  27.4 us (13%)
  other arithmetic  26.9 us (12%)
  matrix products  9.33 us (4%)
    all_to_all x1, blocking collectives, gather_rows(): spread = lax.all_to_all(copies, axis, 0, 0, tiled=False)  23.6 us
    all_to_all x1, blocking collectives, sum_rows(): spread = lax.all_to_all(chunks, axis, 0, 0, tiled=False)  21.2 us
    pallas_call x1, Pallas kernels, window_bwd(): pl.pallas_call(attn_bwd_kernel, grid=(row_units, col_units), in_specs=[pl...  16.5 us
    ppermute x4, waiting for transfers between devices, sum_lat_paired(): got = lax.ppermute(sent, 'lat', [(i, i ^ bit) for i in range(peers)])  13.9 us
    pallas_call x1, Pallas kernels, window_fwd(): pl.pallas_call(attn_fwd_kernel, grid=(row_units, col_units), in_specs=[pl...  10.8 us
    ppermute x4, starting transfers between devices, sum_lat_paired(): got = lax.ppermute(sent, 'lat', [(i, i ^ bit) for i in range(peers)])  10 us
    ppermute x2, waiting for transfers between devices, from_behind(): return lax.ppermute(block, axis, route)  9.27 us
    ppermute x3, starting transfers between devices, chip_partner(): return lax.ppermute(block, 'lat', [(i, i ^ 1) for i in range(peers)])  7.1 us
  transfers between devices with their start and end apart: 15, of which 11 were waited for; matrix products, arithmetic and copies ran while one was open for 13% of the time, Pallas kernels for 0%

profile of v6, /device:TPU:1, one launch (start us, length us, event | category | flops | bytes accessed | tf_op | source)
XLA Modules:
  0.0 216.2 jit_solution(16757330945742082721)
XLA Ops:
  2.3 23.6 %all_to_all.10 = bf16[8,64,1024]{2,1,0:T(8,128)(2,1)S(1)} all-to-all(bf16[8,64,1024]{2,1,0:T(8,128)(2,1)S(1)} %broadcast_in_dim.7), channel_id=1, replica_groups=mesh['lat'=32,'lon'=8] {'lon'}, dimensions={0} | all-to-all | bytes 2097152 | tf_op jit(solution)/shard_map/all_to_all | solution.py:169
  25.9 1.9 collective-permute-start
  34.7 4.5 %collective-permute-start.2 = (bf16[2,1,72,1024]{3,2,1,0:T(8,128)(2,1)}, bf16[2,1,72,1024]{3,2,1,0:T(8,128)(2,1)}, u32[]{:S(2)}, u32[]{:S(2)}) collective-permute-start(bf16[2,1,72,1024]{3,2,1,0:T(8,128)(2,1)} %get-tuple-element.69), channel_id=1, source_target_pairs={{1,0},{2,1},{3,2},{4,3},{5,4},{6,5},{7,6},{0,7},{9,8},{10,9},{11,1... | collective-permute-start | bytes 884744 | tf_op jit(solution)/shard_map/ppermute | solution.py:149
  42.1 4.2 %collective-permute-done.1 = bf16[2,1,72,1024]{3,2,1,0:T(8,128)(2,1)} collective-permute-done((bf16[2,1,72,1024]{3,2,1,0:T(8,128)(2,1)}, bf16[2,1,72,1024]{3,2,1,0:T(8,128)(2,1)}, u32[]{:S(2)}, u32[]{:S(2)}) %collective-permute-start.1) | collective-permute-done | bytes 294944 | tf_op jit(solution)/shard_map/ppermute | solution.py:148
  46.3 3.9 %collective-permute-done.2 = bf16[2,1,72,1024]{3,2,1,0:T(8,128)(2,1)} collective-permute-done((bf16[2,1,72,1024]{3,2,1,0:T(8,128)(2,1)}, bf16[2,1,72,1024]{3,2,1,0:T(8,128)(2,1)}, u32[]{:S(2)}, u32[]{:S(2)}) %collective-permute-start.2) | collective-permute-done | bytes 294944 | tf_op jit(solution)/shard_map/ppermute | solution.py:149
  50.2 1.2 pad_maximum_fusion
  51.4 1.1 fusion.46
  52.5 4.6 %collective-permute-start.3 = (bf16[1,4,72,1024]{3,2,1,0:T(8,128)(2,1)}, bf16[1,4,72,1024]{3,2,1,0:T(8,128)(2,1)}, u32[]{:S(2)}, u32[]{:S(2)}) collective-permute-start(bf16[1,4,72,1024]{3,2,1,0:T(8,128)(2,1)} %get-tuple-element.60), channel_id=1, source_target_pairs={{0,8},{8,16},{16,24},{24,32},{32,40},{40,48},{48,56},{56,64},{64,7... | collective-permute-start | bytes 1769480 | tf_op jit(solution)/shard_map/ppermute | solution.py:148
  57.2 2.1 collective-permute-start.4
  59.5 2.1 reshape.378
  61.6 2.1 copy.60
  63.7 1.9 multiply_convert_fusion.1.q_ref
  65.5 3.1 %collective-permute-done.4 = bf16[1,4,72,1024]{3,2,1,0:T(8,128)(2,1)} collective-permute-done((bf16[1,4,72,1024]{3,2,1,0:T(8,128)(2,1)}, bf16[1,4,72,1024]{3,2,1,0:T(8,128)(2,1)}, u32[]{:S(2)}, u32[]{:S(2)}) %collective-permute-start.4) | collective-permute-done | bytes 589856 | tf_op jit(solution)/shard_map/ppermute | solution.py:149
  68.7 2.9 %fusion.7.kv_ref = bf16[4,4,80,1024]{3,2,1,0:T(8,128)(2,1)} fusion(bf16[1,4,72,1024]{3,2,1,0:T(8,128)(2,1)} %collective-permute-done.4, bf16[1,4,72,1024]{3,2,1,0:T(8,128)(2,1)} %collective-permute-done.3, bf16[2,1,72,1024]{3,2,1,0:T(8,128)(2,1)} %collective-permute-done.2, bf16[2,1,72,1024]{3,2,1,0:T(8,128)(2,1)} %collective-permute-done.1, ...), kind=kLoop, calls=%fused_computation.12 | loop fusion | flops 24903680 | bytes 4980736 | tf_op jit(solution)/shard_map/concatenate | solution.py:150
  71.6 10.8 %shard_map.93 = f32[2,2,72,512]{3,2,1,0:T(8,128)} custom-call(f32[8]{0:T(128)} %tau_ref.3, bf16[2,2,72,512]{3,2,1,0:T(8,128)(2,1)} %multiply_convert_fusion.1.q_ref, bf16[4,4,80,1024]{3,2,1,0:T(8,128)(2,1)} %fusion.7.kv_ref, f32[2,72,320]{2,1,0:T(8,128)} %convert_element_type.145.mask_ref), custom_call_target="tpu_custom_call" | custom-call | tf_op jit(solution)/shard_map/pallas_call | solution.py:103
  82.4 1.1 convert_element_type.146
  83.6 1.5 fusion.48
  86.6 2.2 %convolution_convert_fusion.3 = bf16[288,512]{1,0:T(8,128)(2,1)} fusion(bf16[288,512]{1,0:T(8,128)(2,1)S(1)} %get-tuple-element.66, bf16[512,2048]{1,0:T(8,128)(2,1)} %copy-done.9), kind=kOutput, calls=%fused_computation.27 | convolution fusion | flops 151142400 | bytes 1114112 | tf_op jit(solution)/shard_map/dot_general | solution.py:340
  88.8 16.5 %shard_map.94 = (f32[2,2,72,512]{3,2,1,0:T(8,128)}, f32[4,4,80,1024]{3,2,1,0:T(8,128)}) custom-call(f32[8]{0:T(128)} %tau_ref.3, bf16[2,2,72,512]{3,2,1,0:T(8,128)(2,1)} %multiply_convert_fusion.1.q_ref, bf16[4,4,80,1024]{3,2,1,0:T(8,128)(2,1)} %fusion.7.kv_ref, bf16[2,2,72,512]{3,2,1,0:T(8,128)(2,1)} %bitcast.102, f32[2,72,320]{2,1,0:T(8,128)} %convert_element_type.145.mask_ref), custom_call_target="tpu_custom_call" | custom-call | tf_op jit(solution)/shard_map/pallas_call | solution.py:120
  105.3 2.9 %convert.33 = bf16[4,4,80,1024]{3,2,1,0:T(8,128)(2,1)S(1)} convert(f32[4,4,80,1024]{3,2,1,0:T(8,128)} %get-tuple-element.55) | non-fusion elementwise | flops 1310720 | bytes 7864320 | tf_op jit(solution)/shard_map/convert.17
  108.2 1.2 fusion.44
  109.4 1.9 collective-permute-start.5
  111.3 3.2 %collective-permute-start.6 = (bf16[1,4,72,1024]{3,2,1,0:T(8,128)(2,1)}, bf16[1,4,72,1024]{3,2,1,0:T(8,128)(2,1)}, u32[]{:S(2)}, u32[]{:S(2)}) collective-permute-start(bf16[1,4,72,1024]{3,2,1,0:T(8,128)(2,1)} %get-tuple-element.56), channel_id=1, source_target_pairs={{8,0},{16,8},{24,16},{32,24},{40,32},{48,40},{56,48},{64,56},{72,6... | collective-permute-start | bytes 1769480 | tf_op jit(solution)/shard_map/ppermute | solution.py:163
  114.5 1.1 copy.53
  115.6 1.8 slice.197
  118.4 2.4 %reshape.370 = f32[288,8,64]{2,1,0:T(8,128)} reshape(f32[2,2,72,512]{3,2,1,0:T(8,128)} %get-tuple-element.54) | data formatting | bytes 1179648 | tf_op jit(solution)/shard_map/reshape | solution.py:345
  120.8 2.6 %copy.51 = f32[288,8,64]{0,2,1:T(8,128)} copy(f32[288,8,64]{2,1,0:T(8,128)} %reshape.370) | data formatting | bytes 1179648 | tf_op jit(solution)/shard_map/reshape | solution.py:345
  123.4 2.2 %convolution_convert_fusion.2 = bf16[8,2,32,512]{3,2,1,0:T(8,128)(2,1)} fusion(bf16[8,2,32,288]{3,2,1,0:T(8,128)(2,1)S(1)} %bitcast.95, bf16[288,512]{1,0:T(8,128)(2,1)} %copy-done.17), kind=kOutput, calls=%fused_computation.25 | convolution fusion | flops 151257088 | bytes 1114112 | tf_op jit(solution)/shard_map/dot_general | solution.py:282
  125.6 1.6 add_dynamic-update-slice_fusion
  127.2 1.4 fusion.22
  130.7 4.5 %collective-permute-start.8 = (bf16[2,1,72,1024]{3,2,1,0:T(8,128)(2,1)}, bf16[2,1,72,1024]{3,2,1,0:T(8,128)(2,1)}, u32[]{:S(2)}, u32[]{:S(2)}) collective-permute-start(bf16[2,1,72,1024]{3,2,1,0:T(8,128)(2,1)} %get-tuple-element.58), channel_id=1, source_target_pairs={{1,0},{2,1},{3,2},{4,3},{5,4},{6,5},{7,6},{0,7},{9,8},{10,9},{11,1... | collective-permute-start | bytes 884744 | tf_op jit(solution)/shard_map/ppermute | solution.py:157
  136.4 5.9 %collective-permute-done.7 = bf16[2,1,72,1024]{3,2,1,0:T(8,128)(2,1)} collective-permute-done((bf16[2,1,72,1024]{3,2,1,0:T(8,128)(2,1)}, bf16[2,1,72,1024]{3,2,1,0:T(8,128)(2,1)}, u32[]{:S(2)}, u32[]{:S(2)}) %collective-permute-start.7) | collective-permute-done | bytes 294944 | tf_op jit(solution)/shard_map/ppermute | solution.py:157
  143.3 3.4 %collective-permute-done.8 = bf16[2,1,72,1024]{3,2,1,0:T(8,128)(2,1)} collective-permute-done((bf16[2,1,72,1024]{3,2,1,0:T(8,128)(2,1)}, bf16[2,1,72,1024]{3,2,1,0:T(8,128)(2,1)}, u32[]{:S(2)}, u32[]{:S(2)}) %collective-permute-start.8) | collective-permute-done | bytes 294944 | tf_op jit(solution)/shard_map/ppermute | solution.py:157
  146.7 1.1 fusion.31
  148.6 1.9 convert_multiply_fusion.1
  150.5 1.4 copy.54
  153.2 2.1 fusion.34
  157.2 2.3 %collective-permute-done.9 = bf16[8,32,2048]{2,1,0:T(8,128)(2,1)S(1)} collective-permute-done((bf16[8,32,2048]{2,1,0:T(8,128)(2,1)S(1)}, bf16[8,32,2048]{2,1,0:T(8,128)(2,1)S(1)}, u32[]{:S(2)}, u32[]{:S(2)}) %collective-permute-start.9) | collective-permute-done | bytes 1048608 | tf_op jit(solution)/shard_map/ppermute | solution.py:190
  159.8 21.2 %all_to_all.11 = bf16[8,32,2048]{2,1,0:T(8,128)(2,1)S(1)} all-to-all(bf16[8,32,2048]{2,1,0:T(8,128)(2,1)S(1)} %fusion.12), channel_id=1, replica_groups=mesh['lat'=32,'lon'=8] {'lon'}, dimensions={0} | all-to-all | bytes 2097152 | tf_op jit(solution)/shard_map/all_to_all | solution.py:176
  181.2 1.2 collective-permute-start.10
  182.4 2.7 %collective-permute-done.10 = bf16[32,2048]{1,0:T(8,128)(2,1)S(1)} collective-permute-done((bf16[32,2048]{1,0:T(8,128)(2,1)S(1)}, bf16[32,2048]{1,0:T(8,128)(2,1)S(1)}, u32[]{:S(2)}, u32[]{:S(2)}) %collective-permute-start.10) | collective-permute-done | bytes 131104 | tf_op jit(solution)/shard_map/ppermute | solution.py:222
  185.1 5.2 %collective-permute-start.11 = (bf16[32,2048]{1,0:T(8,128)(2,1)S(1)}, bf16[32,2048]{1,0:T(8,128)(2,1)S(1)}, u32[]{:S(2)}, u32[]{:S(2)}) collective-permute-start(bf16[32,2048]{1,0:T(8,128)(2,1)S(1)} %add_convert_fusion.4), channel_id=1, source_target_pairs={{0,32},{8,40},{16,48},{24,56},{32,0},{40,8},{48,16},{56,24},{64,96... | collective-permute-start | bytes 393224 | tf_op jit(solution)/shard_map/ppermute | solution.py:222
  190.3 3.8 %collective-permute-done.11 = bf16[32,2048]{1,0:T(8,128)(2,1)S(1)} collective-permute-done((bf16[32,2048]{1,0:T(8,128)(2,1)S(1)}, bf16[32,2048]{1,0:T(8,128)(2,1)S(1)}, u32[]{:S(2)}, u32[]{:S(2)}) %collective-permute-start.11) | collective-permute-done | bytes 131104 | tf_op jit(solution)/shard_map/ppermute | solution.py:222
  194.1 3.2 %collective-permute-start.12 = (bf16[32,2048]{1,0:T(8,128)(2,1)S(1)}, bf16[32,2048]{1,0:T(8,128)(2,1)S(1)}, u32[]{:S(2)}, u32[]{:S(2)}) collective-permute-start(bf16[32,2048]{1,0:T(8,128)(2,1)S(1)} %add_convert_fusion.3), channel_id=1, source_target_pairs={{0,64},{8,72},{16,80},{24,88},{32,96},{40,104},{48,112},{56,120},{... | collective-permute-start | bytes 393224 | tf_op jit(solution)/shard_map/ppermute | solution.py:222
  197.4 4.8 %collective-permute-done.12 = bf16[32,2048]{1,0:T(8,128)(2,1)S(1)} collective-permute-done((bf16[32,2048]{1,0:T(8,128)(2,1)S(1)}, bf16[32,2048]{1,0:T(8,128)(2,1)S(1)}, u32[]{:S(2)}, u32[]{:S(2)}) %collective-permute-start.12) | collective-permute-done | bytes 131104 | tf_op jit(solution)/shard_map/ppermute | solution.py:222
  203.6 2.6 %collective-permute-done.13 = bf16[32,2048]{1,0:T(8,128)(2,1)} collective-permute-done((bf16[32,2048]{1,0:T(8,128)(2,1)S(1)}, bf16[32,2048]{1,0:T(8,128)(2,1)}, u32[]{:S(2)}, u32[]{:S(2)}) %collective-permute-start.13) | collective-permute-done | bytes 131104 | tf_op jit(solution)/shard_map/ppermute | solution.py:222
  207.2 4.8 %collective-permute-start.14 = (bf16[32,2048]{1,0:T(8,128)(2,1)S(1)}, bf16[32,2048]{1,0:T(8,128)(2,1)S(1)}, u32[]{:S(2)}, u32[]{:S(2)}) collective-permute-start(bf16[32,2048]{1,0:T(8,128)(2,1)S(1)} %add_convert_fusion.1), channel_id=1, source_target_pairs={{0,8},{8,0},{16,24},{24,16},{32,40},{40,32},{48,56},{56,48},{64,72... | collective-permute-start | bytes 393224 | tf_op jit(solution)/shard_map/ppermute | solution.py:190
  211.9 1.8 fusion.19
  (133 shorter events, 27.3 us)
Async XLA Ops:
  1.8 25.9 %copy-start.23 = (bf16[4,6,12,512]{3,0,2,1:T(4,128)(2,1)S(1)}, bf16[4,6,12,512]{3,0,2,1:T(4,128)(2,1)}, u32[]{:S(2)}) copy-start(bf16[4,6,12,512]{3,0,2,1:T(4,128)(2,1)} %param.14) | copy-start | bytes 884740
  2.2 25.8 %copy-start.18 = (bf16[4,6,12,512]{3,0,2,1:T(4,128)(2,1)S(1)}, bf16[4,6,12,512]{3,0,2,1:T(4,128)(2,1)}, u32[]{:S(2)}) copy-start(bf16[4,6,12,512]{3,0,2,1:T(4,128)(2,1)} %param.19) | copy-start | bytes 884740
  2.2 25.8 %copy-start.26 = (f32[512]{0:T(512)S(1)}, f32[512]{0:T(512)}, u32[]{:S(2)}) copy-start(f32[512]{0:T(512)} %param.17) | copy-start | bytes 6148
  25.9 4.2 %collective-permute-start = (bf16[512,1024]{1,0:T(8,128)(2,1)S(1)}, bf16[512,1024]{1,0:T(8,128)(2,1)S(1)}, u32[]{:S(2)}, u32[]{:S(2)}) collective-permute-start(bf16[512,1024]{1,0:T(8,128)(2,1)S(1)} %bitcast.87), channel_id=1, source_target_pairs={{0,8},{8,0},{16,24},{24,16},{32,40},{40,32},{48,56},{56,48},{64,72... | collective-permute-start | bytes 3145736 | tf_op jit(solution)/shard_map/ppermute | solution.py:190
  27.9 2.9 %copy-start.13 = (bf16[288,512]{1,0:T(8,128)(2,1)}, bf16[288,512]{1,0:T(8,128)(2,1)S(1)}, u32[]{:S(2)}) copy-start(bf16[288,512]{1,0:T(8,128)(2,1)S(1)} %reshape_reshape.10) | copy-start | bytes 884740
  30.8 1.4 copy-start.9
  32.2 0.9 copy-start.4
  33.1 8.6 %copy-start = (f32[288,512]{1,0:T(8,128)}, f32[288,512]{1,0:T(8,128)S(1)}, u32[]{:S(2)}) copy-start(f32[288,512]{1,0:T(8,128)S(1)} %copy.47) | copy-start | bytes 1769476
  33.1 7.5 %copy-start.19 = (f32[2,2,72,80]{3,1,2,0:T(2,128)S(1)}, f32[2,2,72,80]{3,1,2,0:T(2,128)}, u32[]{:S(2)}) copy-start(f32[2,2,72,80]{3,1,2,0:T(2,128)} %and_convert_fusion) | copy-start | bytes 276484
  33.2 8.6 %copy-start.6 = (bf16[288,512]{1,0:T(8,128)(2,1)}, bf16[288,512]{1,0:T(8,128)(2,1)S(1)}, u32[]{:S(2)}) copy-start(bf16[288,512]{1,0:T(8,128)(2,1)S(1)} %fusion.27) | copy-start | bytes 884740
  34.1 12.2 %collective-permute-start.1 = (bf16[2,1,72,1024]{3,2,1,0:T(8,128)(2,1)}, bf16[2,1,72,1024]{3,2,1,0:T(8,128)(2,1)}, u32[]{:S(2)}, u32[]{:S(2)}) collective-permute-start(bf16[2,1,72,1024]{3,2,1,0:T(8,128)(2,1)} %get-tuple-element.68), channel_id=1, source_target_pairs={{0,1},{1,2},{2,3},{3,4},{4,5},{5,6},{6,7},{7,0},{8,9},{9,10},{10,1... | collective-permute-start | bytes 884744 | tf_op jit(solution)/shard_map/ppermute | solution.py:148
  34.7 15.5 %collective-permute-start.2 = (bf16[2,1,72,1024]{3,2,1,0:T(8,128)(2,1)}, bf16[2,1,72,1024]{3,2,1,0:T(8,128)(2,1)}, u32[]{:S(2)}, u32[]{:S(2)}) collective-permute-start(bf16[2,1,72,1024]{3,2,1,0:T(8,128)(2,1)} %get-tuple-element.69), channel_id=1, source_target_pairs={{1,0},{2,1},{3,2},{4,3},{5,4},{6,5},{7,6},{0,7},{9,8},{10,9},{11,1... | collective-permute-start | bytes 884744 | tf_op jit(solution)/shard_map/ppermute | solution.py:149
  41.8 43.8 %copy-start.2 = (f32[288,512]{1,0:T(8,128)}, f32[288,512]{1,0:T(8,128)S(1)}, u32[]{:S(2)}) copy-start(f32[288,512]{1,0:T(8,128)S(1)} %reshape.373) | copy-start | bytes 1769476
  52.5 13.0 %collective-permute-start.3 = (bf16[1,4,72,1024]{3,2,1,0:T(8,128)(2,1)}, bf16[1,4,72,1024]{3,2,1,0:T(8,128)(2,1)}, u32[]{:S(2)}, u32[]{:S(2)}) collective-permute-start(bf16[1,4,72,1024]{3,2,1,0:T(8,128)(2,1)} %get-tuple-element.60), channel_id=1, source_target_pairs={{0,8},{8,16},{16,24},{24,32},{32,40},{40,48},{48,56},{56,64},{64,7... | collective-permute-start | bytes 1769480 | tf_op jit(solution)/shard_map/ppermute | solution.py:148
  57.2 11.5 %collective-permute-start.4 = (bf16[1,4,72,1024]{3,2,1,0:T(8,128)(2,1)}, bf16[1,4,72,1024]{3,2,1,0:T(8,128)(2,1)}, u32[]{:S(2)}, u32[]{:S(2)}) collective-permute-start(bf16[1,4,72,1024]{3,2,1,0:T(8,128)(2,1)} %get-tuple-element.61), channel_id=1, source_target_pairs={{8,0},{16,8},{24,16},{32,24},{40,32},{48,40},{56,48},{64,56},{72,6... | collective-permute-start | bytes 1769480 | tf_op jit(solution)/shard_map/ppermute | solution.py:149
  59.4 4.3 %copy-start.24 = (f32[288,8]{0,1:T(8,128)}, f32[288,8]{0,1:T(8,128)S(1)}, u32[]{:S(2)}) copy-start(f32[288,8]{0,1:T(8,128)S(1)} %multiply_reduce_fusion.1) | copy-start | bytes 27652
  59.5 9.2 %copy-start.7 = (bf16[288,512]{1,0:T(8,128)(2,1)S(1)}, bf16[288,512]{1,0:T(8,128)(2,1)}, u32[]{:S(2)}) copy-start(bf16[288,512]{1,0:T(8,128)(2,1)} %copy-done.6) | copy-start | bytes 884740
  82.4 3.2 %copy-start.14 = (bf16[288,512]{1,0:T(8,128)(2,1)S(1)}, bf16[288,512]{1,0:T(8,128)(2,1)}, u32[]{:S(2)}) copy-start(bf16[288,512]{1,0:T(8,128)(2,1)} %copy-done.13) | copy-start | bytes 884740
  86.6 18.8 %copy-start.17 = (bf16[288,512]{1,0:T(8,128)(2,1)}, bf16[288,512]{1,0:T(8,128)(2,1)S(1)}, u32[]{:S(2)}) copy-start(bf16[288,512]{1,0:T(8,128)(2,1)S(1)} %get-tuple-element.66) | copy-start | bytes 884740
  109.4 16.2 %collective-permute-start.5 = (bf16[1,4,72,1024]{3,2,1,0:T(8,128)(2,1)}, bf16[1,4,72,1024]{3,2,1,0:T(8,128)(2,1)}, u32[]{:S(2)}, u32[]{:S(2)}) collective-permute-start(bf16[1,4,72,1024]{3,2,1,0:T(8,128)(2,1)} %get-tuple-element.57), channel_id=1, source_target_pairs={{0,8},{8,16},{16,24},{24,32},{32,40},{40,48},{48,56},{56,64},{64,7... | collective-permute-start | bytes 1769480 | tf_op jit(solution)/shard_map/ppermute | solution.py:163
  111.3 15.9 %collective-permute-start.6 = (bf16[1,4,72,1024]{3,2,1,0:T(8,128)(2,1)}, bf16[1,4,72,1024]{3,2,1,0:T(8,128)(2,1)}, u32[]{:S(2)}, u32[]{:S(2)}) collective-permute-start(bf16[1,4,72,1024]{3,2,1,0:T(8,128)(2,1)} %get-tuple-element.56), channel_id=1, source_target_pairs={{8,0},{16,8},{24,16},{32,24},{40,32},{48,40},{56,48},{64,56},{72,6... | collective-permute-start | bytes 1769480 | tf_op jit(solution)/shard_map/ppermute | solution.py:163
  118.4 5.0 %copy-start.12 = (bf16[512,288]{1,0:T(8,128)(2,1)S(1)}, bf16[512,288]{1,0:T(8,128)(2,1)}, u32[]{:S(2)}) copy-start(bf16[512,288]{1,0:T(8,128)(2,1)} %copy.58) | copy-start | bytes 884740
  128.6 2.0 copy-start.11
  128.8 6.4 %copy-start.25 = (f32[288,8]{0,1:T(8,128)S(1)}, f32[288,8]{0,1:T(8,128)}, u32[]{:S(2)}) copy-start(f32[288,8]{0,1:T(8,128)} %copy-done.24) | copy-start | bytes 27652
  129.6 12.7 %collective-permute-start.7 = (bf16[2,1,72,1024]{3,2,1,0:T(8,128)(2,1)}, bf16[2,1,72,1024]{3,2,1,0:T(8,128)(2,1)}, u32[]{:S(2)}, u32[]{:S(2)}) collective-permute-start(bf16[2,1,72,1024]{3,2,1,0:T(8,128)(2,1)} %get-tuple-element.59), channel_id=1, source_target_pairs={{7,0},{0,1},{1,2},{2,3},{3,4},{4,5},{5,6},{6,7},{15,8},{8,9},{9,10... | collective-permute-start | bytes 884744 | tf_op jit(solution)/shard_map/ppermute | solution.py:157
  130.7 16.1 %collective-permute-start.8 = (bf16[2,1,72,1024]{3,2,1,0:T(8,128)(2,1)}, bf16[2,1,72,1024]{3,2,1,0:T(8,128)(2,1)}, u32[]{:S(2)}, u32[]{:S(2)}) collective-permute-start(bf16[2,1,72,1024]{3,2,1,0:T(8,128)(2,1)} %get-tuple-element.58), channel_id=1, source_target_pairs={{1,0},{2,1},{3,2},{4,3},{5,4},{6,5},{7,6},{0,7},{9,8},{10,9},{11,1... | collective-permute-start | bytes 884744 | tf_op jit(solution)/shard_map/ppermute | solution.py:157
  150.5 2.7 %copy-start.1 = (f32[288,512]{1,0:T(8,128)S(1)}, f32[288,512]{1,0:T(8,128)}, u32[]{:S(2)}) copy-start(f32[288,512]{1,0:T(8,128)} %copy-done) | copy-start | bytes 1769476
  150.5 2.7 %copy-start.5 = (bf16[288,1536]{1,0:T(8,128)(2,1)S(1)}, bf16[288,1536]{1,0:T(8,128)(2,1)}, u32[]{:S(2)}) copy-start(bf16[288,1536]{1,0:T(8,128)(2,1)} %copy-done.4) | copy-start | bytes 2654212
  153.2 2.2 %copy-start.15 = (bf16[288,512]{1,0:T(8,128)(2,1)S(1)}, bf16[288,512]{1,0:T(8,128)(2,1)}, u32[]{:S(2)}) copy-start(bf16[288,512]{1,0:T(8,128)(2,1)} %copy-done.13) | copy-start | bytes 884740
  153.2 2.2 %copy-start.22 = (bf16[288,512]{1,0:T(8,128)(2,1)S(1)}, bf16[288,512]{1,0:T(8,128)(2,1)}, u32[]{:S(2)}) copy-start(bf16[288,512]{1,0:T(8,128)(2,1)} %slice.270) | copy-start | bytes 884740
  155.3 1.1 copy-start.20
  155.3 1.1 copy-start.21
  155.4 1.2 copy-start.8
  156.7 2.8 %collective-permute-start.9 = (bf16[8,32,2048]{2,1,0:T(8,128)(2,1)S(1)}, bf16[8,32,2048]{2,1,0:T(8,128)(2,1)S(1)}, u32[]{:S(2)}, u32[]{:S(2)}) collective-permute-start(bf16[8,32,2048]{2,1,0:T(8,128)(2,1)S(1)} %fusion.24), channel_id=1, source_target_pairs={{0,8},{8,0},{16,24},{24,16},{32,40},{40,32},{48,56},{56,48},{64,72... | collective-permute-start | bytes 3145736 | tf_op jit(solution)/shard_map/ppermute | solution.py:190
  159.8 42.8 %copy-start.16 = (bf16[288,512]{1,0:T(8,128)(2,1)S(1)}, bf16[288,512]{1,0:T(8,128)(2,1)}, u32[]{:S(2)}) copy-start(bf16[288,512]{1,0:T(8,128)(2,1)} %get-tuple-element.67) | copy-start | bytes 884740
  181.0 30.9 %copy-start.3 = (f32[288,512]{1,0:T(8,128)S(1)}, f32[288,512]{1,0:T(8,128)}, u32[]{:S(2)}) copy-start(f32[288,512]{1,0:T(8,128)} %copy-done.2) | copy-start | bytes 1769476
  181.2 30.7 %copy-start.10 = (bf16[512,2048]{1,0:T(8,128)(2,1)S(1)}, bf16[512,2048]{1,0:T(8,128)(2,1)}, u32[]{:S(2)}) copy-start(bf16[512,2048]{1,0:T(8,128)(2,1)} %copy-done.9) | copy-start | bytes 6291460
  181.2 3.9 %collective-permute-start.10 = (bf16[32,2048]{1,0:T(8,128)(2,1)S(1)}, bf16[32,2048]{1,0:T(8,128)(2,1)S(1)}, u32[]{:S(2)}, u32[]{:S(2)}) collective-permute-start(bf16[32,2048]{1,0:T(8,128)(2,1)S(1)} %reduce_sum.92), channel_id=1, source_target_pairs={{0,16},{8,24},{16,0},{24,8},{32,48},{40,56},{48,32},{56,40},{64,80... | collective-permute-start | bytes 393224 | tf_op jit(solution)/shard_map/ppermute | solution.py:222
  185.1 8.9 %collective-permute-start.11 = (bf16[32,2048]{1,0:T(8,128)(2,1)S(1)}, bf16[32,2048]{1,0:T(8,128)(2,1)S(1)}, u32[]{:S(2)}, u32[]{:S(2)}) collective-permute-start(bf16[32,2048]{1,0:T(8,128)(2,1)S(1)} %add_convert_fusion.4), channel_id=1, source_target_pairs={{0,32},{8,40},{16,48},{24,56},{32,0},{40,8},{48,16},{56,24},{64,96... | collective-permute-start | bytes 393224 | tf_op jit(solution)/shard_map/ppermute | solution.py:222
  194.1 8.0 %collective-permute-start.12 = (bf16[32,2048]{1,0:T(8,128)(2,1)S(1)}, bf16[32,2048]{1,0:T(8,128)(2,1)S(1)}, u32[]{:S(2)}, u32[]{:S(2)}) collective-permute-start(bf16[32,2048]{1,0:T(8,128)(2,1)S(1)} %add_convert_fusion.3), channel_id=1, source_target_pairs={{0,64},{8,72},{16,80},{24,88},{32,96},{40,104},{48,112},{56,120},{... | collective-permute-start | bytes 393224 | tf_op jit(solution)/shard_map/ppermute | solution.py:222
  202.2 4.0 %collective-permute-start.13 = (bf16[32,2048]{1,0:T(8,128)(2,1)S(1)}, bf16[32,2048]{1,0:T(8,128)(2,1)}, u32[]{:S(2)}, u32[]{:S(2)}) collective-permute-start(bf16[32,2048]{1,0:T(8,128)(2,1)S(1)} %add_convert_fusion.2), channel_id=1, source_target_pairs={{0,128},{8,136},{16,144},{24,152},{32,160},{40,168},{48,176},{56,1... | collective-permute-start | bytes 393224 | tf_op jit(solution)/shard_map/ppermute | solution.py:222
  207.2 7.5 %collective-permute-start.14 = (bf16[32,2048]{1,0:T(8,128)(2,1)S(1)}, bf16[32,2048]{1,0:T(8,128)(2,1)S(1)}, u32[]{:S(2)}, u32[]{:S(2)}) collective-permute-start(bf16[32,2048]{1,0:T(8,128)(2,1)S(1)} %add_convert_fusion.1), channel_id=1, source_target_pairs={{0,8},{8,0},{16,24},{24,16},{32,40},{40,32},{48,56},{56,48},{64,72... | collective-permute-start | bytes 393224 | tf_op jit(solution)/shard_map/ppermute | solution.py:190

commit v7 on v6

--- a/solution.py
+++ b/solution.py
@@ -61,7 +61,7 @@
             mixed.append(
                 jnp.dot(probs.astype(jnp.bfloat16), values, preferred_element_type=jnp.float32)
             )
-        out_ref[0, 0, :, lanes] = jnp.where(low, mixed[0], mixed[1])
+        out_ref[0, 0, :, lanes] = jnp.where(low, mixed[0], mixed[1]).astype(out_ref.dtype)
 
 
 def attn_bwd_kernel(tau_ref, q_ref, kv_ref, g_ref, mask_ref, dq_ref, dkv_ref):
@@ -110,7 +110,7 @@
             pl.BlockSpec((1, queries, mask.shape[2]), lambda i, j: ((i + 1) // 2, 0, 0)),
         ],
         out_specs=pl.BlockSpec((1, 1, queries, width), lambda i, j: (i, j, 0, 0)),
-        out_shape=jax.ShapeDtypeStruct(query.shape, jnp.float32),
+        out_shape=jax.ShapeDtypeStruct(query.shape, jnp.bfloat16),
     )(tau, query, ext_kv, mask)
 
 
@@ -332,7 +332,7 @@
     allowed = allowed.transpose(0, 3, 1, 2, 4).reshape(-1, query_count, 4 * block)
     allowed = allowed.astype(jnp.float32)
     mixed = window_fwd(tau, query_u, ext_kv, allowed)
-    attended = mixed.astype(jnp.bfloat16).reshape(tok_count, model_width)
+    attended = mixed.reshape(tok_count, model_width)
     y_rows = jnp.dot(attended, w_out_all, preferred_element_type=jnp.float32)
     normed, inverse = norm_forward(y_rows)
     output = (tok_flat.astype(jnp.float32) + gain * normed).astype(jnp.bfloat16)

time: 217 us -> 216 us (level)
  transfers between devices with their start and end apart: 15 -> 15, of which waited for: 11 -> 11; matrix products, arithmetic and copies ran while one was open for 13% -> 14% of each run, Pallas kernels for 0% -> 0%
where the time goes in v7:
time: 216 us; the launch traced here: 215 us
  blocking collectives  44.8 us (21%)
  starting transfers between devices  39.5 us (18%)
  waiting for transfers between devices  37.6 us (17%)
  local copies, waits for them, and re-layouts  29.5 us (14%)
  Pallas kernels  27.4 us (13%)
  other arithmetic  25.7 us (12%)
  matrix products  9.45 us (4%)
    all_to_all x1, blocking collectives, gather_rows(): spread = lax.all_to_all(copies, axis, 0, 0, tiled=False)  23.6 us
    all_to_all x1, blocking collectives, sum_rows(): spread = lax.all_to_all(chunks, axis, 0, 0, tiled=False)  21.2 us
    pallas_call x1, Pallas kernels, window_bwd(): pl.pallas_call(attn_bwd_kernel, grid=(row_units, col_units), in_specs=[pl...  16.6 us
    ppermute x4, waiting for transfers between devices, sum_lat_paired(): got = lax.ppermute(sent, 'lat', [(i, i ^ bit) for i in range(peers)])  13.9 us
    pallas_call x1, Pallas kernels, window_fwd(): pl.pallas_call(attn_fwd_kernel, grid=(row_units, col_units), in_specs=[pl...  10.8 us
    ppermute x4, starting transfers between devices, sum_lat_paired(): got = lax.ppermute(sent, 'lat', [(i, i ^ bit) for i in range(peers)])  10.1 us
    ppermute x2, waiting for transfers between devices, from_behind(): return lax.ppermute(block, axis, route)  9.27 us
    ppermute x3, starting transfers between devices, chip_partner(): return lax.ppermute(block, 'lat', [(i, i ^ 1) for i in range(peers)])  7.1 us
  transfers between devices with their start and end apart: 15, of which 11 were waited for; matrix products, arithmetic and copies ran while one was open for 14% of the time, Pallas kernels for 0%

profile of v7, /device:TPU:1, one launch (start us, length us, event | category | flops | bytes accessed | tf_op | source)
XLA Modules:
  0.0 215.2 jit_solution(15298724478264661888)
XLA Ops:
  2.3 23.6 %all_to_all.10 = bf16[8,64,1024]{2,1,0:T(8,128)(2,1)S(1)} all-to-all(bf16[8,64,1024]{2,1,0:T(8,128)(2,1)S(1)} %broadcast_in_dim.7), channel_id=1, replica_groups=mesh['lat'=32,'lon'=8] {'lon'}, dimensions={0} | all-to-all | bytes 2097152 | tf_op jit(solution)/shard_map/all_to_all | solution.py:169
  25.9 1.9 collective-permute-start
  34.7 4.5 %collective-permute-start.2 = (bf16[2,1,72,1024]{3,2,1,0:T(8,128)(2,1)}, bf16[2,1,72,1024]{3,2,1,0:T(8,128)(2,1)}, u32[]{:S(2)}, u32[]{:S(2)}) collective-permute-start(bf16[2,1,72,1024]{3,2,1,0:T(8,128)(2,1)} %get-tuple-element.69), channel_id=1, source_target_pairs={{1,0},{2,1},{3,2},{4,3},{5,4},{6,5},{7,6},{0,7},{9,8},{10,9},{11,1... | collective-permute-start | bytes 884744 | tf_op jit(solution)/shard_map/ppermute | solution.py:149
  42.0 4.2 %collective-permute-done.1 = bf16[2,1,72,1024]{3,2,1,0:T(8,128)(2,1)} collective-permute-done((bf16[2,1,72,1024]{3,2,1,0:T(8,128)(2,1)}, bf16[2,1,72,1024]{3,2,1,0:T(8,128)(2,1)}, u32[]{:S(2)}, u32[]{:S(2)}) %collective-permute-start.1) | collective-permute-done | bytes 294944 | tf_op jit(solution)/shard_map/ppermute | solution.py:148
  46.3 3.9 %collective-permute-done.2 = bf16[2,1,72,1024]{3,2,1,0:T(8,128)(2,1)} collective-permute-done((bf16[2,1,72,1024]{3,2,1,0:T(8,128)(2,1)}, bf16[2,1,72,1024]{3,2,1,0:T(8,128)(2,1)}, u32[]{:S(2)}, u32[]{:S(2)}) %collective-permute-start.2) | collective-permute-done | bytes 294944 | tf_op jit(solution)/shard_map/ppermute | solution.py:149
  50.2 1.2 pad_maximum_fusion
  51.4 1.1 fusion.46
  52.5 4.6 %collective-permute-start.3 = (bf16[1,4,72,1024]{3,2,1,0:T(8,128)(2,1)}, bf16[1,4,72,1024]{3,2,1,0:T(8,128)(2,1)}, u32[]{:S(2)}, u32[]{:S(2)}) collective-permute-start(bf16[1,4,72,1024]{3,2,1,0:T(8,128)(2,1)} %get-tuple-element.60), channel_id=1, source_target_pairs={{0,8},{8,16},{16,24},{24,32},{32,40},{40,48},{48,56},{56,64},{64,7... | collective-permute-start | bytes 1769480 | tf_op jit(solution)/shard_map/ppermute | solution.py:148
  57.2 2.1 collective-permute-start.4
  59.5 2.1 reshape.378
  61.6 2.1 copy.60
  63.7 1.9 multiply_convert_fusion.1.q_ref
  65.6 3.1 %collective-permute-done.4 = bf16[1,4,72,1024]{3,2,1,0:T(8,128)(2,1)} collective-permute-done((bf16[1,4,72,1024]{3,2,1,0:T(8,128)(2,1)}, bf16[1,4,72,1024]{3,2,1,0:T(8,128)(2,1)}, u32[]{:S(2)}, u32[]{:S(2)}) %collective-permute-start.4) | collective-permute-done | bytes 589856 | tf_op jit(solution)/shard_map/ppermute | solution.py:149
  68.7 2.9 %fusion.7.kv_ref = bf16[4,4,80,1024]{3,2,1,0:T(8,128)(2,1)} fusion(bf16[1,4,72,1024]{3,2,1,0:T(8,128)(2,1)} %collective-permute-done.4, bf16[1,4,72,1024]{3,2,1,0:T(8,128)(2,1)} %collective-permute-done.3, bf16[2,1,72,1024]{3,2,1,0:T(8,128)(2,1)} %collective-permute-done.2, bf16[2,1,72,1024]{3,2,1,0:T(8,128)(2,1)} %collective-permute-done.1, ...), kind=kLoop, calls=%fused_computation.12 | loop fusion | flops 24903680 | bytes 4980736 | tf_op jit(solution)/shard_map/concatenate | solution.py:150
  71.6 10.8 %shard_map.93 = bf16[2,2,72,512]{3,2,1,0:T(8,128)(2,1)} custom-call(f32[8]{0:T(128)} %tau_ref.3, bf16[2,2,72,512]{3,2,1,0:T(8,128)(2,1)} %multiply_convert_fusion.1.q_ref, bf16[4,4,80,1024]{3,2,1,0:T(8,128)(2,1)} %fusion.7.kv_ref, f32[2,72,320]{2,1,0:T(8,128)} %convert_element_type.142.mask_ref), custom_call_target="tpu_custom_call" | custom-call | tf_op jit(solution)/shard_map/pallas_call | solution.py:103
  82.4 1.6 fusion.48
  85.5 2.2 %convolution_convert_fusion.3 = bf16[288,512]{1,0:T(8,128)(2,1)} fusion(bf16[288,512]{1,0:T(8,128)(2,1)S(1)} %get-tuple-element.66, bf16[512,2048]{1,0:T(8,128)(2,1)} %copy-done.9), kind=kOutput, calls=%fused_computation.27 | convolution fusion | flops 151142400 | bytes 1114112 | tf_op jit(solution)/shard_map/dot_general | solution.py:340
  87.7 16.6 %shard_map.94 = (f32[2,2,72,512]{3,2,1,0:T(8,128)}, f32[4,4,80,1024]{3,2,1,0:T(8,128)}) custom-call(f32[8]{0:T(128)} %tau_ref.3, bf16[2,2,72,512]{3,2,1,0:T(8,128)(2,1)} %multiply_convert_fusion.1.q_ref, bf16[4,4,80,1024]{3,2,1,0:T(8,128)(2,1)} %fusion.7.kv_ref, bf16[2,2,72,512]{3,2,1,0:T(8,128)(2,1)} %bitcast.102, f32[2,72,320]{2,1,0:T(8,128)} %convert_element_type.142.mask_ref), custom_call_target="tpu_custom_call" | custom-call | tf_op jit(solution)/shard_map/pallas_call | solution.py:120
  104.3 2.9 %convert.33 = bf16[4,4,80,1024]{3,2,1,0:T(8,128)(2,1)S(1)} convert(f32[4,4,80,1024]{3,2,1,0:T(8,128)} %get-tuple-element.55) | non-fusion elementwise | flops 1310720 | bytes 7864320 | tf_op jit(solution)/shard_map/convert.17
  107.2 1.2 fusion.44
  108.4 1.9 collective-permute-start.5
  110.3 3.2 %collective-permute-start.6 = (bf16[1,4,72,1024]{3,2,1,0:T(8,128)(2,1)}, bf16[1,4,72,1024]{3,2,1,0:T(8,128)(2,1)}, u32[]{:S(2)}, u32[]{:S(2)}) collective-permute-start(bf16[1,4,72,1024]{3,2,1,0:T(8,128)(2,1)} %get-tuple-element.56), channel_id=1, source_target_pairs={{8,0},{16,8},{24,16},{32,24},{40,32},{48,40},{56,48},{64,56},{72,6... | collective-permute-start | bytes 1769480 | tf_op jit(solution)/shard_map/ppermute | solution.py:163
  114.6 1.9 slice.197
  117.4 2.4 %reshape.370 = f32[288,8,64]{2,1,0:T(8,128)} reshape(f32[2,2,72,512]{3,2,1,0:T(8,128)} %get-tuple-element.54) | data formatting | bytes 1179648 | tf_op jit(solution)/shard_map/reshape | solution.py:345
  119.8 2.6 %copy.51 = f32[288,8,64]{0,2,1:T(8,128)} copy(f32[288,8,64]{2,1,0:T(8,128)} %reshape.370) | data formatting | bytes 1179648 | tf_op jit(solution)/shard_map/reshape | solution.py:345
  122.4 2.2 %convolution_convert_fusion.2 = bf16[8,2,32,512]{3,2,1,0:T(8,128)(2,1)} fusion(bf16[8,2,32,288]{3,2,1,0:T(8,128)(2,1)S(1)} %bitcast.95, bf16[288,512]{1,0:T(8,128)(2,1)} %copy-done.18), kind=kOutput, calls=%fused_computation.25 | convolution fusion | flops 151257088 | bytes 1114112 | tf_op jit(solution)/shard_map/dot_general | solution.py:282
  124.6 1.6 add_dynamic-update-slice_fusion
  126.2 1.4 fusion.22
  129.7 4.5 %collective-permute-start.8 = (bf16[2,1,72,1024]{3,2,1,0:T(8,128)(2,1)}, bf16[2,1,72,1024]{3,2,1,0:T(8,128)(2,1)}, u32[]{:S(2)}, u32[]{:S(2)}) collective-permute-start(bf16[2,1,72,1024]{3,2,1,0:T(8,128)(2,1)} %get-tuple-element.58), channel_id=1, source_target_pairs={{1,0},{2,1},{3,2},{4,3},{5,4},{6,5},{7,6},{0,7},{9,8},{10,9},{11,1... | collective-permute-start | bytes 884744 | tf_op jit(solution)/shard_map/ppermute | solution.py:157
  134.2 1.1 copy.52
  135.4 5.9 %collective-permute-done.7 = bf16[2,1,72,1024]{3,2,1,0:T(8,128)(2,1)} collective-permute-done((bf16[2,1,72,1024]{3,2,1,0:T(8,128)(2,1)}, bf16[2,1,72,1024]{3,2,1,0:T(8,128)(2,1)}, u32[]{:S(2)}, u32[]{:S(2)}) %collective-permute-start.7) | collective-permute-done | bytes 294944 | tf_op jit(solution)/shard_map/ppermute | solution.py:157
  142.3 3.4 %collective-permute-done.8 = bf16[2,1,72,1024]{3,2,1,0:T(8,128)(2,1)} collective-permute-done((bf16[2,1,72,1024]{3,2,1,0:T(8,128)(2,1)}, bf16[2,1,72,1024]{3,2,1,0:T(8,128)(2,1)}, u32[]{:S(2)}, u32[]{:S(2)}) %collective-permute-start.8) | collective-permute-done | bytes 294944 | tf_op jit(solution)/shard_map/ppermute | solution.py:157
  145.7 1.1 fusion.31
  147.6 1.9 convert_multiply_fusion.1
  149.5 1.4 copy.54
  151.1 1.1 copy.55
  152.2 2.1 fusion.34
  156.2 2.3 %collective-permute-done.9 = bf16[8,32,2048]{2,1,0:T(8,128)(2,1)S(1)} collective-permute-done((bf16[8,32,2048]{2,1,0:T(8,128)(2,1)S(1)}, bf16[8,32,2048]{2,1,0:T(8,128)(2,1)S(1)}, u32[]{:S(2)}, u32[]{:S(2)}) %collective-permute-start.9) | collective-permute-done | bytes 1048608 | tf_op jit(solution)/shard_map/ppermute | solution.py:190
  158.8 21.2 %all_to_all.11 = bf16[8,32,2048]{2,1,0:T(8,128)(2,1)S(1)} all-to-all(bf16[8,32,2048]{2,1,0:T(8,128)(2,1)S(1)} %fusion.12), channel_id=1, replica_groups=mesh['lat'=32,'lon'=8] {'lon'}, dimensions={0} | all-to-all | bytes 2097152 | tf_op jit(solution)/shard_map/all_to_all | solution.py:176
  180.2 1.2 collective-permute-start.10
  181.4 2.7 %collective-permute-done.10 = bf16[32,2048]{1,0:T(8,128)(2,1)S(1)} collective-permute-done((bf16[32,2048]{1,0:T(8,128)(2,1)S(1)}, bf16[32,2048]{1,0:T(8,128)(2,1)S(1)}, u32[]{:S(2)}, u32[]{:S(2)}) %collective-permute-start.10) | collective-permute-done | bytes 131104 | tf_op jit(solution)/shard_map/ppermute | solution.py:222
  184.1 5.2 %collective-permute-start.11 = (bf16[32,2048]{1,0:T(8,128)(2,1)S(1)}, bf16[32,2048]{1,0:T(8,128)(2,1)S(1)}, u32[]{:S(2)}, u32[]{:S(2)}) collective-permute-start(bf16[32,2048]{1,0:T(8,128)(2,1)S(1)} %add_convert_fusion.4), channel_id=1, source_target_pairs={{0,32},{8,40},{16,48},{24,56},{32,0},{40,8},{48,16},{56,24},{64,96... | collective-permute-start | bytes 393224 | tf_op jit(solution)/shard_map/ppermute | solution.py:222
  189.3 3.8 %collective-permute-done.11 = bf16[32,2048]{1,0:T(8,128)(2,1)S(1)} collective-permute-done((bf16[32,2048]{1,0:T(8,128)(2,1)S(1)}, bf16[32,2048]{1,0:T(8,128)(2,1)S(1)}, u32[]{:S(2)}, u32[]{:S(2)}) %collective-permute-start.11) | collective-permute-done | bytes 131104 | tf_op jit(solution)/shard_map/ppermute | solution.py:222
  193.1 3.2 %collective-permute-start.12 = (bf16[32,2048]{1,0:T(8,128)(2,1)S(1)}, bf16[32,2048]{1,0:T(8,128)(2,1)S(1)}, u32[]{:S(2)}, u32[]{:S(2)}) collective-permute-start(bf16[32,2048]{1,0:T(8,128)(2,1)S(1)} %add_convert_fusion.3), channel_id=1, source_target_pairs={{0,64},{8,72},{16,80},{24,88},{32,96},{40,104},{48,112},{56,120},{... | collective-permute-start | bytes 393224 | tf_op jit(solution)/shard_map/ppermute | solution.py:222
  196.3 4.8 %collective-permute-done.12 = bf16[32,2048]{1,0:T(8,128)(2,1)S(1)} collective-permute-done((bf16[32,2048]{1,0:T(8,128)(2,1)S(1)}, bf16[32,2048]{1,0:T(8,128)(2,1)S(1)}, u32[]{:S(2)}, u32[]{:S(2)}) %collective-permute-start.12) | collective-permute-done | bytes 131104 | tf_op jit(solution)/shard_map/ppermute | solution.py:222
  202.6 2.6 %collective-permute-done.13 = bf16[32,2048]{1,0:T(8,128)(2,1)} collective-permute-done((bf16[32,2048]{1,0:T(8,128)(2,1)S(1)}, bf16[32,2048]{1,0:T(8,128)(2,1)}, u32[]{:S(2)}, u32[]{:S(2)}) %collective-permute-start.13) | collective-permute-done | bytes 131104 | tf_op jit(solution)/shard_map/ppermute | solution.py:222
  206.2 4.8 %collective-permute-start.14 = (bf16[32,2048]{1,0:T(8,128)(2,1)S(1)}, bf16[32,2048]{1,0:T(8,128)(2,1)S(1)}, u32[]{:S(2)}, u32[]{:S(2)}) collective-permute-start(bf16[32,2048]{1,0:T(8,128)(2,1)S(1)} %add_convert_fusion.1), channel_id=1, source_target_pairs={{0,8},{8,0},{16,24},{24,16},{32,40},{40,32},{48,56},{56,48},{64,72... | collective-permute-start | bytes 393224 | tf_op jit(solution)/shard_map/ppermute | solution.py:190
  210.9 1.8 fusion.19
  (134 shorter events, 26.2 us)
Async XLA Ops:
  1.8 25.9 %copy-start.24 = (bf16[4,6,12,512]{3,0,2,1:T(4,128)(2,1)S(1)}, bf16[4,6,12,512]{3,0,2,1:T(4,128)(2,1)}, u32[]{:S(2)}) copy-start(bf16[4,6,12,512]{3,0,2,1:T(4,128)(2,1)} %param.14) | copy-start | bytes 884740
  2.2 25.8 %copy-start.19 = (bf16[4,6,12,512]{3,0,2,1:T(4,128)(2,1)S(1)}, bf16[4,6,12,512]{3,0,2,1:T(4,128)(2,1)}, u32[]{:S(2)}) copy-start(bf16[4,6,12,512]{3,0,2,1:T(4,128)(2,1)} %param.19) | copy-start | bytes 884740
  2.2 25.8 %copy-start.27 = (f32[512]{0:T(512)S(1)}, f32[512]{0:T(512)}, u32[]{:S(2)}) copy-start(f32[512]{0:T(512)} %param.17) | copy-start | bytes 6148
  25.9 4.2 %collective-permute-start = (bf16[512,1024]{1,0:T(8,128)(2,1)S(1)}, bf16[512,1024]{1,0:T(8,128)(2,1)S(1)}, u32[]{:S(2)}, u32[]{:S(2)}) collective-permute-start(bf16[512,1024]{1,0:T(8,128)(2,1)S(1)} %bitcast.87), channel_id=1, source_target_pairs={{0,8},{8,0},{16,24},{24,16},{32,40},{40,32},{48,56},{56,48},{64,72... | collective-permute-start | bytes 3145736 | tf_op jit(solution)/shard_map/ppermute | solution.py:190
  27.9 2.9 %copy-start.14 = (bf16[288,512]{1,0:T(8,128)(2,1)}, bf16[288,512]{1,0:T(8,128)(2,1)S(1)}, u32[]{:S(2)}) copy-start(bf16[288,512]{1,0:T(8,128)(2,1)S(1)} %reshape_reshape.10) | copy-start | bytes 884740
  30.8 1.4 copy-start.9
  32.2 0.9 copy-start.4
  33.1 8.5 %copy-start = (f32[288,512]{1,0:T(8,128)}, f32[288,512]{1,0:T(8,128)S(1)}, u32[]{:S(2)}) copy-start(f32[288,512]{1,0:T(8,128)S(1)} %copy.47) | copy-start | bytes 1769476
  33.1 7.5 %copy-start.20 = (f32[2,2,72,80]{3,1,2,0:T(2,128)S(1)}, f32[2,2,72,80]{3,1,2,0:T(2,128)}, u32[]{:S(2)}) copy-start(f32[2,2,72,80]{3,1,2,0:T(2,128)} %and_convert_fusion) | copy-start | bytes 276484
  33.2 8.5 %copy-start.6 = (bf16[288,512]{1,0:T(8,128)(2,1)}, bf16[288,512]{1,0:T(8,128)(2,1)S(1)}, u32[]{:S(2)}) copy-start(bf16[288,512]{1,0:T(8,128)(2,1)S(1)} %fusion.27) | copy-start | bytes 884740
  34.1 12.2 %collective-permute-start.1 = (bf16[2,1,72,1024]{3,2,1,0:T(8,128)(2,1)}, bf16[2,1,72,1024]{3,2,1,0:T(8,128)(2,1)}, u32[]{:S(2)}, u32[]{:S(2)}) collective-permute-start(bf16[2,1,72,1024]{3,2,1,0:T(8,128)(2,1)} %get-tuple-element.68), channel_id=1, source_target_pairs={{0,1},{1,2},{2,3},{3,4},{4,5},{5,6},{6,7},{7,0},{8,9},{9,10},{10,1... | collective-permute-start | bytes 884744 | tf_op jit(solution)/shard_map/ppermute | solution.py:148
  34.7 15.5 %collective-permute-start.2 = (bf16[2,1,72,1024]{3,2,1,0:T(8,128)(2,1)}, bf16[2,1,72,1024]{3,2,1,0:T(8,128)(2,1)}, u32[]{:S(2)}, u32[]{:S(2)}) collective-permute-start(bf16[2,1,72,1024]{3,2,1,0:T(8,128)(2,1)} %get-tuple-element.69), channel_id=1, source_target_pairs={{1,0},{2,1},{3,2},{4,3},{5,4},{6,5},{7,6},{0,7},{9,8},{10,9},{11,1... | collective-permute-start | bytes 884744 | tf_op jit(solution)/shard_map/ppermute | solution.py:149
  41.8 42.7 %copy-start.2 = (f32[288,512]{1,0:T(8,128)}, f32[288,512]{1,0:T(8,128)S(1)}, u32[]{:S(2)}) copy-start(f32[288,512]{1,0:T(8,128)S(1)} %reshape.373) | copy-start | bytes 1769476
  52.5 13.0 %collective-permute-start.3 = (bf16[1,4,72,1024]{3,2,1,0:T(8,128)(2,1)}, bf16[1,4,72,1024]{3,2,1,0:T(8,128)(2,1)}, u32[]{:S(2)}, u32[]{:S(2)}) collective-permute-start(bf16[1,4,72,1024]{3,2,1,0:T(8,128)(2,1)} %get-tuple-element.60), channel_id=1, source_target_pairs={{0,8},{8,16},{16,24},{24,32},{32,40},{40,48},{48,56},{56,64},{64,7... | collective-permute-start | bytes 1769480 | tf_op jit(solution)/shard_map/ppermute | solution.py:148
  57.2 11.5 %collective-permute-start.4 = (bf16[1,4,72,1024]{3,2,1,0:T(8,128)(2,1)}, bf16[1,4,72,1024]{3,2,1,0:T(8,128)(2,1)}, u32[]{:S(2)}, u32[]{:S(2)}) collective-permute-start(bf16[1,4,72,1024]{3,2,1,0:T(8,128)(2,1)} %get-tuple-element.61), channel_id=1, source_target_pairs={{8,0},{16,8},{24,16},{32,24},{40,32},{48,40},{56,48},{64,56},{72,6... | collective-permute-start | bytes 1769480 | tf_op jit(solution)/shard_map/ppermute | solution.py:149
  59.4 4.3 %copy-start.25 = (f32[288,8]{0,1:T(8,128)}, f32[288,8]{0,1:T(8,128)S(1)}, u32[]{:S(2)}) copy-start(f32[288,8]{0,1:T(8,128)S(1)} %multiply_reduce_fusion.1) | copy-start | bytes 27652
  59.5 9.2 %copy-start.7 = (bf16[288,512]{1,0:T(8,128)(2,1)S(1)}, bf16[288,512]{1,0:T(8,128)(2,1)}, u32[]{:S(2)}) copy-start(bf16[288,512]{1,0:T(8,128)(2,1)} %copy-done.6) | copy-start | bytes 884740
  82.4 2.1 copy-start.15
  85.5 18.8 %copy-start.18 = (bf16[288,512]{1,0:T(8,128)(2,1)}, bf16[288,512]{1,0:T(8,128)(2,1)S(1)}, u32[]{:S(2)}) copy-start(bf16[288,512]{1,0:T(8,128)(2,1)S(1)} %get-tuple-element.66) | copy-start | bytes 884740
  108.4 16.2 %collective-permute-start.5 = (bf16[1,4,72,1024]{3,2,1,0:T(8,128)(2,1)}, bf16[1,4,72,1024]{3,2,1,0:T(8,128)(2,1)}, u32[]{:S(2)}, u32[]{:S(2)}) collective-permute-start(bf16[1,4,72,1024]{3,2,1,0:T(8,128)(2,1)} %get-tuple-element.57), channel_id=1, source_target_pairs={{0,8},{8,16},{16,24},{24,32},{32,40},{40,48},{48,56},{56,64},{64,7... | collective-permute-start | bytes 1769480 | tf_op jit(solution)/shard_map/ppermute | solution.py:163
  110.3 15.9 %collective-permute-start.6 = (bf16[1,4,72,1024]{3,2,1,0:T(8,128)(2,1)}, bf16[1,4,72,1024]{3,2,1,0:T(8,128)(2,1)}, u32[]{:S(2)}, u32[]{:S(2)}) collective-permute-start(bf16[1,4,72,1024]{3,2,1,0:T(8,128)(2,1)} %get-tuple-element.56), channel_id=1, source_target_pairs={{8,0},{16,8},{24,16},{32,24},{40,32},{48,40},{56,48},{64,56},{72,6... | collective-permute-start | bytes 1769480 | tf_op jit(solution)/shard_map/ppermute | solution.py:163
  114.6 1.9 copy-start.12
  117.4 5.0 %copy-start.13 = (bf16[512,288]{1,0:T(8,128)(2,1)S(1)}, bf16[512,288]{1,0:T(8,128)(2,1)}, u32[]{:S(2)}) copy-start(bf16[512,288]{1,0:T(8,128)(2,1)} %copy.58) | copy-start | bytes 884740
  127.6 2.0 copy-start.11
  127.8 6.4 %copy-start.26 = (f32[288,8]{0,1:T(8,128)S(1)}, f32[288,8]{0,1:T(8,128)}, u32[]{:S(2)}) copy-start(f32[288,8]{0,1:T(8,128)} %copy-done.25) | copy-start | bytes 27652
  128.6 12.7 %collective-permute-start.7 = (bf16[2,1,72,1024]{3,2,1,0:T(8,128)(2,1)}, bf16[2,1,72,1024]{3,2,1,0:T(8,128)(2,1)}, u32[]{:S(2)}, u32[]{:S(2)}) collective-permute-start(bf16[2,1,72,1024]{3,2,1,0:T(8,128)(2,1)} %get-tuple-element.59), channel_id=1, source_target_pairs={{7,0},{0,1},{1,2},{2,3},{3,4},{4,5},{5,6},{6,7},{15,8},{8,9},{9,10... | collective-permute-start | bytes 884744 | tf_op jit(solution)/shard_map/ppermute | solution.py:157
  129.7 16.1 %collective-permute-start.8 = (bf16[2,1,72,1024]{3,2,1,0:T(8,128)(2,1)}, bf16[2,1,72,1024]{3,2,1,0:T(8,128)(2,1)}, u32[]{:S(2)}, u32[]{:S(2)}) collective-permute-start(bf16[2,1,72,1024]{3,2,1,0:T(8,128)(2,1)} %get-tuple-element.58), channel_id=1, source_target_pairs={{1,0},{2,1},{3,2},{4,3},{5,4},{6,5},{7,6},{0,7},{9,8},{10,9},{11,1... | collective-permute-start | bytes 884744 | tf_op jit(solution)/shard_map/ppermute | solution.py:157
  149.5 2.7 %copy-start.1 = (f32[288,512]{1,0:T(8,128)S(1)}, f32[288,512]{1,0:T(8,128)}, u32[]{:S(2)}) copy-start(f32[288,512]{1,0:T(8,128)} %copy-done) | copy-start | bytes 1769476
  149.5 2.7 %copy-start.5 = (bf16[288,1536]{1,0:T(8,128)(2,1)S(1)}, bf16[288,1536]{1,0:T(8,128)(2,1)}, u32[]{:S(2)}) copy-start(bf16[288,1536]{1,0:T(8,128)(2,1)} %copy-done.4) | copy-start | bytes 2654212
  152.2 2.2 %copy-start.16 = (bf16[288,512]{1,0:T(8,128)(2,1)S(1)}, bf16[288,512]{1,0:T(8,128)(2,1)}, u32[]{:S(2)}) copy-start(bf16[288,512]{1,0:T(8,128)(2,1)} %copy-done.14) | copy-start | bytes 884740
  152.2 2.2 %copy-start.23 = (bf16[288,512]{1,0:T(8,128)(2,1)S(1)}, bf16[288,512]{1,0:T(8,128)(2,1)}, u32[]{:S(2)}) copy-start(bf16[288,512]{1,0:T(8,128)(2,1)} %slice.270) | copy-start | bytes 884740
  154.3 1.1 copy-start.21
  154.3 1.1 copy-start.22
  154.3 1.2 copy-start.8
  155.7 2.8 %collective-permute-start.9 = (bf16[8,32,2048]{2,1,0:T(8,128)(2,1)S(1)}, bf16[8,32,2048]{2,1,0:T(8,128)(2,1)S(1)}, u32[]{:S(2)}, u32[]{:S(2)}) collective-permute-start(bf16[8,32,2048]{2,1,0:T(8,128)(2,1)S(1)} %fusion.24), channel_id=1, source_target_pairs={{0,8},{8,0},{16,24},{24,16},{32,40},{40,32},{48,56},{56,48},{64,72... | collective-permute-start | bytes 3145736 | tf_op jit(solution)/shard_map/ppermute | solution.py:190
  158.8 42.8 %copy-start.17 = (bf16[288,512]{1,0:T(8,128)(2,1)S(1)}, bf16[288,512]{1,0:T(8,128)(2,1)}, u32[]{:S(2)}) copy-start(bf16[288,512]{1,0:T(8,128)(2,1)} %get-tuple-element.67) | copy-start | bytes 884740
  180.0 30.9 %copy-start.3 = (f32[288,512]{1,0:T(8,128)S(1)}, f32[288,512]{1,0:T(8,128)}, u32[]{:S(2)}) copy-start(f32[288,512]{1,0:T(8,128)} %copy-done.2) | copy-start | bytes 1769476
  180.2 30.7 %copy-start.10 = (bf16[512,2048]{1,0:T(8,128)(2,1)S(1)}, bf16[512,2048]{1,0:T(8,128)(2,1)}, u32[]{:S(2)}) copy-start(bf16[512,2048]{1,0:T(8,128)(2,1)} %copy-done.9) | copy-start | bytes 6291460
  180.2 3.9 %collective-permute-start.10 = (bf16[32,2048]{1,0:T(8,128)(2,1)S(1)}, bf16[32,2048]{1,0:T(8,128)(2,1)S(1)}, u32[]{:S(2)}, u32[]{:S(2)}) collective-permute-start(bf16[32,2048]{1,0:T(8,128)(2,1)S(1)} %reduce_sum.92), channel_id=1, source_target_pairs={{0,16},{8,24},{16,0},{24,8},{32,48},{40,56},{48,32},{56,40},{64,80... | collective-permute-start | bytes 393224 | tf_op jit(solution)/shard_map/ppermute | solution.py:222
  184.1 9.0 %collective-permute-start.11 = (bf16[32,2048]{1,0:T(8,128)(2,1)S(1)}, bf16[32,2048]{1,0:T(8,128)(2,1)S(1)}, u32[]{:S(2)}, u32[]{:S(2)}) collective-permute-start(bf16[32,2048]{1,0:T(8,128)(2,1)S(1)} %add_convert_fusion.4), channel_id=1, source_target_pairs={{0,32},{8,40},{16,48},{24,56},{32,0},{40,8},{48,16},{56,24},{64,96... | collective-permute-start | bytes 393224 | tf_op jit(solution)/shard_map/ppermute | solution.py:222
  193.1 8.0 %collective-permute-start.12 = (bf16[32,2048]{1,0:T(8,128)(2,1)S(1)}, bf16[32,2048]{1,0:T(8,128)(2,1)S(1)}, u32[]{:S(2)}, u32[]{:S(2)}) collective-permute-start(bf16[32,2048]{1,0:T(8,128)(2,1)S(1)} %add_convert_fusion.3), channel_id=1, source_target_pairs={{0,64},{8,72},{16,80},{24,88},{32,96},{40,104},{48,112},{56,120},{... | collective-permute-start | bytes 393224 | tf_op jit(solution)/shard_map/ppermute | solution.py:222
  201.2 4.0 %collective-permute-start.13 = (bf16[32,2048]{1,0:T(8,128)(2,1)S(1)}, bf16[32,2048]{1,0:T(8,128)(2,1)}, u32[]{:S(2)}, u32[]{:S(2)}) collective-permute-start(bf16[32,2048]{1,0:T(8,128)(2,1)S(1)} %add_convert_fusion.2), channel_id=1, source_target_pairs={{0,128},{8,136},{16,144},{24,152},{32,160},{40,168},{48,176},{56,1... | collective-permute-start | bytes 393224 | tf_op jit(solution)/shard_map/ppermute | solution.py:222
  206.2 7.5 %collective-permute-start.14 = (bf16[32,2048]{1,0:T(8,128)(2,1)S(1)}, bf16[32,2048]{1,0:T(8,128)(2,1)S(1)}, u32[]{:S(2)}, u32[]{:S(2)}) collective-permute-start(bf16[32,2048]{1,0:T(8,128)(2,1)S(1)} %add_convert_fusion.1), channel_id=1, source_target_pairs={{0,8},{8,0},{16,24},{24,16},{32,40},{40,32},{48,56},{56,48},{64,72... | collective-permute-start | bytes 393224 | tf_op jit(solution)/shard_map/ppermute | solution.py:190
